TPU v7x, 128 devices: a whole 4x4x4 slice. The times are simulated.
128 devices in a mesh: tm: 64 (over z, y, x), tile: 2 (over core).
Axes of the slice: x: 4, y: 4, z: 4, core: 2. Of those that a mesh axis runs over, the one named last changes fastest.
Arguments:
- pivot_inverse: bfloat16 [64, 1024, 1024], P('tm', 'tile'), may hold values from -0.2 to 8.2, as said below
- mult_left: bfloat16 [64, 1024, 1024], P('tm', 'tile'), may hold values from -0.09375 to 0.09375
- mult_right: bfloat16 [64, 1024, 1024], P('tm', 'tile'), may hold values from -0.09375 to 0.09375
- mult_tip: bfloat16 [64, 64, 1024], P('tm', 'tile'), may hold values from -0.09375 to 0.09375
- root_cross: bfloat16 [64, 1024], P(None, 'tile'), may hold values from -0.59765625 to 0.59765625
- root_tip: bfloat16 [64, 64], replicated, may hold values from -0.2 to 8.2, as said below
Outputs:
- marginal_cov: bfloat16 [64, 1024, 1024], P('tm', 'tile')
- cross_cov: bfloat16 [64, 1024, 2048], P('tm', 'tile')
- tip_cov: bfloat16 [64, 64, 1024], P('tm', None, 'tile')
Inputs may be any that keep to these rules, and one draw needn't show every extreme that they name: `pivot_inverse`: each of the 64 matrices is symmetric. `root_tip`: symmetric.
All inputs are finite; a program needn't handle non-finite values.
Results may differ from a plain program's by a relative error of at most 0.006.
Values may be sent and summed in bfloat16 or wider, within the bound.
No kernel may reach another device: no remote copies, remote signals or barrier semaphores. Data moves between devices by JAX's collectives and lax.ppermute only.
A program may use at most 128 MiB of HBM per device.

v0:
```python
import jax
import jax.numpy as jnp
from jax import lax
from jax.sharding import PartitionSpec as P


def from_behind(shard, axis, by):
    devices = lax.axis_size(axis)
    return lax.ppermute(shard, axis, [(i, (i + by) % devices) for i in range(devices)])


def product(left_matrix, right_matrix):
    return jnp.dot(left_matrix, right_matrix, preferred_element_type=jnp.float32)


def pivot_test(block, level_index):
    return jnp.mod(block, 2 ** (level_index + 1)) == 2**level_index - 1


def body(pivot_inverse, mult_left, mult_right, mult_tip, root_cross, root_tip):
    part_count = lax.axis_size("tm")
    level_count = part_count.bit_length() - 1
    block = jnp.mod(lax.axis_index("tm") + 5, part_count)
    tile_index = lax.axis_index("tile")
    tile_rows = pivot_inverse.shape[1]
    own_start = tile_index * tile_rows
    own_left = mult_left[0]
    own_right = mult_right[0]
    inverse_rows = pivot_inverse[0]
    full_left, full_right, full_tip = (
        lax.all_gather(own_left, "tile", axis=0, tiled=True),
        lax.all_gather(own_right, "tile", axis=0, tiled=True),
        lax.all_gather(mult_tip[0], "tile", axis=0, tiled=True),
    )
    stacked = jnp.concatenate([full_left, full_right, full_tip], axis=0)
    is_root = block == part_count - 1
    tip_cols = lax.dynamic_slice_in_dim(full_tip, own_start, tile_rows, 1)
    zero_rows = jnp.zeros_like(inverse_rows)
    zero_tip = jnp.zeros_like(root_cross)
    diag_rows = jnp.where(is_root, inverse_rows, zero_rows)
    tip_block = jnp.where(is_root, root_cross, zero_tip)
    self_left = zero_rows
    self_right = zero_rows
    near_left = zero_rows
    near_right = zero_rows
    tip_own = product(root_tip, tip_cols)
    for level_index in reversed(range(level_count)):
        distance = 2**level_index
        active = pivot_test(block, level_index)
        has_left = block >= distance
        left_lower = jnp.mod(block - distance, 2 ** (level_index + 2)) == 2 ** (level_index + 1) - 1
        left_diag, left_tip, left_self, left_near = from_behind(
            (diag_rows, tip_block, self_right, near_right), "tm", distance
        )
        right_diag, right_tip, right_self, right_near = from_behind(
            (diag_rows, tip_block, self_left, near_left), "tm", -distance
        )
        left_right = jnp.where(left_lower, left_self, right_near)
        right_left = jnp.where(left_lower, left_near, right_self)
        left_diag = jnp.where(has_left, left_diag, zero_rows)
        left_tip = jnp.where(has_left, left_tip, zero_tip)
        left_right = jnp.where(has_left, left_right, zero_rows)
        right_left = jnp.where(has_left, right_left, zero_rows)
        operand = jnp.concatenate(
            [
                jnp.concatenate([left_diag, left_right, left_tip.T], axis=1),
                jnp.concatenate([right_left, right_diag, right_tip.T], axis=1),
            ],
            axis=0,
        )
        fresh_both = (-product(operand, stacked)).astype(jnp.bfloat16)
        fresh_a = fresh_both[:tile_rows]
        fresh_b = fresh_both[tile_rows:]
        tip_part = product(left_tip, own_left) + product(right_tip, own_right)
        tip_sum = lax.psum_scatter(tip_part, "tile", scatter_dimension=1, tiled=True)
        fresh_tip = (-(tip_sum + tip_own)).astype(jnp.bfloat16)
        turned = lax.all_to_all(
            jnp.stack([fresh_a, fresh_b]), "tile", split_axis=2, concat_axis=1, tiled=True
        )
        own_a = turned[0].T
        own_b = turned[1].T
        total = product(jnp.concatenate([own_a, own_b, fresh_tip.T], axis=1), stacked)
        fresh_diag = (inverse_rows.astype(jnp.float32) - total).astype(jnp.bfloat16)
        diag_rows = jnp.where(active, fresh_diag, diag_rows)
        tip_block = jnp.where(active, fresh_tip, tip_block)
        near_left = jnp.where(active, fresh_a, near_left)
        near_right = jnp.where(active, fresh_b, near_right)
        self_left = jnp.where(active, own_a, self_left)
        self_right = jnp.where(active, own_b, self_right)
    crossing = jnp.concatenate([self_left, self_right], axis=1)
    return (diag_rows[None], crossing[None], tip_block[None])


def solution(mesh):
    placed = (
        P("tm", "tile", None),
        P("tm", "tile", None),
        P("tm", "tile", None),
        P("tm", "tile", None),
        P(None, "tile"),
        P(),
    )
    return jax.shard_map(
        body,
        mesh=mesh,
        in_specs=placed,
        out_specs=(P("tm", "tile", None), P("tm", "tile", None), P("tm", None, "tile")),
        check_vma=False,
    )
```

profile of v0, /device:TPU:31, one launch (start us, length us, event | category | flops | bytes accessed | tf_op | source)
XLA Modules:
  0.0 821.4 jit_solution(4311508959548928089)
XLA Ops:
  19.8 11.2 %reduce-scatter.7.cloned.1.call-done = f32[64,512]{1,0:T(8,128)} async-done(((f32[64,1024]{1,0:T(8,128)}), f32[64,512]{1,0:T(8,128)}) %reduce-scatter.7.cloned.1.call-update) | async-done | bytes 131088 | tf_op jit(solution)/shard_map/reduce_scatter | solution.py:75
  49.0 18.4 %collective-permute-done = bf16[512,1024]{1,0:T(8,128)(2,1)S(1)} collective-permute-done((bf16[512,1024]{1,0:T(8,128)(2,1)}, bf16[512,1024]{1,0:T(8,128)(2,1)S(1)}, u32[]{:S(2)}, u32[]{:S(2)}) %collective-permute-start) | collective-permute-done | bytes 1048608 | tf_op jit(solution)/shard_map/ppermute | solution.py:9
  71.2 18.7 %collective-permute-done.1 = bf16[512,1024]{1,0:T(8,128)(2,1)S(1)} collective-permute-done((bf16[512,1024]{1,0:T(8,128)(2,1)}, bf16[512,1024]{1,0:T(8,128)(2,1)S(1)}, u32[]{:S(2)}, u32[]{:S(2)}) %collective-permute-start.1) | collective-permute-done | bytes 1048608 | tf_op jit(solution)/shard_map/ppermute | solution.py:9
  140.3 12.0 %collective-permute-done.3 = bf16[512,1024]{1,0:T(8,128)(2,1)} collective-permute-done((bf16[512,1024]{1,0:T(8,128)(2,1)}, bf16[512,1024]{1,0:T(8,128)(2,1)}, u32[]{:S(2)}, u32[]{:S(2)}) %collective-permute-start.3) | collective-permute-done | bytes 1048608 | tf_op jit(solution)/shard_map/ppermute | solution.py:9
  157.1 17.6 %collective-permute-done.4 = bf16[512,1024]{1,0:T(8,128)(2,1)} collective-permute-done((bf16[512,1024]{1,0:T(8,128)(2,1)}, bf16[512,1024]{1,0:T(8,128)(2,1)}, u32[]{:S(2)}, u32[]{:S(2)}) %collective-permute-start.4) | collective-permute-done | bytes 1048608 | tf_op jit(solution)/shard_map/ppermute | solution.py:9
  179.4 17.8 %collective-permute-done.7 = bf16[512,1024]{1,0:T(8,128)(2,1)} collective-permute-done((bf16[512,1024]{1,0:T(8,128)(2,1)}, bf16[512,1024]{1,0:T(8,128)(2,1)}, u32[]{:S(2)}, u32[]{:S(2)}) %collective-permute-start.7) | collective-permute-done | bytes 1048608 | tf_op jit(solution)/shard_map/ppermute | solution.py:9
  255.6 10.1 %collective-permute-done.11 = bf16[512,1024]{1,0:T(8,128)(2,1)} collective-permute-done((bf16[512,1024]{1,0:T(8,128)(2,1)}, bf16[512,1024]{1,0:T(8,128)(2,1)}, u32[]{:S(2)}, u32[]{:S(2)}) %collective-permute-start.11) | collective-permute-done | bytes 1048608 | tf_op jit(solution)/shard_map/ppermute | solution.py:9
  270.4 17.8 %collective-permute-done.12 = bf16[512,1024]{1,0:T(8,128)(2,1)} collective-permute-done((bf16[512,1024]{1,0:T(8,128)(2,1)}, bf16[512,1024]{1,0:T(8,128)(2,1)}, u32[]{:S(2)}, u32[]{:S(2)}) %collective-permute-start.12) | collective-permute-done | bytes 1048608 | tf_op jit(solution)/shard_map/ppermute | solution.py:9
  288.2 23.6 %collective-permute-done.13 = bf16[512,1024]{1,0:T(8,128)(2,1)} collective-permute-done((bf16[512,1024]{1,0:T(8,128)(2,1)}, bf16[512,1024]{1,0:T(8,128)(2,1)}, u32[]{:S(2)}, u32[]{:S(2)}) %collective-permute-start.13) | collective-permute-done | bytes 1048608 | tf_op jit(solution)/shard_map/ppermute | solution.py:9
  313.4 21.0 %collective-permute-done.16 = bf16[512,1024]{1,0:T(8,128)(2,1)} collective-permute-done((bf16[512,1024]{1,0:T(8,128)(2,1)}, bf16[512,1024]{1,0:T(8,128)(2,1)}, u32[]{:S(2)}, u32[]{:S(2)}) %collective-permute-start.16) | collective-permute-done | bytes 1048608 | tf_op jit(solution)/shard_map/ppermute | solution.py:9
  334.3 21.3 %collective-permute-done.15 = bf16[512,1024]{1,0:T(8,128)(2,1)} collective-permute-done((bf16[512,1024]{1,0:T(8,128)(2,1)}, bf16[512,1024]{1,0:T(8,128)(2,1)}, u32[]{:S(2)}, u32[]{:S(2)}) %collective-permute-start.15) | collective-permute-done | bytes 1048608 | tf_op jit(solution)/shard_map/ppermute | solution.py:9
  357.0 22.3 %collective-permute-done.17 = bf16[512,1024]{1,0:T(8,128)(2,1)} collective-permute-done((bf16[512,1024]{1,0:T(8,128)(2,1)}, bf16[512,1024]{1,0:T(8,128)(2,1)}, u32[]{:S(2)}, u32[]{:S(2)}) %collective-permute-start.17) | collective-permute-done | bytes 1048608 | tf_op jit(solution)/shard_map/ppermute | solution.py:9
  442.0 20.1 %collective-permute-done.20 = bf16[512,1024]{1,0:T(8,128)(2,1)} collective-permute-done((bf16[512,1024]{1,0:T(8,128)(2,1)}, bf16[512,1024]{1,0:T(8,128)(2,1)}, u32[]{:S(2)}, u32[]{:S(2)}) %collective-permute-start.20) | collective-permute-done | bytes 1048608 | tf_op jit(solution)/shard_map/ppermute | solution.py:9
  471.8 12.8 %collective-permute-done.23 = bf16[512,1024]{1,0:T(8,128)(2,1)} collective-permute-done((bf16[512,1024]{1,0:T(8,128)(2,1)}, bf16[512,1024]{1,0:T(8,128)(2,1)}, u32[]{:S(2)}, u32[]{:S(2)}) %collective-permute-start.23) | collective-permute-done | bytes 1048608 | tf_op jit(solution)/shard_map/ppermute | solution.py:9
  511.1 8.8 %all_to_all.93 = bf16[2,512,1024]{1,0,2:T(2,128)(2,1)S(1)} all-to-all(bf16[2,512,1024]{1,0,2:T(2,128)(2,1)} %copy.74), channel_id=1, replica_groups=mesh['tm'=64,'tile'=2] {'tile'}, dimensions={2} | all-to-all | bytes 4194304 | tf_op jit(solution)/shard_map/all_to_all | solution.py:77
  545.8 14.3 %collective-permute-done.42 = bf16[64,512]{1,0:T(8,128)(2,1)S(1)} collective-permute-done((bf16[64,512]{1,0:T(8,128)(2,1)S(1)}, bf16[64,512]{1,0:T(8,128)(2,1)S(1)}, u32[]{:S(2)}, u32[]{:S(2)}) %collective-permute-start.42) | collective-permute-done | bytes 65568 | tf_op jit(solution)/shard_map/ppermute | solution.py:9
  569.6 13.2 %collective-permute-done.28 = bf16[512,1024]{1,0:T(8,128)(2,1)} collective-permute-done((bf16[512,1024]{1,0:T(8,128)(2,1)}, bf16[512,1024]{1,0:T(8,128)(2,1)}, u32[]{:S(2)}, u32[]{:S(2)}) %collective-permute-start.28) | collective-permute-done | bytes 1048608 | tf_op jit(solution)/shard_map/ppermute | solution.py:9
  585.5 18.7 %collective-permute-done.29 = bf16[512,1024]{1,0:T(8,128)(2,1)} collective-permute-done((bf16[512,1024]{1,0:T(8,128)(2,1)S(1)}, bf16[512,1024]{1,0:T(8,128)(2,1)}, u32[]{:S(2)}, u32[]{:S(2)}) %collective-permute-start.29) | collective-permute-done | bytes 1048608 | tf_op jit(solution)/shard_map/ppermute | solution.py:9
  605.8 20.9 %collective-permute-done.32 = bf16[512,1024]{1,0:T(8,128)(2,1)} collective-permute-done((bf16[512,1024]{1,0:T(8,128)(2,1)}, bf16[512,1024]{1,0:T(8,128)(2,1)}, u32[]{:S(2)}, u32[]{:S(2)}) %collective-permute-start.32) | collective-permute-done | bytes 1048608 | tf_op jit(solution)/shard_map/ppermute | solution.py:9
  626.7 23.5 %collective-permute-done.31 = bf16[512,1024]{1,0:T(8,128)(2,1)} collective-permute-done((bf16[512,1024]{1,0:T(8,128)(2,1)}, bf16[512,1024]{1,0:T(8,128)(2,1)}, u32[]{:S(2)}, u32[]{:S(2)}) %collective-permute-start.31) | collective-permute-done | bytes 1048608 | tf_op jit(solution)/shard_map/ppermute | solution.py:9
  651.6 20.0 %collective-permute-done.33 = bf16[512,1024]{1,0:T(8,128)(2,1)S(1)} collective-permute-done((bf16[512,1024]{1,0:T(8,128)(2,1)}, bf16[512,1024]{1,0:T(8,128)(2,1)S(1)}, u32[]{:S(2)}, u32[]{:S(2)}) %collective-permute-start.33) | collective-permute-done | bytes 1048608 | tf_op jit(solution)/shard_map/ppermute | solution.py:9
  720.0 10.6 %collective-permute-done.35 = bf16[512,1024]{1,0:T(8,128)(2,1)} collective-permute-done((bf16[512,1024]{1,0:T(8,128)(2,1)}, bf16[512,1024]{1,0:T(8,128)(2,1)}, u32[]{:S(2)}, u32[]{:S(2)}) %collective-permute-start.35) | collective-permute-done | bytes 1048608 | tf_op jit(solution)/shard_map/ppermute | solution.py:9
  735.0 18.0 %collective-permute-done.36 = bf16[512,1024]{1,0:T(8,128)(2,1)} collective-permute-done((bf16[512,1024]{1,0:T(8,128)(2,1)S(1)}, bf16[512,1024]{1,0:T(8,128)(2,1)}, u32[]{:S(2)}, u32[]{:S(2)}) %collective-permute-start.36) | collective-permute-done | bytes 1048608 | tf_op jit(solution)/shard_map/ppermute | solution.py:9
  761.1 14.4 %collective-permute-done.39 = bf16[512,1024]{1,0:T(8,128)(2,1)} collective-permute-done((bf16[512,1024]{1,0:T(8,128)(2,1)}, bf16[512,1024]{1,0:T(8,128)(2,1)}, u32[]{:S(2)}, u32[]{:S(2)}) %collective-permute-start.39) | collective-permute-done | bytes 1048608 | tf_op jit(solution)/shard_map/ppermute | solution.py:9
  (394 shorter events, 398.8 us)
Async XLA Ops:
  16.5 52.0 %reduce-scatter.9.cloned.1.call-start = ((), (), s32[]{:S(2)}) async-start(), calls=%async_computation.13 | async-start | bytes 393216 | tf_op jit(solution)/shard_map/reduce_scatter | solution.py:75
  40.7 51.7 %all-gather.6.cloned.1.call-start = ((), (), s32[]{:S(2)}) async-start(), calls=%async_computation.18 | async-start | bytes 3145728 | tf_op jit(solution)/shard_map/all_gather | solution.py:31
  41.4 51.0 %all-gather.8.cloned.1.call-start = ((), (), s32[]{:S(2)}) async-start(), calls=%async_computation.19 | async-start | bytes 3145728 | tf_op jit(solution)/shard_map/all_gather | solution.py:32
  42.6 110.9 %reduce-scatter.11.cloned.1.call-start = ((), (), s32[]{:S(2)}) async-start(), calls=%async_computation.14 | async-start | bytes 393216 | tf_op jit(solution)/shard_map/reduce_scatter | solution.py:75
  127.7 287.6 %reduce-scatter.13.cloned.1.call-start = ((), (), s32[]{:S(2)}) async-start(), calls=%async_computation.15 | async-start | bytes 393216 | tf_op jit(solution)/shard_map/reduce_scatter | solution.py:75
  135.7 61.6 %collective-permute-start.7 = (bf16[512,1024]{1,0:T(8,128)(2,1)}, bf16[512,1024]{1,0:T(8,128)(2,1)}, u32[]{:S(2)}, u32[]{:S(2)}) collective-permute-start(bf16[512,1024]{1,0:T(8,128)(2,1)} %get-tuple-element.52), channel_id=1, source_target_pairs={{0,32},{2,34},{4,36},{6,38},{8,40},{10,42},{12,44},{14,46},{16,48}... | collective-permute-start | bytes 3145736 | tf_op jit(solution)/shard_map/ppermute | solution.py:9
  152.3 51.0 %collective-permute-start.9 = (bf16[512,1024]{1,0:T(8,128)(2,1)}, bf16[512,1024]{1,0:T(8,128)(2,1)}, u32[]{:S(2)}, u32[]{:S(2)}) collective-permute-start(bf16[512,1024]{1,0:T(8,128)(2,1)} %fusion.156), channel_id=1, source_target_pairs={{0,96},{2,98},{4,100},{6,102},{8,104},{10,106},{12,108},{14,110},{... | collective-permute-start | bytes 3145736 | tf_op jit(solution)/shard_map/ppermute | solution.py:9
  174.8 66.2 %collective-permute-start.22 = (bf16[64,512]{1,0:T(8,128)(2,1)}, bf16[64,512]{1,0:T(8,128)(2,1)S(1)}, u32[]{:S(2)}, u32[]{:S(2)}) collective-permute-start(bf16[64,512]{1,0:T(8,128)(2,1)} %get-tuple-element.15), channel_id=1, source_target_pairs={{0,8},{2,10},{4,12},{6,14},{8,16},{10,18},{12,20},{14,22},{16,24},... | collective-permute-start | bytes 196616 | tf_op jit(solution)/shard_map/ppermute | solution.py:9
  175.7 66.1 %collective-permute-start.26 = (bf16[64,512]{1,0:T(8,128)(2,1)}, bf16[64,512]{1,0:T(8,128)(2,1)}, u32[]{:S(2)}, u32[]{:S(2)}) collective-permute-start(bf16[64,512]{1,0:T(8,128)(2,1)} %get-tuple-element.15), channel_id=1, source_target_pairs={{0,120},{2,122},{4,124},{6,126},{8,0},{10,2},{12,4},{14,6},{16,8},... | collective-permute-start | bytes 196616 | tf_op jit(solution)/shard_map/ppermute | solution.py:9
  248.8 63.0 %collective-permute-start.13 = (bf16[512,1024]{1,0:T(8,128)(2,1)}, bf16[512,1024]{1,0:T(8,128)(2,1)}, u32[]{:S(2)}, u32[]{:S(2)}) collective-permute-start(bf16[512,1024]{1,0:T(8,128)(2,1)} %get-tuple-element.43), channel_id=1, source_target_pairs={{0,112},{2,114},{4,116},{6,118},{8,120},{10,122},{12,124},{14,126}... | collective-permute-start | bytes 3145736 | tf_op jit(solution)/shard_map/ppermute | solution.py:9
  250.2 84.1 %collective-permute-start.16 = (bf16[512,1024]{1,0:T(8,128)(2,1)}, bf16[512,1024]{1,0:T(8,128)(2,1)}, u32[]{:S(2)}, u32[]{:S(2)}) collective-permute-start(bf16[512,1024]{1,0:T(8,128)(2,1)} %broadcast_select_fusion.7), channel_id=1, source_target_pairs={{0,112},{2,114},{4,116},{6,118},{8,120},{10,122},{12,124},{14,126}... | collective-permute-start | bytes 3145736 | tf_op jit(solution)/shard_map/ppermute | solution.py:9
  253.9 101.7 %collective-permute-start.15 = (bf16[512,1024]{1,0:T(8,128)(2,1)}, bf16[512,1024]{1,0:T(8,128)(2,1)}, u32[]{:S(2)}, u32[]{:S(2)}) collective-permute-start(bf16[512,1024]{1,0:T(8,128)(2,1)} %get-tuple-element.46), channel_id=1, source_target_pairs={{0,16},{2,18},{4,20},{6,22},{8,24},{10,26},{12,28},{14,30},{16,32}... | collective-permute-start | bytes 3145736 | tf_op jit(solution)/shard_map/ppermute | solution.py:9
  265.7 113.5 %collective-permute-start.17 = (bf16[512,1024]{1,0:T(8,128)(2,1)}, bf16[512,1024]{1,0:T(8,128)(2,1)}, u32[]{:S(2)}, u32[]{:S(2)}) collective-permute-start(bf16[512,1024]{1,0:T(8,128)(2,1)} %fusion.153), channel_id=1, source_target_pairs={{0,112},{2,114},{4,116},{6,118},{8,120},{10,122},{12,124},{14,126}... | collective-permute-start | bytes 3145736 | tf_op jit(solution)/shard_map/ppermute | solution.py:9
  269.1 265.3 %reduce-scatter.15.cloned.1.call-start = ((), (), s32[]{:S(2)}) async-start(), calls=%async_computation.16 | async-start | bytes 393216 | tf_op jit(solution)/shard_map/reduce_scatter | solution.py:75
  428.5 56.0 %collective-permute-start.23 = (bf16[512,1024]{1,0:T(8,128)(2,1)}, bf16[512,1024]{1,0:T(8,128)(2,1)}, u32[]{:S(2)}, u32[]{:S(2)}) collective-permute-start(bf16[512,1024]{1,0:T(8,128)(2,1)} %get-tuple-element.40), channel_id=1, source_target_pairs={{0,8},{2,10},{4,12},{6,14},{8,16},{10,18},{12,20},{14,22},{16,24},... | collective-permute-start | bytes 3145736 | tf_op jit(solution)/shard_map/ppermute | solution.py:9
  439.6 54.7 %collective-permute-start.25 = (bf16[512,1024]{1,0:T(8,128)(2,1)}, bf16[512,1024]{1,0:T(8,128)(2,1)}, u32[]{:S(2)}, u32[]{:S(2)}) collective-permute-start(bf16[512,1024]{1,0:T(8,128)(2,1)} %fusion.150), channel_id=1, source_target_pairs={{0,120},{2,122},{4,124},{6,126},{8,0},{10,2},{12,4},{14,6},{16,8},... | collective-permute-start | bytes 3145736 | tf_op jit(solution)/shard_map/ppermute | solution.py:9
  440.6 291.4 %reduce-scatter.17.cloned.1.call-start = ((), (), s32[]{:S(2)}) async-start(), calls=%async_computation.17 | async-start | bytes 393216 | tf_op jit(solution)/shard_map/reduce_scatter | solution.py:75
  538.5 65.7 %collective-permute-start.29 = (bf16[512,1024]{1,0:T(8,128)(2,1)S(1)}, bf16[512,1024]{1,0:T(8,128)(2,1)}, u32[]{:S(2)}, u32[]{:S(2)}) collective-permute-start(bf16[512,1024]{1,0:T(8,128)(2,1)S(1)} %copy-done.7), channel_id=1, source_target_pairs={{0,124},{2,126},{4,0},{6,2},{8,4},{10,6},{12,8},{14,10},{16,12},{1... | collective-permute-start | bytes 3145736 | tf_op jit(solution)/shard_map/ppermute | solution.py:9
  543.5 83.2 %collective-permute-start.32 = (bf16[512,1024]{1,0:T(8,128)(2,1)}, bf16[512,1024]{1,0:T(8,128)(2,1)}, u32[]{:S(2)}, u32[]{:S(2)}) collective-permute-start(bf16[512,1024]{1,0:T(8,128)(2,1)} %broadcast_select_fusion.17), channel_id=1, source_target_pairs={{0,124},{2,126},{4,0},{6,2},{8,4},{10,6},{12,8},{14,10},{16,12},{1... | collective-permute-start | bytes 3145736 | tf_op jit(solution)/shard_map/ppermute | solution.py:9
  560.7 89.6 %collective-permute-start.31 = (bf16[512,1024]{1,0:T(8,128)(2,1)}, bf16[512,1024]{1,0:T(8,128)(2,1)}, u32[]{:S(2)}, u32[]{:S(2)}) collective-permute-start(bf16[512,1024]{1,0:T(8,128)(2,1)} %get-tuple-element.34), channel_id=1, source_target_pairs={{0,4},{2,6},{4,8},{6,10},{8,12},{10,14},{12,16},{14,18},{16,20},{1... | collective-permute-start | bytes 3145736 | tf_op jit(solution)/shard_map/ppermute | solution.py:9
  566.1 105.4 %collective-permute-start.33 = (bf16[512,1024]{1,0:T(8,128)(2,1)}, bf16[512,1024]{1,0:T(8,128)(2,1)S(1)}, u32[]{:S(2)}, u32[]{:S(2)}) collective-permute-start(bf16[512,1024]{1,0:T(8,128)(2,1)} %fusion.147), channel_id=1, source_target_pairs={{0,124},{2,126},{4,0},{6,2},{8,4},{10,6},{12,8},{14,10},{16,12},{1... | collective-permute-start | bytes 3145736 | tf_op jit(solution)/shard_map/ppermute | solution.py:9
  582.8 123.1 %collective-permute-start.38 = (bf16[64,512]{1,0:T(8,128)(2,1)}, bf16[64,512]{1,0:T(8,128)(2,1)}, u32[]{:S(2)}, u32[]{:S(2)}) collective-permute-start(bf16[64,512]{1,0:T(8,128)(2,1)} %copy-done.41), channel_id=1, source_target_pairs={{0,2},{2,4},{4,6},{6,8},{8,10},{10,12},{12,14},{14,16},{16,18},{18... | collective-permute-start | bytes 196616 | tf_op jit(solution)/shard_map/ppermute | solution.py:9
  713.9 61.6 %collective-permute-start.39 = (bf16[512,1024]{1,0:T(8,128)(2,1)}, bf16[512,1024]{1,0:T(8,128)(2,1)}, u32[]{:S(2)}, u32[]{:S(2)}) collective-permute-start(bf16[512,1024]{1,0:T(8,128)(2,1)} %get-tuple-element.28), channel_id=1, source_target_pairs={{0,2},{2,4},{4,6},{6,8},{8,10},{10,12},{12,14},{14,16},{16,18},{18... | collective-permute-start | bytes 3145736 | tf_op jit(solution)/shard_map/ppermute | solution.py:9
  730.6 53.0 %collective-permute-start.41 = (bf16[512,1024]{1,0:T(8,128)(2,1)}, bf16[512,1024]{1,0:T(8,128)(2,1)}, u32[]{:S(2)}, u32[]{:S(2)}) collective-permute-start(bf16[512,1024]{1,0:T(8,128)(2,1)} %fusion.144), channel_id=1, source_target_pairs={{0,126},{2,0},{4,2},{6,4},{8,6},{10,8},{12,10},{14,12},{16,14},{18... | collective-permute-start | bytes 3145736 | tf_op jit(solution)/shard_map/ppermute | solution.py:9
  (113 other events, 2248.9 us)
Sparse Core Ops, SparseCore 0:
  16.6 14.3 reduce-scatter.6
  40.8 10.5 reduce-scatter.8
  53.1 14.5 all-gather.5
  69.2 14.6 all-gather.7
  127.8 13.2 reduce-scatter.10
  269.2 12.5 reduce-scatter.12
  440.8 14.1 reduce-scatter.14
  708.0 16.4 reduce-scatter.16
where the time goes:
time: 835 us; the launch traced here: 821 us
  waiting for transfers between devices  448 us (54%)
  local copies, waits for them, and re-layouts  88 us (11%)
  matrix products  80.9 us (10%)
  other arithmetic  75.7 us (9%)
  starting transfers between devices  62.1 us (7%)
  blocking collectives  50.9 us (6%)
  between operations  15.5 us (2%)
    ppermute x43, waiting for transfers between devices, from_behind(): lax.ppermute(shard, axis, [(i, (i + by) % devices) for i in range(devices)])  436 us
    dot_general x25, matrix products, product(): jnp.dot(left_matrix, right_matrix, preferred_element_type=jnp.float32)  80.9 us
    ppermute x43, starting transfers between devices, from_behind(): lax.ppermute(shard, axis, [(i, (i + by) % devices) for i in range(devices)])  61.8 us
    all_to_all x6, blocking collectives, body(): lax.all_to_all(jnp.stack([fresh_a, fresh_b]), 'tile', split_axis=2, conca...  47.8 us
    another operation x7, local copies, waits for them, and re-layouts, body(): jnp.stack([fresh_a, fresh_b])  33.1 us
    unnamed x184, local copies, waits for them, and re-layouts  17.9 us
  transfers between devices with their start and end apart: 51, of which 33 were waited for; matrix products, arithmetic and copies ran while one was open for 25% of the time, Pallas kernels for 0%

commit v1 on v0

v1 whole, which is shorter than its diff:
```python
import numpy as np

import jax
import jax.numpy as jnp
from jax import lax
from jax.sharding import PartitionSpec as P


def product(left_matrix, right_matrix):
    return jnp.dot(left_matrix, right_matrix, preferred_element_type=jnp.float32)


def level_of(block, steps, levels):
    if block == steps - 1:
        return levels
    level = 0
    while (block >> level) & 1:
        level += 1
    return level


def plan(steps, levels, offset):
    where_is = lambda block: (block - offset) % steps
    levels_plan = {}
    for level_index in reversed(range(levels)):
        distance = 2**level_index
        crit_from_left, crit_from_right = [], []
        pre_from_left, pre_from_right = [], []
        c_left = [False] * steps
        active = [False] * steps
        for block in range(steps):
            if block % (2 * distance) != distance - 1:
                continue
            active[where_is(block)] = True
            left_id, right_id = block - distance, block + distance
            if left_id >= 0 and level_of(left_id, steps, levels) == level_index + 1:
                c_left[where_is(block)] = True
                crit_from_left.append((where_is(left_id), where_is(block)))
                pre_from_right.append((where_is(right_id), where_is(block)))
            else:
                crit_from_right.append((where_is(right_id), where_is(block)))
                if left_id >= 0:
                    pre_from_left.append((where_is(left_id), where_is(block)))
        levels_plan[level_index] = dict(
            crit_from_left=crit_from_left,
            crit_from_right=crit_from_right,
            pre_from_left=pre_from_left,
            pre_from_right=pre_from_right,
            c_left=c_left,
            active=active,
        )
    return levels_plan


def pick(flag, if_true, if_false):
    if if_true is None:
        return if_false
    if if_false is None:
        return if_true
    return jnp.where(flag, if_true, if_false)


def send(values, pairs):
    if not pairs:
        return None
    return lax.ppermute(values, "tm", pairs)


def tile_transpose(rows):
    turned = lax.all_to_all(rows[None], "tile", split_axis=2, concat_axis=1, tiled=True)
    return turned[0].T


def body(pivot_inverse, mult_left, mult_right, mult_tip, root_cross, root_tip):
    steps = lax.axis_size("tm")
    levels = steps.bit_length() - 1
    offset = 5 % steps
    levels_plan = plan(steps, levels, offset)
    position = lax.axis_index("tm")
    tile_index = lax.axis_index("tile")
    tile_rows = pivot_inverse.shape[1]

    own_left = mult_left[0]
    own_right = mult_right[0]
    inverse_rows = pivot_inverse[0]
    full_left = lax.all_gather(own_left, "tile", axis=0, tiled=True)
    full_right = lax.all_gather(own_right, "tile", axis=0, tiled=True)
    full_tip = lax.all_gather(mult_tip[0], "tile", axis=0, tiled=True)
    tip_cols = lax.dynamic_slice_in_dim(full_tip, tile_index * tile_rows, tile_rows, 1)
    tip_own = product(root_tip, tip_cols)

    zero_rows = jnp.zeros_like(inverse_rows)
    zero_tip = jnp.zeros_like(root_cross)

    def table(values):
        return jnp.asarray(np.array(values, dtype=bool))[position]

    up_diag, up_tip, up_self_left, up_self_right = inverse_rows, root_cross, zero_rows, zero_rows
    state_diag, state_tip = inverse_rows, root_cross
    state_cross = jnp.zeros((tile_rows, 2 * inverse_rows.shape[1]), inverse_rows.dtype)
    history = {levels: (state_diag, state_tip)}

    for level_index in reversed(range(levels)):
        step_plan = levels_plan[level_index]
        c_left = table(step_plan["c_left"])
        active = table(step_plan["active"])

        from_left = send((up_diag, up_tip, up_self_right), step_plan["crit_from_left"])
        from_right = send((up_diag, up_tip, up_self_left), step_plan["crit_from_right"])
        near_diag = pick(c_left, *(None if r is None else r[0] for r in (from_left, from_right)))
        near_tip = pick(c_left, *(None if r is None else r[1] for r in (from_left, from_right)))
        cross = pick(c_left, *(None if r is None else r[2] for r in (from_left, from_right)))

        older = history.get(level_index + 2)
        if older is None:
            far_diag, far_tip = zero_rows, zero_tip
        else:
            g_left = send(older, step_plan["pre_from_left"])
            g_right = send(older, step_plan["pre_from_right"])
            if g_left is None and g_right is None:
                far_diag, far_tip = zero_rows, zero_tip
            else:
                far_diag = pick(c_left, *(None if r is None else r[0] for r in (g_right, g_left)))
                far_tip = pick(c_left, *(None if r is None else r[1] for r in (g_right, g_left)))

        first = jnp.where(c_left, full_left, full_right)
        second = jnp.where(c_left, full_right, full_left)
        first_rows = jnp.where(c_left, own_left, own_right)
        second_rows = jnp.where(c_left, own_right, own_left)
        stacked = jnp.concatenate([first, second, full_tip], axis=0)

        cross_turned = tile_transpose(cross)
        operand = jnp.concatenate(
            [
                jnp.concatenate([near_diag, cross, near_tip.T], axis=1),
                jnp.concatenate([cross_turned, far_diag, far_tip.T], axis=1),
            ],
            axis=0,
        )
        fresh_both = (-product(operand, stacked)).astype(jnp.bfloat16)
        fresh_near = fresh_both[:tile_rows]
        fresh_far = fresh_both[tile_rows:]
        tip_part = product(near_tip, first_rows) + product(far_tip, second_rows)
        tip_sum = lax.psum_scatter(tip_part, "tile", scatter_dimension=1, tiled=True)
        fresh_tip = (-(tip_sum + tip_own)).astype(jnp.bfloat16)
        turned = lax.all_to_all(
            jnp.stack([fresh_near, fresh_far]), "tile", split_axis=2, concat_axis=1, tiled=True
        )
        own_near = turned[0].T
        own_far = turned[1].T
        total = product(jnp.concatenate([own_near, own_far, fresh_tip.T], axis=1), stacked)
        fresh_diag = (inverse_rows.astype(jnp.float32) - total).astype(jnp.bfloat16)
        self_left = jnp.where(c_left, own_near, own_far)
        self_right = jnp.where(c_left, own_far, own_near)

        state_diag = jnp.where(active, fresh_diag, state_diag)
        state_tip = jnp.where(active, fresh_tip, state_tip)
        state_cross = jnp.where(active, jnp.concatenate([self_left, self_right], axis=1), state_cross)
        history[level_index] = (state_diag, state_tip)
        up_diag, up_tip, up_self_left, up_self_right = fresh_diag, fresh_tip, self_left, self_right

    return (state_diag[None], state_cross[None], state_tip[None])


def solution(mesh):
    placed = (
        P("tm", "tile", None),
        P("tm", "tile", None),
        P("tm", "tile", None),
        P("tm", "tile", None),
        P(None, "tile"),
        P(),
    )
    return jax.shard_map(
        body,
        mesh=mesh,
        in_specs=placed,
        out_specs=(P("tm", "tile", None), P("tm", "tile", None), P("tm", None, "tile")),
        check_vma=False,
    )
```

time: 835 us -> 733 us (0.88)
  the two profiles are of different devices: /device:TPU:31 before, /device:TPU:7 now
where the time goes in v1:
time: 733 us; the launch traced here: 721 us
  waiting for transfers between devices  182 us (25%)
  local copies, waits for them, and re-layouts  149 us (20%)
  other arithmetic  137 us (19%)
  matrix products  85.8 us (12%)
  blocking collectives  81.2 us (11%)
  starting transfers between devices  68.6 us (9%)
  between operations  16.9 us (2%)
    ppermute x51, waiting for transfers between devices, send(): return lax.ppermute(values, 'tm', pairs)  132 us
    dot_general x25, matrix products, product(): jnp.dot(left_matrix, right_matrix, preferred_element_type=jnp.float32)  85.8 us
    ppermute x51, starting transfers between devices, send(): return lax.ppermute(values, 'tm', pairs)  68.3 us
    unnamed x6, other arithmetic  50.5 us
    reduce_scatter x6, waiting for transfers between devices, body(): lax.psum_scatter(tip_part, 'tile', scatter_dimension=1, tiled=True)  49.9 us
    unnamed x238, local copies, waits for them, and re-layouts  45.5 us
    all_to_all x6, blocking collectives, body(): lax.all_to_all(jnp.stack([fresh_near, fresh_far]), 'tile', split_axis=2,...  40.2 us
    all_to_all x6, blocking collectives, tile_transpose(): lax.all_to_all(rows[None], 'tile', split_axis=2, concat_axis=1, tiled=True)  38.7 us
  transfers between devices with their start and end apart: 59, of which 6 were waited for; matrix products, arithmetic and copies ran while one was open for 45% of the time, Pallas kernels for 0%

profile of v1, /device:TPU:7, one launch (start us, length us, event | category | flops | bytes accessed | tf_op | source)
XLA Modules:
  0.0 721.0 jit_solution(5155810023884559803)
XLA Ops:
  16.7 14.0 %reduce-scatter.7.cloned.1.call-done = f32[64,512]{1,0:T(8,128)} async-done(((f32[64,1024]{1,0:T(8,128)}), f32[64,512]{1,0:T(8,128)}) %reduce-scatter.7.cloned.1.call-update) | async-done | bytes 131088 | tf_op jit(solution)/shard_map/reduce_scatter | solution.py:144
  37.7 13.7 %reduce-scatter.9.cloned.1.call-done = f32[64,512]{1,0:T(8,128)} async-done(((f32[64,1024]{1,0:T(8,128)}), f32[64,512]{1,0:T(8,128)}) %reduce-scatter.9.cloned.1.call-update) | async-done | bytes 131088 | tf_op jit(solution)/shard_map/reduce_scatter | solution.py:144
  73.6 7.1 reduce
  111.8 8.3 %negate_convert_fusion.5 = bf16[1024,1024]{1,0:T(8,128)(2,1)S(1)} fusion(bf16[512,64]{1,0:T(8,128)(2,1)S(1)} %transpose.113, bf16[512,1024]{1,0:T(8,128)(2,1)} %copy-done.42, bf16[512,1024]{1,0:T(8,128)(2,1)} %bitcast.483, bf16[512,64]{1,0:T(8,128)(2,1)} %bitcast.505, bf16[512,1024]{1,0:T(8,128)(2,1)S(1)} %copy-done.41, ...), kind=kOutput, calls=%fused_computation.89 | convolution fusion | flops 4470210560 | bytes 10747904 | tf_op jit(solution)/shard_map/dot_general | solution.py:10
  128.0 6.9 all_to_all.181
  153.1 10.5 %broadcast_select_fusion.1 = (bf16[1024,1024]{1,0:T(8,128)(2,1)}, bf16[1024,1024]{1,0:T(8,128)(2,1)}, bf16[1024,1024]{1,0:T(8,128)(2,1)}, bf16[1024,1024]{1,0:T(...) fusion(pred[]{:T(512)} %bitcast.2, ...), kind=kLoop, calls=%fused_computation.151 | loop fusion | flops 10485760 | bytes 25165828 | tf_op jit(solution)/shard_map/jit(_where)/select_n | solution.py:126
  176.3 9.1 %reduce.1 = bf16[1024,512]{1,0:T(8,128)(2,1)} reduce(bf16[1024,1,512]{2,1,0:T(2,128)(2,1)} %bitcast.417, bf16[]{:T(256)} %broadcast.52), dimensions={1}, to_apply=%bitcast.377.reduce_sub_computation | reduce | bytes 2097154
  218.0 6.6 all_to_all.183
  258.5 9.1 %reduce.2 = bf16[1024,512]{1,0:T(8,128)(2,1)} reduce(bf16[1024,1,512]{2,1,0:T(2,128)(2,1)} %bitcast.418, bf16[]{:T(256)} %broadcast.52), dimensions={1}, to_apply=%bitcast.379.reduce_sub_computation | reduce | bytes 2097154
  340.2 9.1 %reduce.3 = bf16[1024,512]{1,0:T(8,128)(2,1)} reduce(bf16[1024,1,512]{2,1,0:T(2,128)(2,1)} %bitcast.419, bf16[]{:T(256)} %broadcast.52), dimensions={1}, to_apply=%bitcast.381.reduce_sub_computation | reduce | bytes 2097154
  351.9 6.8 all_to_all.186
  396.7 6.9 broadcast_select_fusion.10
  404.9 32.2 %collective-permute-done.50 = bf16[64,512]{1,0:T(8,128)(2,1)} collective-permute-done((bf16[64,512]{1,0:T(8,128)(2,1)}, bf16[64,512]{1,0:T(8,128)(2,1)}, u32[]{:S(2)}, u32[]{:S(2)}) %collective-permute-start.50) | collective-permute-done | bytes 65568 | tf_op jit(solution)/shard_map/ppermute | solution.py:66
  459.7 8.1 %reduce.4 = bf16[1024,512]{1,0:T(8,128)(2,1)} reduce(bf16[1024,1,512]{2,1,0:T(2,128)(2,1)S(1)} %bitcast.420, bf16[]{:T(256)} %broadcast.52), dimensions={1}, to_apply=%bitcast.383.reduce_sub_computation | reduce | bytes 2097154
  469.6 7.5 %all_to_all.188 = bf16[2,2,131072]{2,1,0:T(2,128)(2,1)} all-to-all(bf16[2,2,131072]{2,1,0:T(2,128)(2,1)S(1)} %reshape.222), channel_id=1, replica_groups=mesh['tm'=64,'tile'=2] {'tile'}, dimensions={0} | all-to-all | bytes 2097152 | tf_op jit(solution)/shard_map/all_to_all | solution.py:70
  495.9 6.6 all_to_all.189
  519.9 22.2 %reduce-scatter.17.cloned.1.call-done = f32[64,512]{1,0:T(8,128)} async-done(((f32[64,1024]{1,0:T(8,128)}), f32[64,512]{1,0:T(8,128)}) %reduce-scatter.17.cloned.1.call-update) | async-done | bytes 131088 | tf_op jit(solution)/shard_map/reduce_scatter | solution.py:144
  545.8 40.1 %collective-permute-done.48 = bf16[512,1024]{1,0:T(8,128)(2,1)} collective-permute-done((bf16[512,1024]{1,0:T(8,128)(2,1)}, bf16[512,1024]{1,0:T(8,128)(2,1)}, u32[]{:S(2)}, u32[]{:S(2)}) %collective-permute-start.48) | collective-permute-done | bytes 1048608 | tf_op jit(solution)/shard_map/ppermute | solution.py:66
  588.9 59.2 %collective-permute-done.44 = bf16[512,1024]{1,0:T(8,128)(2,1)} collective-permute-done((bf16[512,1024]{1,0:T(8,128)(2,1)S(1)}, bf16[512,1024]{1,0:T(8,128)(2,1)}, u32[]{:S(2)}, u32[]{:S(2)}) %collective-permute-start.44) | collective-permute-done | bytes 1048608 | tf_op jit(solution)/shard_map/ppermute | solution.py:66
  651.8 8.1 %reduce.5 = bf16[1024,512]{1,0:T(8,128)(2,1)} reduce(bf16[1024,1,512]{2,1,0:T(2,128)(2,1)S(1)} %bitcast.415, bf16[]{:T(256)} %broadcast.52), dimensions={1}, to_apply=%bitcast.385.reduce_sub_computation | reduce | bytes 2097154
  661.7 6.7 all_to_all.190
  684.4 6.9 all_to_all.191
  697.9 6.8 fusion.127
  704.8 8.9 %maximum_select_fusion = bf16[1,512,2048]{2,1,0:T(8,128)(2,1)} fusion(bf16[1,512,1024]{2,1,0:T(8,128)(2,1)S(1)} %get-tuple-element.26, bf16[1,512,1024]{2,1,0:T(8,128)(2,1)S(1)} %get-tuple-element.25, bf16[1,512,1024]{2,1,0:T(8,128)(2,1)} %bitcast.95, bf16[1,512,1024]{2,1,0:T(8,128)(2,1)S(1)} %bitcast.474, bf16[1,512,1024]{2,1,0:T(8,128)(2,1)} %bitcast.97, ...), kind=kLoop, calls=%fused_computation.138 | loop fusion | flops 31457280 | bytes 14680070 | tf_op jit(solution)/shard_map/jit(_where)/select_n | solution.py:158
  (490 shorter events, 382.9 us)
Async XLA Ops:
  36.4 58.3 %reduce-scatter.11.cloned.1.call-start = ((), (), s32[]{:S(2)}) async-start(), calls=%async_computation.20 | async-start | bytes 393216 | tf_op jit(solution)/shard_map/reduce_scatter | solution.py:144
  59.9 51.9 %all-gather.6.cloned.1.call-start = ((), (), s32[]{:S(2)}) async-start(), calls=%async_computation.24 | async-start | bytes 3145728 | tf_op jit(solution)/shard_map/all_gather | solution.py:87
  60.5 51.3 %all-gather.8.cloned.1.call-start = ((), (), s32[]{:S(2)}) async-start(), calls=%async_computation.25 | async-start | bytes 3145728 | tf_op jit(solution)/shard_map/all_gather | solution.py:86
  61.4 102.1 %reduce-scatter.13.cloned.1.call-start = ((), (), s32[]{:S(2)}) async-start(), calls=%async_computation.21 | async-start | bytes 393216 | tf_op jit(solution)/shard_map/reduce_scatter | solution.py:144
  61.5 50.3 %collective-permute-start = (bf16[512,1024]{1,0:T(8,128)(2,1)}, bf16[512,1024]{1,0:T(8,128)(2,1)}, u32[]{:S(2)}, u32[]{:S(2)}) collective-permute-start(bf16[512,1024]{1,0:T(8,128)(2,1)} %bitcast.506), channel_id=1, source_target_pairs={{116,52},{117,53}} | collective-permute-start | bytes 3145736 | tf_op jit(solution)/shard_map/ppermute | solution.py:66
  63.1 140.7 %collective-permute-start.9 = (bf16[512,1024]{1,0:T(8,128)(2,1)}, bf16[512,1024]{1,0:T(8,128)(2,1)}, u32[]{:S(2)}, u32[]{:S(2)}) collective-permute-start(bf16[512,1024]{1,0:T(8,128)(2,1)} %bitcast.507), channel_id=1, source_target_pairs={{116,84},{117,85}} | collective-permute-start | bytes 3145736 | tf_op jit(solution)/shard_map/ppermute | solution.py:66
  111.7 214.9 %reduce-scatter.15.cloned.1.call-start = ((), (), s32[]{:S(2)}) async-start(), calls=%async_computation.22 | async-start | bytes 393216 | tf_op jit(solution)/shard_map/reduce_scatter | solution.py:144
  146.3 54.4 %collective-permute-start.3 = (bf16[512,1024]{1,0:T(8,128)(2,1)}, bf16[512,1024]{1,0:T(8,128)(2,1)}, u32[]{:S(2)}, u32[]{:S(2)}) collective-permute-start(bf16[512,1024]{1,0:T(8,128)(2,1)} %fusion.108), channel_id=1, source_target_pairs={{52,84},{53,85}} | collective-permute-start | bytes 3145736 | tf_op jit(solution)/shard_map/ppermute | solution.py:66
  148.1 53.7 %collective-permute-start.4 = (bf16[512,1024]{1,0:T(8,128)(2,1)}, bf16[512,1024]{1,0:T(8,128)(2,1)}, u32[]{:S(2)}, u32[]{:S(2)}) collective-permute-start(bf16[512,1024]{1,0:T(8,128)(2,1)} %fusion.108), channel_id=1, source_target_pairs={{52,20},{53,21}} | collective-permute-start | bytes 3145736 | tf_op jit(solution)/shard_map/ppermute | solution.py:66
  167.9 70.4 %collective-permute-start.35 = (bf16[64,512]{1,0:T(8,128)(2,1)}, bf16[64,512]{1,0:T(8,128)(2,1)}, u32[]{:S(2)}, u32[]{:S(2)}) collective-permute-start(bf16[64,512]{1,0:T(8,128)(2,1)} %get-tuple-element.6), channel_id=1, source_target_pairs={{124,0},{12,16},{28,32},{44,48},{60,64},{76,80},{92,96},{108,112},... | collective-permute-start | bytes 196616 | tf_op jit(solution)/shard_map/ppermute | solution.py:66
  169.2 69.8 %collective-permute-start.39 = (bf16[64,512]{1,0:T(8,128)(2,1)}, bf16[64,512]{1,0:T(8,128)(2,1)S(1)}, u32[]{:S(2)}, u32[]{:S(2)}) collective-permute-start(bf16[64,512]{1,0:T(8,128)(2,1)} %get-tuple-element.7), channel_id=1, source_target_pairs={{4,0},{20,16},{36,32},{52,48},{68,64},{84,80},{100,96},{116,112},{... | collective-permute-start | bytes 196616 | tf_op jit(solution)/shard_map/ppermute | solution.py:66
  249.3 292.8 %reduce-scatter.17.cloned.1.call-start = ((), (), s32[]{:S(2)}) async-start(), calls=%async_computation.23 | async-start | bytes 393216 | tf_op jit(solution)/shard_map/reduce_scatter | solution.py:144
  250.8 72.8 %collective-permute-start.27 = (bf16[512,1024]{1,0:T(8,128)(2,1)}, bf16[512,1024]{1,0:T(8,128)(2,1)}, u32[]{:S(2)}, u32[]{:S(2)}) collective-permute-start(bf16[512,1024]{1,0:T(8,128)(2,1)} %get-tuple-element.10), channel_id=1, source_target_pairs={{20,12},{52,44},{84,76},{116,108},{21,13},{53,45},{85,77},{117,109}} | collective-permute-start | bytes 3145736 | tf_op jit(solution)/shard_map/ppermute | solution.py:66
  327.5 76.1 %collective-permute-start.49 = (bf16[64,512]{1,0:T(8,128)(2,1)}, bf16[64,512]{1,0:T(8,128)(2,1)}, u32[]{:S(2)}, u32[]{:S(2)}) collective-permute-start(bf16[64,512]{1,0:T(8,128)(2,1)} %get-tuple-element.5), channel_id=1, source_target_pairs={{124,122},{4,2},{12,10},{20,18},{28,26},{36,34},{44,42},{52,50},{6... | collective-permute-start | bytes 196616 | tf_op jit(solution)/shard_map/ppermute | solution.py:66
  331.6 105.5 %collective-permute-start.50 = (bf16[64,512]{1,0:T(8,128)(2,1)}, bf16[64,512]{1,0:T(8,128)(2,1)}, u32[]{:S(2)}, u32[]{:S(2)}) collective-permute-start(bf16[64,512]{1,0:T(8,128)(2,1)} %get-tuple-element.5), channel_id=1, source_target_pairs={{124,126},{4,6},{12,14},{20,22},{28,30},{36,38},{44,46},{52,54},{6... | collective-permute-start | bytes 196616 | tf_op jit(solution)/shard_map/ppermute | solution.py:66
  332.9 105.8 %collective-permute-start.45 = (bf16[64,512]{1,0:T(8,128)(2,1)S(1)}, bf16[64,512]{1,0:T(8,128)(2,1)}, u32[]{:S(2)}, u32[]{:S(2)}) collective-permute-start(bf16[64,512]{1,0:T(8,128)(2,1)S(1)} %negate_convert_fusion.7), channel_id=1, source_target_pairs={{120,122},{0,2},{8,10},{16,18},{24,26},{32,34},{40,42},{48,50},{56... | collective-permute-start | bytes 196616 | tf_op jit(solution)/shard_map/ppermute | solution.py:66
  393.0 53.6 %collective-permute-start.33 = (bf16[512,1024]{1,0:T(8,128)(2,1)}, bf16[512,1024]{1,0:T(8,128)(2,1)}, u32[]{:S(2)}, u32[]{:S(2)}) collective-permute-start(bf16[512,1024]{1,0:T(8,128)(2,1)} %get-tuple-element.38), channel_id=1, source_target_pairs={{124,0},{12,16},{28,32},{44,48},{60,64},{76,80},{92,96},{108,112},... | collective-permute-start | bytes 3145736 | tf_op jit(solution)/shard_map/ppermute | solution.py:66
  394.7 59.5 %collective-permute-start.34 = (bf16[512,1024]{1,0:T(8,128)(2,1)S(1)}, bf16[512,1024]{1,0:T(8,128)(2,1)}, u32[]{:S(2)}, u32[]{:S(2)}) collective-permute-start(bf16[512,1024]{1,0:T(8,128)(2,1)S(1)} %get-tuple-element.37), channel_id=1, source_target_pairs={{124,120},{12,8},{28,24},{44,40},{60,56},{76,72},{92,88},{108,104}... | collective-permute-start | bytes 3145736 | tf_op jit(solution)/shard_map/ppermute | solution.py:66
  454.2 63.0 %collective-permute-start.47 = (bf16[512,1024]{1,0:T(8,128)(2,1)}, bf16[512,1024]{1,0:T(8,128)(2,1)}, u32[]{:S(2)}, u32[]{:S(2)}) collective-permute-start(bf16[512,1024]{1,0:T(8,128)(2,1)} %get-tuple-element.8), channel_id=1, source_target_pairs={{124,122},{4,2},{12,10},{20,18},{28,26},{36,34},{44,42},{52,50},{6... | collective-permute-start | bytes 3145736 | tf_op jit(solution)/shard_map/ppermute | solution.py:66
  480.7 105.2 %collective-permute-start.48 = (bf16[512,1024]{1,0:T(8,128)(2,1)}, bf16[512,1024]{1,0:T(8,128)(2,1)}, u32[]{:S(2)}, u32[]{:S(2)}) collective-permute-start(bf16[512,1024]{1,0:T(8,128)(2,1)} %get-tuple-element.8), channel_id=1, source_target_pairs={{124,126},{4,6},{12,14},{20,22},{28,30},{36,38},{44,46},{52,54},{6... | collective-permute-start | bytes 3145736 | tf_op jit(solution)/shard_map/ppermute | solution.py:66
  508.7 80.2 %collective-permute-start.43 = (bf16[512,1024]{1,0:T(8,128)(2,1)}, bf16[512,1024]{1,0:T(8,128)(2,1)}, u32[]{:S(2)}, u32[]{:S(2)}) collective-permute-start(bf16[512,1024]{1,0:T(8,128)(2,1)} %get-tuple-element.32), channel_id=1, source_target_pairs={{120,122},{0,2},{8,10},{16,18},{24,26},{32,34},{40,42},{48,50},{56... | collective-permute-start | bytes 3145736 | tf_op jit(solution)/shard_map/ppermute | solution.py:66
  510.3 137.7 %collective-permute-start.44 = (bf16[512,1024]{1,0:T(8,128)(2,1)S(1)}, bf16[512,1024]{1,0:T(8,128)(2,1)}, u32[]{:S(2)}, u32[]{:S(2)}) collective-permute-start(bf16[512,1024]{1,0:T(8,128)(2,1)S(1)} %get-tuple-element.31), channel_id=1, source_target_pairs={{120,118},{0,126},{8,6},{16,14},{24,22},{32,30},{40,38},{48,46},{5... | collective-permute-start | bytes 3145736 | tf_op jit(solution)/shard_map/ppermute | solution.py:66
  515.5 156.6 %collective-permute-start.41 = (bf16[512,1024]{1,0:T(8,128)(2,1)}, bf16[512,1024]{1,0:T(8,128)(2,1)}, u32[]{:S(2)}, u32[]{:S(2)}) collective-permute-start(bf16[512,1024]{1,0:T(8,128)(2,1)} %fusion.112), channel_id=1, source_target_pairs={{120,122},{0,2},{8,10},{16,18},{24,26},{32,34},{40,42},{48,50},{56... | collective-permute-start | bytes 3145736 | tf_op jit(solution)/shard_map/ppermute | solution.py:66
  517.2 154.9 %collective-permute-start.42 = (bf16[512,1024]{1,0:T(8,128)(2,1)}, bf16[512,1024]{1,0:T(8,128)(2,1)}, u32[]{:S(2)}, u32[]{:S(2)}) collective-permute-start(bf16[512,1024]{1,0:T(8,128)(2,1)} %fusion.112), channel_id=1, source_target_pairs={{120,118},{0,126},{8,6},{16,14},{24,22},{32,30},{40,38},{48,46},{5... | collective-permute-start | bytes 3145736 | tf_op jit(solution)/shard_map/ppermute | solution.py:66
  (135 other events, 1530.6 us)
Sparse Core Ops, SparseCore 0:
  13.0 17.5 reduce-scatter.6
  36.5 14.8 reduce-scatter.8
  60.0 17.3 reduce-scatter.10
  78.9 14.5 all-gather.5
  95.0 14.5 all-gather.7
  111.8 38.1 reduce-scatter.12
  249.4 74.5 reduce-scatter.14
  454.3 87.7 reduce-scatter.16

commit v2 on v1

--- a/solution.py
+++ b/solution.py
@@ -66,9 +66,23 @@
     return lax.ppermute(values, "tm", pairs)
 
 
-def tile_transpose(rows):
-    turned = lax.all_to_all(rows[None], "tile", split_axis=2, concat_axis=1, tiled=True)
-    return turned[0].T
+def swap_tiles(values):
+    return lax.ppermute(values, "tile", [(0, 1), (1, 0)])
+
+
+def tile_transpose(blocks, is_first):
+    half = blocks.shape[1]
+    left, right = blocks[:, :, :half], blocks[:, :, half:]
+    mine = jnp.where(is_first, left, right)
+    got = swap_tiles(jnp.where(is_first, right, left))
+    top = jnp.where(is_first, mine, got)
+    bottom = jnp.where(is_first, got, mine)
+    return jnp.concatenate([jnp.swapaxes(top, 1, 2), jnp.swapaxes(bottom, 1, 2)], axis=2)
+
+
+def join_tiles(halves, is_first):
+    got = swap_tiles(halves)
+    return jnp.where(is_first, jnp.concatenate([halves, got], axis=-1), jnp.concatenate([got, halves], axis=-1))
 
 
 def body(pivot_inverse, mult_left, mult_right, mult_tip, root_cross, root_tip):
@@ -78,7 +92,18 @@
     levels_plan = plan(steps, levels, offset)
     position = lax.axis_index("tm")
     tile_index = lax.axis_index("tile")
+    is_first = tile_index == 0
     tile_rows = pivot_inverse.shape[1]
+
+    def table(values):
+        return jnp.asarray(np.array(values, dtype=bool))[position]
+
+    own_role = [False] * steps
+    for level_index, step_plan in levels_plan.items():
+        for where_at in range(steps):
+            if step_plan["active"][where_at]:
+                own_role[where_at] = step_plan["c_left"][where_at]
+    role = table(own_role)
 
     own_left = mult_left[0]
     own_right = mult_right[0]
@@ -86,14 +111,17 @@
     full_left = lax.all_gather(own_left, "tile", axis=0, tiled=True)
     full_right = lax.all_gather(own_right, "tile", axis=0, tiled=True)
     full_tip = lax.all_gather(mult_tip[0], "tile", axis=0, tiled=True)
-    tip_cols = lax.dynamic_slice_in_dim(full_tip, tile_index * tile_rows, tile_rows, 1)
+    first = jnp.where(role, full_left, full_right)
+    second = jnp.where(role, full_right, full_left)
+    stacked = jnp.concatenate([first, second, full_tip], axis=0)
+    col_start = tile_index * tile_rows
+    first_cols = lax.dynamic_slice_in_dim(first, col_start, tile_rows, 1)
+    second_cols = lax.dynamic_slice_in_dim(second, col_start, tile_rows, 1)
+    tip_cols = lax.dynamic_slice_in_dim(full_tip, col_start, tile_rows, 1)
     tip_own = product(root_tip, tip_cols)
 
     zero_rows = jnp.zeros_like(inverse_rows)
     zero_tip = jnp.zeros_like(root_cross)
-
-    def table(values):
-        return jnp.asarray(np.array(values, dtype=bool))[position]
 
     up_diag, up_tip, up_self_left, up_self_right = inverse_rows, root_cross, zero_rows, zero_rows
     state_diag, state_tip = inverse_rows, root_cross
@@ -102,34 +130,25 @@
 
     for level_index in reversed(range(levels)):
         step_plan = levels_plan[level_index]
-        c_left = table(step_plan["c_left"])
         active = table(step_plan["active"])
 
         from_left = send((up_diag, up_tip, up_self_right), step_plan["crit_from_left"])
         from_right = send((up_diag, up_tip, up_self_left), step_plan["crit_from_right"])
-        near_diag = pick(c_left, *(None if r is None else r[0] for r in (from_left, from_right)))
-        near_tip = pick(c_left, *(None if r is None else r[1] for r in (from_left, from_right)))
-        cross = pick(c_left, *(None if r is None else r[2] for r in (from_left, from_right)))
+        near_diag = pick(role, *(None if r is None else r[0] for r in (from_left, from_right)))
+        near_tip = pick(role, *(None if r is None else r[1] for r in (from_left, from_right)))
+        cross = pick(role, *(None if r is None else r[2] for r in (from_left, from_right)))
 
         older = history.get(level_index + 2)
-        if older is None:
-            far_diag, far_tip = zero_rows, zero_tip
-        else:
+        far_diag, far_tip = zero_rows, zero_tip
+        if older is not None:
             g_left = send(older, step_plan["pre_from_left"])
             g_right = send(older, step_plan["pre_from_right"])
-            if g_left is None and g_right is None:
-                far_diag, far_tip = zero_rows, zero_tip
-            else:
-                far_diag = pick(c_left, *(None if r is None else r[0] for r in (g_right, g_left)))
-                far_tip = pick(c_left, *(None if r is None else r[1] for r in (g_right, g_left)))
+            if g_left is not None or g_right is not None:
+                far_diag = pick(role, *(None if r is None else r[0] for r in (g_right, g_left)))
+                far_tip = pick(role, *(None if r is None else r[1] for r in (g_right, g_left)))
 
-        first = jnp.where(c_left, full_left, full_right)
-        second = jnp.where(c_left, full_right, full_left)
-        first_rows = jnp.where(c_left, own_left, own_right)
-        second_rows = jnp.where(c_left, own_right, own_left)
-        stacked = jnp.concatenate([first, second, full_tip], axis=0)
-
-        cross_turned = tile_transpose(cross)
+        cross_turned = tile_transpose(cross[None], is_first)[0]
+        tips_full = join_tiles(jnp.stack([near_tip, far_tip]), is_first)
         operand = jnp.concatenate(
             [
                 jnp.concatenate([near_diag, cross, near_tip.T], axis=1),
@@ -140,18 +159,15 @@
         fresh_both = (-product(operand, stacked)).astype(jnp.bfloat16)
         fresh_near = fresh_both[:tile_rows]
         fresh_far = fresh_both[tile_rows:]
-        tip_part = product(near_tip, first_rows) + product(far_tip, second_rows)
-        tip_sum = lax.psum_scatter(tip_part, "tile", scatter_dimension=1, tiled=True)
-        fresh_tip = (-(tip_sum + tip_own)).astype(jnp.bfloat16)
-        turned = lax.all_to_all(
-            jnp.stack([fresh_near, fresh_far]), "tile", split_axis=2, concat_axis=1, tiled=True
-        )
-        own_near = turned[0].T
-        own_far = turned[1].T
+        tip_y = product(tips_full[0], first_cols) + product(tips_full[1], second_cols) + tip_own
+        fresh_tip = (-tip_y).astype(jnp.bfloat16)
+        turned = tile_transpose(jnp.stack([fresh_near, fresh_far]), is_first)
+        own_near = turned[0]
+        own_far = turned[1]
         total = product(jnp.concatenate([own_near, own_far, fresh_tip.T], axis=1), stacked)
         fresh_diag = (inverse_rows.astype(jnp.float32) - total).astype(jnp.bfloat16)
-        self_left = jnp.where(c_left, own_near, own_far)
-        self_right = jnp.where(c_left, own_far, own_near)
+        self_left = jnp.where(role, own_near, own_far)
+        self_right = jnp.where(role, own_far, own_near)
 
         state_diag = jnp.where(active, fresh_diag, state_diag)
         state_tip = jnp.where(active, fresh_tip, state_tip)

time: 733 us -> 628 us (0.86)
  the two profiles are of different devices: /device:TPU:7 before, /device:TPU:31 now
where the time goes in v2:
time: 628 us; the launch traced here: 617 us
  waiting for transfers between devices  267 us (43%)
  other arithmetic  108 us (17%)
  matrix products  85.1 us (14%)
  local copies, waits for them, and re-layouts  73.3 us (12%)
  starting transfers between devices  65.3 us (10%)
  between operations  16.2 us (3%)
    ppermute x51, waiting for transfers between devices, send(): return lax.ppermute(values, 'tm', pairs)  229 us
    dot_general x25, matrix products, product(): jnp.dot(left_matrix, right_matrix, preferred_element_type=jnp.float32)  85.1 us
    ppermute x51, starting transfers between devices, send(): return lax.ppermute(values, 'tm', pairs)  57.3 us
    select_n x14, other arithmetic, pick(): return jnp.where(flag, if_true, if_false)  30.6 us
    select_n x11, other arithmetic, body(): self_left = jnp.where(role, own_near, own_far)  18.6 us
    all_gather x1, waiting for transfers between devices, body(): full_right = lax.all_gather(own_right, 'tile', axis=0, tiled=True)  16.3 us
    unnamed x168, local copies, waits for them, and re-layouts  15.9 us
  transfers between devices with their start and end apart: 71, of which 12 were waited for; matrix products, arithmetic and copies ran while one was open for 25% of the time, Pallas kernels for 0%

profile of v2, /device:TPU:31, one launch (start us, length us, event | category | flops | bytes accessed | tf_op | source)
XLA Modules:
  0.0 616.7 jit_solution(11658298001432726784)
XLA Ops:
  15.6 9.9 %all-gather.6.cloned.1.call-done = bf16[1,1024,1024]{2,1,0:T(8,128)(2,1)} async-done(((bf16[1,512,1024]{2,1,0:T(8,128)(2,1)}), bf16[1,1024,1024]{2,1,0:T(8,128)(2,1)}) %all-gather.6.cloned.1.call-update) | async-done | bytes 2097168 | tf_op jit(solution)/shard_map/all_gather | solution.py:111
  25.5 16.3 %all-gather.8.cloned.1.call-done = bf16[1,1024,1024]{2,1,0:T(8,128)(2,1)} async-done(((bf16[1,512,1024]{2,1,0:T(8,128)(2,1)}), bf16[1,1024,1024]{2,1,0:T(8,128)(2,1)}) %all-gather.8.cloned.1.call-update) | async-done | bytes 2097168 | tf_op jit(solution)/shard_map/all_gather | solution.py:112
  41.9 3.2 broadcast_select_fusion
  58.5 3.0 broadcast_select_fusion.67
  80.3 6.6 %negate_convert_fusion.5 = bf16[1024,1024]{1,0:T(8,128)(2,1)S(1)} fusion(bf16[512,64]{1,0:T(8,128)(2,1)S(1)} %transpose.166, bf16[512,1024]{1,0:T(8,128)(2,1)} %broadcast_in_dim.31, bf16[512,1024]{1,0:T(8,128)(2,1)S(1)} %copy-done.36, bf16[512,64]{1,0:T(8,128)(2,1)S(1)} %copy-done.59, bf16[512,1024]{1,0:T(8,128)(2,1)S(1)} %collective-permute-done.1, ...), kind=kOutput, calls=%fused_computation.84 | convolution fusion | flops 4470210560 | bytes 10747904 | tf_op jit(solution)/shard_map/dot_general | solution.py:10
  100.2 11.1 %collective-permute-done.66 = bf16[64,512]{1,0:T(8,128)(2,1)S(1)} collective-permute-done((bf16[64,512]{1,0:T(8,128)(2,1)S(1)}, bf16[64,512]{1,0:T(8,128)(2,1)S(1)}, u32[]{:S(2)}, u32[]{:S(2)}) %collective-permute-start.66) | collective-permute-done | bytes 65568 | tf_op jit(solution)/shard_map/ppermute | solution.py:66
  112.6 6.9 %collective-permute-done.61 = bf16[64,512]{1,0:T(8,128)(2,1)S(1)} collective-permute-done((bf16[64,512]{1,0:T(8,128)(2,1)S(1)}, bf16[64,512]{1,0:T(8,128)(2,1)S(1)}, u32[]{:S(2)}, u32[]{:S(2)}) %collective-permute-start.61) | collective-permute-done | bytes 65568 | tf_op jit(solution)/shard_map/ppermute | solution.py:66
  129.8 4.9 fusion.108
  149.5 6.3 %negate_convert_fusion.4 = bf16[1024,1024]{1,0:T(8,128)(2,1)S(1)} fusion(bf16[512,64]{1,0:T(8,128)(2,1)S(1)} %copy-done.64, bf16[512,1024]{1,0:T(8,128)(2,1)} %collective-permute-done.13, bf16[512,1024]{1,0:T(8,128)(2,1)S(1)} %maximum_bitcast_fusion.1, bf16[512,64]{1,0:T(8,128)(2,1)S(1)} %copy-done.65, bf16[512,1024]{1,0:T(8,128)(2,1)S(1)} %copy-done.42, ...), kind=kOutput, calls=%fused_computation.83 | convolution fusion | flops 4470210560 | bytes 10747904 | tf_op jit(solution)/shard_map/dot_general | solution.py:10
  165.5 6.9 %broadcast_select_fusion.29 = (bf16[512,1024]{1,0:T(8,128)(2,1)}, bf16[512,1024]{1,0:T(8,128)(2,1)}, bf16[512,1024]{1,0:T(8,128)(2,1)}) fusion(pred[]{:T(512)} %bitcast.65, bf16[512,1024]{1,0:T(8,128)(2,1)} %fusion.108, bf16[1,512,1024]{2,1,0:T(8,128)(2,1)} %param.13, pred[]{:T(512)} %bitcast.47, bf16[64,1024]{1,0:T(8,128)(2,1)S(1)} %bitcast.404, ...), kind=kOutput, calls=%fused_computation.267 | convolution fusion | flops 2236678144 | bytes 11730946 | tf_op jit(solution)/shard_map/dot_general | solution.py:10
  192.1 5.1 negate_convert_fusion.3
  207.3 4.9 fusion.110
  221.8 3.0 broadcast_select_fusion.32
  237.9 6.3 %negate_convert_fusion.2 = bf16[1024,1024]{1,0:T(8,128)(2,1)S(1)} fusion(bf16[512,64]{0,1:T(8,128)(2,1)S(1)} %copy-done.72, bf16[512,1024]{0,1:T(8,128)(2,1)S(1)} %copy-done.41, bf16[512,1024]{0,1:T(8,128)(2,1)S(1)} %maximum_bitcast_fusion.3, bf16[512,64]{0,1:T(8,128)(2,1)S(1)} %copy-done.73, bf16[512,1024]{0,1:T(8,128)(2,1)S(1)} %broadcast_select_fusion.8, ...), kind=kOutput, calls=%fused_computation.81 | convolution fusion | flops 4470210560 | bytes 10747904 | tf_op jit(solution)/shard_map/dot_general | solution.py:10
  253.8 7.0 %broadcast_select_fusion.27 = (bf16[512,1024]{1,0:T(8,128)(2,1)}, bf16[512,1024]{1,0:T(8,128)(2,1)}, bf16[512,1024]{1,0:T(8,128)(2,1)}) fusion(pred[]{:T(512)} %bitcast.103, bf16[512,1024]{1,0:T(8,128)(2,1)} %fusion.110, bf16[512,1024]{1,0:T(8,128)(2,1)S(1)} %copy-done.75, pred[]{:T(512)} %bitcast.83, bf16[64,1024]{1,0:T(8,128)(2,1)S(1)} %bitcast.408, ...), kind=kOutput, calls=%fused_computation.265 | convolution fusion | flops 2236678144 | bytes 12779522 | tf_op jit(solution)/shard_map/dot_general | solution.py:10
  280.9 3.0 broadcast_select_fusion.37
  287.4 7.7 %negate_convert_fusion.1 = bf16[1024,1024]{1,0:T(8,128)(2,1)S(1)} fusion(bf16[512,64]{1,0:T(8,128)(2,1)} %copy.114, bf16[512,1024]{1,0:T(8,128)(2,1)} %broadcast_select_fusion.34, bf16[512,1024]{1,0:T(8,128)(2,1)} %copy.113, bf16[512,64]{1,0:T(8,128)(2,1)} %copy.112, bf16[512,1024]{1,0:T(8,128)(2,1)S(1)} %broadcast_select_fusion.31, ...), kind=kOutput, calls=%fused_computation.80 | convolution fusion | flops 4470210560 | bytes 10747904 | tf_op jit(solution)/shard_map/dot_general | solution.py:10
  323.1 5.0 fusion.112
  335.1 203.3 %collective-permute-done.59 = bf16[512,1024]{0,1:T(8,128)(2,1)} collective-permute-done((bf16[512,1024]{0,1:T(8,128)(2,1)}, bf16[512,1024]{0,1:T(8,128)(2,1)}, u32[]{:S(2)}, u32[]{:S(2)}) %collective-permute-start.59) | collective-permute-done | bytes 1048608 | tf_op jit(solution)/shard_map/ppermute | solution.py:66
  553.1 7.8 %collective-permute-done.57 = bf16[512,1024]{1,0:T(8,128)(2,1)} collective-permute-done((bf16[512,1024]{1,0:T(8,128)(2,1)}, bf16[512,1024]{1,0:T(8,128)(2,1)}, u32[]{:S(2)}, u32[]{:S(2)}) %collective-permute-start.57) | collective-permute-done | bytes 1048608 | tf_op jit(solution)/shard_map/ppermute | solution.py:66
  574.9 6.6 %negate_convert_fusion = bf16[1024,1024]{1,0:T(8,128)(2,1)S(1)} fusion(bf16[512,64]{1,0:T(8,128)(2,1)S(1)} %copy-done.60, bf16[512,1024]{1,0:T(8,128)(2,1)S(1)} %copy-done.37, bf16[512,1024]{1,0:T(8,128)(2,1)S(1)} %maximum_bitcast_fusion.5, bf16[512,64]{1,0:T(8,128)(2,1)S(1)} %copy-done.61, bf16[512,1024]{1,0:T(8,128)(2,1)} %copy.122, ...), kind=kOutput, calls=%fused_computation.79 | convolution fusion | flops 4470210560 | bytes 10747904 | tf_op jit(solution)/shard_map/dot_general | solution.py:10
  591.6 6.5 %maximum_select_fusion = bf16[1,512,2048]{1,2,0:T(8,128)(2,1)} fusion(bf16[1,512,1024]{1,2,0:T(8,128)(2,1)S(1)} %get-tuple-element.55, bf16[1,512,1024]{1,2,0:T(8,128)(2,1)S(1)} %get-tuple-element.52, bf16[1,512,1024]{1,2,0:T(8,128)(2,1)S(1)} %broadcast_select_fusion.23, bf16[1,512,1024]{1,2,0:T(8,128)(2,1)S(1)} %copy-done.35, ...), kind=kLoop, calls=%fused_computation.151 | loop fusion | flops 31457280 | bytes 14680070 | tf_op jit(solution)/shard_map/jit(_where)/select_n | solution.py:174
  598.1 3.9 copy.133
  602.0 7.4 %fusion.141 = bf16[1,512,1024]{2,1,0:T(8,128)(2,1)} fusion(bf16[512,64]{0,1:T(8,128)(2,1)S(1)} %copy-done.67, bf16[512,1024]{0,1:T(8,128)(2,1)S(1)} %get-tuple-element.53, bf16[512,1024]{0,1:T(8,128)(2,1)} %get-tuple-element.54, bf16[512,1024]{1,0:T(8,128)(2,1)} %fusion.112, bf16[512,1024]{1,0:T(8,128)(2,1)} %get-tuple-element.26, pred[]{:T(512)} %bitcast.116, ...), kind=kOutput, calls=%fused_computation.160 | convolution fusion | flops 2236678144 | bytes 10682370 | tf_op jit(solution)/shard_map/dot_general | solution.py:10
  (444 shorter events, 247.8 us)
Async XLA Ops:
  7.2 18.3 %all-gather.6.cloned.1.call-start = ((), (), s32[]{:S(2)}) async-start(), calls=%async_computation | async-start | bytes 3145728 | tf_op jit(solution)/shard_map/all_gather | solution.py:111
  7.9 33.9 %all-gather.8.cloned.1.call-start = ((), (), s32[]{:S(2)}) async-start(), calls=%async_computation.1 | async-start | bytes 3145728 | tf_op jit(solution)/shard_map/all_gather | solution.py:112
  10.5 46.5 %collective-permute-start.1 = (bf16[512,1024]{1,0:T(8,128)(2,1)}, bf16[512,1024]{1,0:T(8,128)(2,1)S(1)}, u32[]{:S(2)}, u32[]{:S(2)}) collective-permute-start(bf16[512,1024]{1,0:T(8,128)(2,1)} %broadcast_in_dim.31), channel_id=1, source_target_pairs={{116,52},{117,53}} | collective-permute-start | bytes 3145736 | tf_op jit(solution)/shard_map/ppermute | solution.py:66
  49.4 30.8 %collective-permute-start = (bf16[512,1024]{1,0:T(8,128)(2,1)}, bf16[512,1024]{1,0:T(8,128)(2,1)}, u32[]{:S(2)}, u32[]{:S(2)}) collective-permute-start(bf16[512,1024]{1,0:T(8,128)(2,1)} %bitcast.1), channel_id=1, source_target_pairs={{116,52},{117,53}} | collective-permute-start | bytes 3145736 | tf_op jit(solution)/shard_map/ppermute | solution.py:66
  95.1 29.6 %collective-permute-start.4 = (bf16[2,512,512]{2,1,0:T(8,128)(2,1)S(1)}, bf16[2,512,512]{2,1,0:T(8,128)(2,1)S(1)}, u32[]{:S(2)}, u32[]{:S(2)}) collective-permute-start(bf16[2,512,512]{2,1,0:T(8,128)(2,1)S(1)} %broadcast_select_fusion.51), channel_id=1, source_target_pairs={{0,1},{1,0},{2,3},{3,2},{4,5},{5,4},{6,7},{7,6},{8,9},{9,8},{10,11... | collective-permute-start | bytes 3145736 | tf_op jit(solution)/shard_map/ppermute | solution.py:70
  95.5 15.8 %collective-permute-start.66 = (bf16[64,512]{1,0:T(8,128)(2,1)S(1)}, bf16[64,512]{1,0:T(8,128)(2,1)S(1)}, u32[]{:S(2)}, u32[]{:S(2)}) collective-permute-start(bf16[64,512]{1,0:T(8,128)(2,1)S(1)} %get-tuple-element.32), channel_id=1, source_target_pairs={{124,126},{4,6},{12,14},{20,22},{28,30},{36,38},{44,46},{52,54},{6... | collective-permute-start | bytes 196616 | tf_op jit(solution)/shard_map/ppermute | solution.py:66
  96.8 14.5 %collective-permute-start.65 = (bf16[64,512]{1,0:T(8,128)(2,1)S(1)}, bf16[64,512]{1,0:T(8,128)(2,1)S(1)}, u32[]{:S(2)}, u32[]{:S(2)}) collective-permute-start(bf16[64,512]{1,0:T(8,128)(2,1)S(1)} %get-tuple-element.32), channel_id=1, source_target_pairs={{124,122},{4,2},{12,10},{20,18},{28,26},{36,34},{44,42},{52,50},{6... | collective-permute-start | bytes 196616 | tf_op jit(solution)/shard_map/ppermute | solution.py:66
  98.2 21.3 %collective-permute-start.61 = (bf16[64,512]{1,0:T(8,128)(2,1)S(1)}, bf16[64,512]{1,0:T(8,128)(2,1)S(1)}, u32[]{:S(2)}, u32[]{:S(2)}) collective-permute-start(bf16[64,512]{1,0:T(8,128)(2,1)S(1)} %get-tuple-element.117), channel_id=1, source_target_pairs={{120,118},{0,126},{8,6},{16,14},{24,22},{32,30},{40,38},{48,46},{5... | collective-permute-start | bytes 196616 | tf_op jit(solution)/shard_map/ppermute | solution.py:66
  99.5 20.0 %collective-permute-start.60 = (bf16[64,512]{1,0:T(8,128)(2,1)S(1)}, bf16[64,512]{1,0:T(8,128)(2,1)S(1)}, u32[]{:S(2)}, u32[]{:S(2)}) collective-permute-start(bf16[64,512]{1,0:T(8,128)(2,1)S(1)} %get-tuple-element.117), channel_id=1, source_target_pairs={{120,122},{0,2},{8,10},{16,18},{24,26},{32,34},{40,42},{48,50},{56... | collective-permute-start | bytes 196616 | tf_op jit(solution)/shard_map/ppermute | solution.py:66
  162.7 14.7 %collective-permute-start.20 = (bf16[512,1024]{0,1:T(8,128)(2,1)S(1)}, bf16[512,1024]{0,1:T(8,128)(2,1)S(1)}, u32[]{:S(2)}, u32[]{:S(2)}) collective-permute-start(bf16[512,1024]{0,1:T(8,128)(2,1)S(1)} %get-tuple-element.68), channel_id=1, source_target_pairs={{20,4},{84,68},{21,5},{85,69}} | collective-permute-start | bytes 3145736 | tf_op jit(solution)/shard_map/ppermute | solution.py:66
  163.5 19.0 %collective-permute-start.19 = (bf16[512,1024]{0,1:T(8,128)(2,1)S(1)}, bf16[512,1024]{0,1:T(8,128)(2,1)}, u32[]{:S(2)}, u32[]{:S(2)}) collective-permute-start(bf16[512,1024]{0,1:T(8,128)(2,1)S(1)} %get-tuple-element.69), channel_id=1, source_target_pairs={{20,36},{84,100},{21,37},{85,101}} | collective-permute-start | bytes 3145736 | tf_op jit(solution)/shard_map/ppermute | solution.py:66
  172.5 13.6 %collective-permute-start.25 = (bf16[512,1024]{1,0:T(8,128)(2,1)}, bf16[512,1024]{1,0:T(8,128)(2,1)}, u32[]{:S(2)}, u32[]{:S(2)}) collective-permute-start(bf16[512,1024]{1,0:T(8,128)(2,1)} %get-tuple-element.31), channel_id=1, source_target_pairs={{52,68},{53,69}} | collective-permute-start | bytes 3145736 | tf_op jit(solution)/shard_map/ppermute | solution.py:66
  251.2 14.5 %collective-permute-start.46 = (bf16[512,1024]{0,1:T(8,128)(2,1)S(1)}, bf16[512,1024]{0,1:T(8,128)(2,1)S(1)}, u32[]{:S(2)}, u32[]{:S(2)}) collective-permute-start(bf16[512,1024]{0,1:T(8,128)(2,1)S(1)} %get-tuple-element.60), channel_id=1, source_target_pairs={{124,120},{12,8},{28,24},{44,40},{60,56},{76,72},{92,88},{108,104}... | collective-permute-start | bytes 3145736 | tf_op jit(solution)/shard_map/ppermute | solution.py:66
  252.1 20.9 %collective-permute-start.45 = (bf16[512,1024]{0,1:T(8,128)(2,1)S(1)}, bf16[512,1024]{0,1:T(8,128)(2,1)}, u32[]{:S(2)}, u32[]{:S(2)}) collective-permute-start(bf16[512,1024]{0,1:T(8,128)(2,1)S(1)} %get-tuple-element.61), channel_id=1, source_target_pairs={{124,0},{12,16},{28,32},{44,48},{60,64},{76,80},{92,96},{108,112},... | collective-permute-start | bytes 3145736 | tf_op jit(solution)/shard_map/ppermute | solution.py:66
  260.7 17.1 %collective-permute-start.51 = (bf16[512,1024]{1,0:T(8,128)(2,1)}, bf16[512,1024]{1,0:T(8,128)(2,1)}, u32[]{:S(2)}, u32[]{:S(2)}) collective-permute-start(bf16[512,1024]{1,0:T(8,128)(2,1)} %get-tuple-element.27), channel_id=1, source_target_pairs={{4,8},{20,24},{36,40},{52,56},{68,72},{84,88},{100,104},{5,9},{21,... | collective-permute-start | bytes 3145736 | tf_op jit(solution)/shard_map/ppermute | solution.py:66
  262.4 15.5 %collective-permute-start.50 = (bf16[512,1024]{1,0:T(8,128)(2,1)}, bf16[512,1024]{1,0:T(8,128)(2,1)}, u32[]{:S(2)}, u32[]{:S(2)}) collective-permute-start(bf16[512,1024]{1,0:T(8,128)(2,1)} %get-tuple-element.27), channel_id=1, source_target_pairs={{4,0},{20,16},{36,32},{52,48},{68,64},{84,80},{100,96},{116,112},{... | collective-permute-start | bytes 3145736 | tf_op jit(solution)/shard_map/ppermute | solution.py:66
  264.0 16.8 %collective-permute-start.44 = (bf16[512,1024]{1,0:T(8,128)(2,1)}, bf16[512,1024]{1,0:T(8,128)(2,1)}, u32[]{:S(2)}, u32[]{:S(2)}) collective-permute-start(bf16[512,1024]{1,0:T(8,128)(2,1)} %get-tuple-element.121), channel_id=1, source_target_pairs={{124,120},{12,8},{28,24},{44,40},{60,56},{76,72},{92,88},{108,104}... | collective-permute-start | bytes 3145736 | tf_op jit(solution)/shard_map/ppermute | solution.py:66
  266.7 14.2 %collective-permute-start.43 = (bf16[512,1024]{1,0:T(8,128)(2,1)}, bf16[512,1024]{1,0:T(8,128)(2,1)}, u32[]{:S(2)}, u32[]{:S(2)}) collective-permute-start(bf16[512,1024]{1,0:T(8,128)(2,1)} %get-tuple-element.121), channel_id=1, source_target_pairs={{124,0},{12,16},{28,32},{44,48},{60,64},{76,80},{92,96},{108,112},... | collective-permute-start | bytes 3145736 | tf_op jit(solution)/shard_map/ppermute | solution.py:66
  304.7 239.0 %collective-permute-start.64 = (bf16[512,1024]{1,0:T(8,128)(2,1)}, bf16[512,1024]{1,0:T(8,128)(2,1)}, u32[]{:S(2)}, u32[]{:S(2)}) collective-permute-start(bf16[512,1024]{1,0:T(8,128)(2,1)} %get-tuple-element.26), channel_id=1, source_target_pairs={{124,126},{4,6},{12,14},{20,22},{28,30},{36,38},{44,46},{52,54},{6... | collective-permute-start | bytes 3145736 | tf_op jit(solution)/shard_map/ppermute | solution.py:66
  306.0 237.7 %collective-permute-start.63 = (bf16[512,1024]{1,0:T(8,128)(2,1)}, bf16[512,1024]{1,0:T(8,128)(2,1)}, u32[]{:S(2)}, u32[]{:S(2)}) collective-permute-start(bf16[512,1024]{1,0:T(8,128)(2,1)} %get-tuple-element.26), channel_id=1, source_target_pairs={{124,122},{4,2},{12,10},{20,18},{28,26},{36,34},{44,42},{52,50},{6... | collective-permute-start | bytes 3145736 | tf_op jit(solution)/shard_map/ppermute | solution.py:66
  321.8 216.6 %collective-permute-start.59 = (bf16[512,1024]{0,1:T(8,128)(2,1)}, bf16[512,1024]{0,1:T(8,128)(2,1)}, u32[]{:S(2)}, u32[]{:S(2)}) collective-permute-start(bf16[512,1024]{0,1:T(8,128)(2,1)} %broadcast_select_fusion.2), channel_id=1, source_target_pairs={{120,118},{0,126},{8,6},{16,14},{24,22},{32,30},{40,38},{48,46},{5... | collective-permute-start | bytes 3145736 | tf_op jit(solution)/shard_map/ppermute | solution.py:66
  328.1 232.7 %collective-permute-start.57 = (bf16[512,1024]{1,0:T(8,128)(2,1)}, bf16[512,1024]{1,0:T(8,128)(2,1)}, u32[]{:S(2)}, u32[]{:S(2)}) collective-permute-start(bf16[512,1024]{1,0:T(8,128)(2,1)} %fusion.112), channel_id=1, source_target_pairs={{120,118},{0,126},{8,6},{16,14},{24,22},{32,30},{40,38},{48,46},{5... | collective-permute-start | bytes 3145736 | tf_op jit(solution)/shard_map/ppermute | solution.py:66
  329.4 231.4 %collective-permute-start.56 = (bf16[512,1024]{1,0:T(8,128)(2,1)}, bf16[512,1024]{1,0:T(8,128)(2,1)}, u32[]{:S(2)}, u32[]{:S(2)}) collective-permute-start(bf16[512,1024]{1,0:T(8,128)(2,1)} %fusion.112), channel_id=1, source_target_pairs={{120,122},{0,2},{8,10},{16,18},{24,26},{32,34},{40,42},{48,50},{56... | collective-permute-start | bytes 3145736 | tf_op jit(solution)/shard_map/ppermute | solution.py:66
  542.7 21.2 %collective-permute-start.62 = (bf16[1,512,512]{1,2,0:T(8,128)(2,1)}, bf16[1,512,512]{1,2,0:T(8,128)(2,1)}, u32[]{:S(2)}, u32[]{:S(2)}) collective-permute-start(bf16[1,512,512]{1,2,0:T(8,128)(2,1)} %get-tuple-element.85), channel_id=1, source_target_pairs={{0,1},{1,0},{2,3},{3,2},{4,5},{5,4},{6,7},{7,6},{8,9},{9,8},{10,11... | collective-permute-start | bytes 1572872 | tf_op jit(solution)/shard_map/ppermute | solution.py:70
  (130 other events, 739.3 us)
Sparse Core Ops, SparseCore 0:
  9.7 15.8 all-gather.5
  27.2 14.6 all-gather.7

commit v3 on v2

--- a/solution.py
+++ b/solution.py
@@ -80,9 +80,11 @@
     return jnp.concatenate([jnp.swapaxes(top, 1, 2), jnp.swapaxes(bottom, 1, 2)], axis=2)
 
 
-def join_tiles(halves, is_first):
+def join_tiles(halves, is_first, axis=-1):
     got = swap_tiles(halves)
-    return jnp.where(is_first, jnp.concatenate([halves, got], axis=-1), jnp.concatenate([got, halves], axis=-1))
+    return jnp.where(
+        is_first, jnp.concatenate([halves, got], axis=axis), jnp.concatenate([got, halves], axis=axis)
+    )
 
 
 def body(pivot_inverse, mult_left, mult_right, mult_tip, root_cross, root_tip):
@@ -108,9 +110,9 @@
     own_left = mult_left[0]
     own_right = mult_right[0]
     inverse_rows = pivot_inverse[0]
-    full_left = lax.all_gather(own_left, "tile", axis=0, tiled=True)
-    full_right = lax.all_gather(own_right, "tile", axis=0, tiled=True)
-    full_tip = lax.all_gather(mult_tip[0], "tile", axis=0, tiled=True)
+    full_left = join_tiles(own_left, is_first, axis=0)
+    full_right = join_tiles(own_right, is_first, axis=0)
+    full_tip = join_tiles(mult_tip[0], is_first, axis=0)
     first = jnp.where(role, full_left, full_right)
     second = jnp.where(role, full_right, full_left)
     stacked = jnp.concatenate([first, second, full_tip], axis=0)
@@ -123,7 +125,7 @@
     zero_rows = jnp.zeros_like(inverse_rows)
     zero_tip = jnp.zeros_like(root_cross)
 
-    up_diag, up_tip, up_self_left, up_self_right = inverse_rows, root_cross, zero_rows, zero_rows
+    up_diag, up_tip, up_self_left, up_self_right = inverse_rows, root_cross, None, None
     state_diag, state_tip = inverse_rows, root_cross
     state_cross = jnp.zeros((tile_rows, 2 * inverse_rows.shape[1]), inverse_rows.dtype)
     history = {levels: (state_diag, state_tip)}
@@ -132,11 +134,16 @@
         step_plan = levels_plan[level_index]
         active = table(step_plan["active"])
 
-        from_left = send((up_diag, up_tip, up_self_right), step_plan["crit_from_left"])
-        from_right = send((up_diag, up_tip, up_self_left), step_plan["crit_from_right"])
+        from_left = send((up_diag, up_tip), step_plan["crit_from_left"])
+        from_right = send((up_diag, up_tip), step_plan["crit_from_right"])
         near_diag = pick(role, *(None if r is None else r[0] for r in (from_left, from_right)))
         near_tip = pick(role, *(None if r is None else r[1] for r in (from_left, from_right)))
-        cross = pick(role, *(None if r is None else r[2] for r in (from_left, from_right)))
+        if up_self_left is None:
+            cross = None
+        else:
+            cross_left = send(up_self_right, step_plan["crit_from_left"])
+            cross_right = send(up_self_left, step_plan["crit_from_right"])
+            cross = pick(role, cross_left, cross_right)
 
         older = history.get(level_index + 2)
         far_diag, far_tip = zero_rows, zero_tip
@@ -147,18 +154,20 @@
                 far_diag = pick(role, *(None if r is None else r[0] for r in (g_right, g_left)))
                 far_tip = pick(role, *(None if r is None else r[1] for r in (g_right, g_left)))
 
-        cross_turned = tile_transpose(cross[None], is_first)[0]
         tips_full = join_tiles(jnp.stack([near_tip, far_tip]), is_first)
-        operand = jnp.concatenate(
-            [
-                jnp.concatenate([near_diag, cross, near_tip.T], axis=1),
-                jnp.concatenate([cross_turned, far_diag, far_tip.T], axis=1),
-            ],
-            axis=0,
-        )
-        fresh_both = (-product(operand, stacked)).astype(jnp.bfloat16)
-        fresh_near = fresh_both[:tile_rows]
-        fresh_far = fresh_both[tile_rows:]
+        if cross is None:
+            near_operand = jnp.concatenate([near_diag, near_tip.T], axis=1)
+            near_mult = jnp.concatenate([first, full_tip], axis=0)
+            far_operand = jnp.concatenate([far_diag, far_tip.T], axis=1)
+            far_mult = jnp.concatenate([second, full_tip], axis=0)
+        else:
+            cross_turned = tile_transpose(cross[None], is_first)[0]
+            near_operand = jnp.concatenate([near_diag, cross, near_tip.T], axis=1)
+            near_mult = stacked
+            far_operand = jnp.concatenate([cross_turned, far_diag, far_tip.T], axis=1)
+            far_mult = stacked
+        fresh_far = (-product(far_operand, far_mult)).astype(jnp.bfloat16)
+        fresh_near = (-product(near_operand, near_mult)).astype(jnp.bfloat16)
         tip_y = product(tips_full[0], first_cols) + product(tips_full[1], second_cols) + tip_own
         fresh_tip = (-tip_y).astype(jnp.bfloat16)
         turned = tile_transpose(jnp.stack([fresh_near, fresh_far]), is_first)

time: 628 us -> 612 us (0.975)
  the two profiles are of different devices: /device:TPU:31 before, /device:TPU:95 now
where the time goes in v3:
time: 612 us; the launch traced here: 600 us
  waiting for transfers between devices  241 us (39%)
  other arithmetic  134 us (22%)
  matrix products  75.9 us (12%)
  local copies, waits for them, and re-layouts  73.4 us (12%)
  starting transfers between devices  72.5 us (12%)
    ppermute x50, waiting for transfers between devices, send(): return lax.ppermute(values, 'tm', pairs)  237 us
    dot_general x31, matrix products, product(): jnp.dot(left_matrix, right_matrix, preferred_element_type=jnp.float32)  75.9 us
    ppermute x50, starting transfers between devices, send(): return lax.ppermute(values, 'tm', pairs)  64.5 us
    select_n x14, other arithmetic, pick(): return jnp.where(flag, if_true, if_false)  30.4 us
    select_n x11, other arithmetic, body(): self_left = jnp.where(role, own_near, own_far)  23.3 us
    transpose x11, other arithmetic, tile_transpose(): jnp.swapaxes(top, 1, 2)  17.3 us
    unnamed x195, local copies, waits for them, and re-layouts  13.9 us
  transfers between devices with their start and end apart: 70, of which 8 were waited for; matrix products, arithmetic and copies ran while one was open for 32% of the time, Pallas kernels for 0%

profile of v3, /device:TPU:95, one launch (start us, length us, event | category | flops | bytes accessed | tf_op | source)
XLA Modules:
  0.0 600.0 jit_solution(15669363215548655971)
XLA Ops:
  7.7 4.2 broadcast_select_fusion.1
  53.3 16.6 %collective-permute-done.67 = bf16[64,512]{1,0:T(8,128)(2,1)S(1)} collective-permute-done((bf16[64,512]{1,0:T(8,128)(2,1)S(1)}, bf16[64,512]{1,0:T(8,128)(2,1)S(1)}, u32[]{:S(2)}, u32[]{:S(2)}) %collective-permute-start.67) | collective-permute-done | bytes 65568 | tf_op jit(solution)/shard_map/ppermute | solution.py:66
  71.1 7.0 %collective-permute-done.62 = bf16[64,512]{1,0:T(8,128)(2,1)S(1)} collective-permute-done((bf16[64,512]{1,0:T(8,128)(2,1)S(1)}, bf16[64,512]{1,0:T(8,128)(2,1)S(1)}, u32[]{:S(2)}, u32[]{:S(2)}) %collective-permute-start.62) | collective-permute-done | bytes 65568 | tf_op jit(solution)/shard_map/ppermute | solution.py:66
  91.4 4.9 fusion.100
  103.7 2.9 broadcast_select_fusion.19
  117.9 4.6 fusion.141
  133.5 4.0 fusion.144
  152.8 6.9 %broadcast_select_fusion.31 = (bf16[512,1024]{1,0:T(8,128)(2,1)}, bf16[512,1024]{1,0:T(8,128)(2,1)}, bf16[512,1024]{1,0:T(8,128)(2,1)}) fusion(pred[]{:T(512)} %bitcast.59, bf16[512,1024]{1,0:T(8,128)(2,1)} %fusion.100, bf16[1,512,1024]{2,1,0:T(8,128)(2,1)} %param.13, pred[]{:T(512)} %bitcast.41, bf16[64,1024]{1,0:T(8,128)(2,1)S(1)} %copy-done.59, ...), kind=kOutput, calls=%fused_computation.256 | convolution fusion | flops 2236678144 | bytes 11730946 | tf_op jit(solution)/shard_map/dot_general | solution.py:10
  200.6 4.9 fusion.102
  226.5 2.9 copy.127
  239.8 3.6 subtract_convert_fusion
  245.7 4.0 broadcast_select_fusion.29
  292.9 3.3 bitcast_select_fusion
  301.1 5.0 fusion.103
  307.3 189.3 %collective-permute-done.65 = bf16[512,1024]{1,0:T(8,128)(2,1)} collective-permute-done((bf16[512,1024]{1,0:T(8,128)(2,1)}, bf16[512,1024]{1,0:T(8,128)(2,1)}, u32[]{:S(2)}, u32[]{:S(2)}) %collective-permute-start.65) | collective-permute-done | bytes 1048608 | tf_op jit(solution)/shard_map/ppermute | solution.py:66
  499.8 3.9 copy.161
  508.9 14.0 %collective-permute-done.60 = bf16[512,1024]{0,1:T(8,128)(2,1)} collective-permute-done((bf16[512,1024]{0,1:T(8,128)(2,1)}, bf16[512,1024]{0,1:T(8,128)(2,1)}, u32[]{:S(2)}, u32[]{:S(2)}) %collective-permute-start.60) | collective-permute-done | bytes 1048608 | tf_op jit(solution)/shard_map/ppermute | solution.py:66
  523.0 2.9 broadcast_select_fusion.11
  535.7 9.7 %collective-permute-done.58 = bf16[512,1024]{1,0:T(8,128)(2,1)} collective-permute-done((bf16[512,1024]{1,0:T(8,128)(2,1)}, bf16[512,1024]{1,0:T(8,128)(2,1)}, u32[]{:S(2)}, u32[]{:S(2)}) %collective-permute-start.58) | collective-permute-done | bytes 1048608 | tf_op jit(solution)/shard_map/ppermute | solution.py:66
  547.4 3.6 fusion.165
  569.2 4.0 copy.162
  581.8 6.4 %maximum_select_fusion.2 = bf16[1,512,2048]{1,2,0:T(8,128)(2,1)} fusion(bf16[1,512,1024]{1,2,0:T(8,128)(2,1)S(1)} %get-tuple-element.55, bf16[1,512,1024]{1,2,0:T(8,128)(2,1)S(1)} %get-tuple-element.52, bf16[1,512,1024]{1,2,0:T(8,128)(2,1)S(1)} %broadcast_select_fusion.25, bf16[1,512,1024]{1,2,0:T(8,128)(2,1)S(1)} %copy-done.50, ...), kind=kLoop, calls=%fused_computation.139 | loop fusion | flops 23068672 | bytes 14680070 | tf_op jit(solution)/shard_map/jit(_where)/select_n | solution.py:183
  588.2 3.9 copy.163
  592.2 7.4 %fusion.174 = bf16[1,512,1024]{2,1,0:T(8,128)(2,1)} fusion(bf16[512,64]{0,1:T(8,128)(2,1)S(1)} %copy-done.84, bf16[512,1024]{0,1:T(8,128)(2,1)S(1)} %get-tuple-element.53, bf16[512,1024]{0,1:T(8,128)(2,1)} %get-tuple-element.54, bf16[512,1024]{1,0:T(8,128)(2,1)} %fusion.103, bf16[512,1024]{1,0:T(8,128)(2,1)} %get-tuple-element.26, pred[]{:T(512)} %bitcast.109, ...), kind=kOutput, calls=%fused_computation.175 | convolution fusion | flops 2236678144 | bytes 10682370 | tf_op jit(solution)/shard_map/dot_general | solution.py:10
  (469 shorter events, 277.1 us)
Async XLA Ops:
  24.9 16.1 %collective-permute-start = (bf16[512,1024]{1,0:T(8,128)(2,1)}, bf16[512,1024]{1,0:T(8,128)(2,1)}, u32[]{:S(2)}, u32[]{:S(2)}) collective-permute-start(bf16[512,1024]{1,0:T(8,128)(2,1)} %bitcast.1), channel_id=1, source_target_pairs={{116,52},{117,53}} | collective-permute-start | bytes 3145736 | tf_op jit(solution)/shard_map/ppermute | solution.py:66
  48.2 34.7 %collective-permute-start.5 = (bf16[2,512,512]{2,1,0:T(8,128)(2,1)S(1)}, bf16[2,512,512]{2,1,0:T(8,128)(2,1)S(1)}, u32[]{:S(2)}, u32[]{:S(2)}) collective-permute-start(bf16[2,512,512]{2,1,0:T(8,128)(2,1)S(1)} %broadcast_select_fusion.51), channel_id=1, source_target_pairs={{0,1},{1,0},{2,3},{3,2},{4,5},{5,4},{6,7},{7,6},{8,9},{9,8},{10,11... | collective-permute-start | bytes 3145736 | tf_op jit(solution)/shard_map/ppermute | solution.py:70
  48.6 21.3 %collective-permute-start.67 = (bf16[64,512]{1,0:T(8,128)(2,1)S(1)}, bf16[64,512]{1,0:T(8,128)(2,1)S(1)}, u32[]{:S(2)}, u32[]{:S(2)}) collective-permute-start(bf16[64,512]{1,0:T(8,128)(2,1)S(1)} %get-tuple-element.32), channel_id=1, source_target_pairs={{124,126},{4,6},{12,14},{20,22},{28,30},{36,38},{44,46},{52,54},{6... | collective-permute-start | bytes 196616 | tf_op jit(solution)/shard_map/ppermute | solution.py:66
  49.9 20.0 %collective-permute-start.66 = (bf16[64,512]{1,0:T(8,128)(2,1)S(1)}, bf16[64,512]{1,0:T(8,128)(2,1)S(1)}, u32[]{:S(2)}, u32[]{:S(2)}) collective-permute-start(bf16[64,512]{1,0:T(8,128)(2,1)S(1)} %get-tuple-element.32), channel_id=1, source_target_pairs={{124,122},{4,2},{12,10},{20,18},{28,26},{36,34},{44,42},{52,50},{6... | collective-permute-start | bytes 196616 | tf_op jit(solution)/shard_map/ppermute | solution.py:66
  51.4 26.8 %collective-permute-start.62 = (bf16[64,512]{1,0:T(8,128)(2,1)S(1)}, bf16[64,512]{1,0:T(8,128)(2,1)S(1)}, u32[]{:S(2)}, u32[]{:S(2)}) collective-permute-start(bf16[64,512]{1,0:T(8,128)(2,1)S(1)} %get-tuple-element.106), channel_id=1, source_target_pairs={{120,118},{0,126},{8,6},{16,14},{24,22},{32,30},{40,38},{48,46},{5... | collective-permute-start | bytes 196616 | tf_op jit(solution)/shard_map/ppermute | solution.py:66
  52.7 25.5 %collective-permute-start.61 = (bf16[64,512]{1,0:T(8,128)(2,1)S(1)}, bf16[64,512]{1,0:T(8,128)(2,1)S(1)}, u32[]{:S(2)}, u32[]{:S(2)}) collective-permute-start(bf16[64,512]{1,0:T(8,128)(2,1)S(1)} %get-tuple-element.106), channel_id=1, source_target_pairs={{120,122},{0,2},{8,10},{16,18},{24,26},{32,34},{40,42},{48,50},{56... | collective-permute-start | bytes 196616 | tf_op jit(solution)/shard_map/ppermute | solution.py:66
  87.9 15.8 %collective-permute-start.10 = (bf16[512,1024]{0,1:T(8,128)(2,1)}, bf16[512,1024]{0,1:T(8,128)(2,1)}, u32[]{:S(2)}, u32[]{:S(2)}) collective-permute-start(bf16[512,1024]{0,1:T(8,128)(2,1)} %get-tuple-element.62), channel_id=1, source_target_pairs={{52,20},{53,21}} | collective-permute-start | bytes 3145736 | tf_op jit(solution)/shard_map/ppermute | solution.py:66
  96.3 19.5 %collective-permute-start.8 = (bf16[512,1024]{1,0:T(8,128)(2,1)}, bf16[512,1024]{1,0:T(8,128)(2,1)}, u32[]{:S(2)}, u32[]{:S(2)}) collective-permute-start(bf16[512,1024]{1,0:T(8,128)(2,1)} %fusion.100), channel_id=1, source_target_pairs={{52,20},{53,21}} | collective-permute-start | bytes 3145736 | tf_op jit(solution)/shard_map/ppermute | solution.py:66
  98.0 17.8 %collective-permute-start.7 = (bf16[512,1024]{1,0:T(8,128)(2,1)}, bf16[512,1024]{1,0:T(8,128)(2,1)}, u32[]{:S(2)}, u32[]{:S(2)}) collective-permute-start(bf16[512,1024]{1,0:T(8,128)(2,1)} %fusion.100), channel_id=1, source_target_pairs={{52,84},{53,85}} | collective-permute-start | bytes 3145736 | tf_op jit(solution)/shard_map/ppermute | solution.py:66
  99.7 33.8 %collective-permute-start.14 = (bf16[512,1024]{1,0:T(8,128)(2,1)}, bf16[512,1024]{1,0:T(8,128)(2,1)}, u32[]{:S(2)}, u32[]{:S(2)}) collective-permute-start(bf16[512,1024]{1,0:T(8,128)(2,1)} %bitcast.1), channel_id=1, source_target_pairs={{116,84},{117,85}} | collective-permute-start | bytes 3145736 | tf_op jit(solution)/shard_map/ppermute | solution.py:66
  149.0 18.0 %collective-permute-start.21 = (bf16[512,1024]{1,0:T(8,128)(2,1)}, bf16[512,1024]{1,0:T(8,128)(2,1)}, u32[]{:S(2)}, u32[]{:S(2)}) collective-permute-start(bf16[512,1024]{1,0:T(8,128)(2,1)} %get-tuple-element.60), channel_id=1, source_target_pairs={{20,4},{84,68},{21,5},{85,69}} | collective-permute-start | bytes 3145736 | tf_op jit(solution)/shard_map/ppermute | solution.py:66
  150.7 18.8 %collective-permute-start.20 = (bf16[512,1024]{1,0:T(8,128)(2,1)}, bf16[512,1024]{1,0:T(8,128)(2,1)}, u32[]{:S(2)}, u32[]{:S(2)}) collective-permute-start(bf16[512,1024]{1,0:T(8,128)(2,1)} %get-tuple-element.61), channel_id=1, source_target_pairs={{20,36},{84,100},{21,37},{85,101}} | collective-permute-start | bytes 3145736 | tf_op jit(solution)/shard_map/ppermute | solution.py:66
  186.7 20.5 %collective-permute-start.39 = (bf16[512,1024]{0,1:T(8,128)(2,1)}, bf16[512,1024]{0,1:T(8,128)(2,1)}, u32[]{:S(2)}, u32[]{:S(2)}) collective-permute-start(bf16[512,1024]{0,1:T(8,128)(2,1)} %copy.124), channel_id=1, source_target_pairs={{20,28},{52,60},{84,92},{21,29},{53,61},{85,93}} | collective-permute-start | bytes 3145736 | tf_op jit(solution)/shard_map/ppermute | solution.py:66
  188.3 21.3 %collective-permute-start.38 = (bf16[512,1024]{0,1:T(8,128)(2,1)}, bf16[512,1024]{0,1:T(8,128)(2,1)}, u32[]{:S(2)}, u32[]{:S(2)}) collective-permute-start(bf16[512,1024]{0,1:T(8,128)(2,1)} %copy.124), channel_id=1, source_target_pairs={{20,12},{52,44},{84,76},{116,108},{21,13},{53,45},{85,77},{117,109}} | collective-permute-start | bytes 3145736 | tf_op jit(solution)/shard_map/ppermute | solution.py:66
  197.1 14.4 %collective-permute-start.34 = (bf16[512,1024]{1,0:T(8,128)(2,1)}, bf16[512,1024]{1,0:T(8,128)(2,1)}, u32[]{:S(2)}, u32[]{:S(2)}) collective-permute-start(bf16[512,1024]{1,0:T(8,128)(2,1)} %get-tuple-element.58), channel_id=1, source_target_pairs={{4,124},{36,28},{68,60},{100,92},{5,125},{37,29},{69,61},{101,93}} | collective-permute-start | bytes 3145736 | tf_op jit(solution)/shard_map/ppermute | solution.py:66
  236.3 18.6 %collective-permute-start.47 = (bf16[512,1024]{0,1:T(8,128)(2,1)}, bf16[512,1024]{0,1:T(8,128)(2,1)}, u32[]{:S(2)}, u32[]{:S(2)}) collective-permute-start(bf16[512,1024]{0,1:T(8,128)(2,1)} %get-tuple-element.56), channel_id=1, source_target_pairs={{124,120},{12,8},{28,24},{44,40},{60,56},{76,72},{92,88},{108,104}... | collective-permute-start | bytes 3145736 | tf_op jit(solution)/shard_map/ppermute | solution.py:66
  238.1 19.2 %collective-permute-start.46 = (bf16[512,1024]{0,1:T(8,128)(2,1)}, bf16[512,1024]{0,1:T(8,128)(2,1)}, u32[]{:S(2)}, u32[]{:S(2)}) collective-permute-start(bf16[512,1024]{0,1:T(8,128)(2,1)} %get-tuple-element.57), channel_id=1, source_target_pairs={{124,0},{12,16},{28,32},{44,48},{60,64},{76,80},{92,96},{108,112},... | collective-permute-start | bytes 3145736 | tf_op jit(solution)/shard_map/ppermute | solution.py:66
  282.3 214.3 %collective-permute-start.65 = (bf16[512,1024]{1,0:T(8,128)(2,1)}, bf16[512,1024]{1,0:T(8,128)(2,1)}, u32[]{:S(2)}, u32[]{:S(2)}) collective-permute-start(bf16[512,1024]{1,0:T(8,128)(2,1)} %get-tuple-element.26), channel_id=1, source_target_pairs={{124,126},{4,6},{12,14},{20,22},{28,30},{36,38},{44,46},{52,54},{6... | collective-permute-start | bytes 3145736 | tf_op jit(solution)/shard_map/ppermute | solution.py:66
  283.6 220.2 %collective-permute-start.64 = (bf16[512,1024]{1,0:T(8,128)(2,1)}, bf16[512,1024]{1,0:T(8,128)(2,1)}, u32[]{:S(2)}, u32[]{:S(2)}) collective-permute-start(bf16[512,1024]{1,0:T(8,128)(2,1)} %get-tuple-element.26), channel_id=1, source_target_pairs={{124,122},{4,2},{12,10},{20,18},{28,26},{36,34},{44,42},{52,50},{6... | collective-permute-start | bytes 3145736 | tf_op jit(solution)/shard_map/ppermute | solution.py:66
  296.2 210.4 %collective-permute-start.59 = (bf16[512,1024]{1,0:T(8,128)(2,1)}, bf16[512,1024]{1,0:T(8,128)(2,1)}, u32[]{:S(2)}, u32[]{:S(2)}) collective-permute-start(bf16[512,1024]{1,0:T(8,128)(2,1)} %bitcast_select_fusion), channel_id=1, source_target_pairs={{120,122},{0,2},{8,10},{16,18},{24,26},{32,34},{40,42},{48,50},{56... | collective-permute-start | bytes 3145736 | tf_op jit(solution)/shard_map/ppermute | solution.py:66
  299.7 223.2 %collective-permute-start.60 = (bf16[512,1024]{0,1:T(8,128)(2,1)}, bf16[512,1024]{0,1:T(8,128)(2,1)}, u32[]{:S(2)}, u32[]{:S(2)}) collective-permute-start(bf16[512,1024]{0,1:T(8,128)(2,1)} %broadcast_select_fusion.10), channel_id=1, source_target_pairs={{120,118},{0,126},{8,6},{16,14},{24,22},{32,30},{40,38},{48,46},{5... | collective-permute-start | bytes 3145736 | tf_op jit(solution)/shard_map/ppermute | solution.py:66
  306.1 239.4 %collective-permute-start.58 = (bf16[512,1024]{1,0:T(8,128)(2,1)}, bf16[512,1024]{1,0:T(8,128)(2,1)}, u32[]{:S(2)}, u32[]{:S(2)}) collective-permute-start(bf16[512,1024]{1,0:T(8,128)(2,1)} %fusion.103), channel_id=1, source_target_pairs={{120,118},{0,126},{8,6},{16,14},{24,22},{32,30},{40,38},{48,46},{5... | collective-permute-start | bytes 3145736 | tf_op jit(solution)/shard_map/ppermute | solution.py:66
  496.6 48.8 %collective-permute-start.57 = (bf16[512,1024]{1,0:T(8,128)(2,1)}, bf16[512,1024]{1,0:T(8,128)(2,1)}, u32[]{:S(2)}, u32[]{:S(2)}) collective-permute-start(bf16[512,1024]{1,0:T(8,128)(2,1)} %fusion.103), channel_id=1, source_target_pairs={{120,122},{0,2},{8,10},{16,18},{24,26},{32,34},{40,42},{48,50},{56... | collective-permute-start | bytes 3145736 | tf_op jit(solution)/shard_map/ppermute | solution.py:66
  534.7 16.3 %collective-permute-start.63 = (bf16[1,512,512]{1,2,0:T(8,128)(2,1)}, bf16[1,512,512]{1,2,0:T(8,128)(2,1)}, u32[]{:S(2)}, u32[]{:S(2)}) collective-permute-start(bf16[1,512,512]{1,2,0:T(8,128)(2,1)} %get-tuple-element.71), channel_id=1, source_target_pairs={{0,1},{1,0},{2,3},{3,2},{4,5},{5,4},{6,7},{7,6},{8,9},{9,8},{10,11... | collective-permute-start | bytes 1572872 | tf_op jit(solution)/shard_map/ppermute | solution.py:70
  (142 other events, 1099.3 us)

commit v4 on v3

--- a/solution.py
+++ b/solution.py
@@ -181,6 +181,8 @@
         state_diag = jnp.where(active, fresh_diag, state_diag)
         state_tip = jnp.where(active, fresh_tip, state_tip)
         state_cross = jnp.where(active, jnp.concatenate([self_left, self_right], axis=1), state_cross)
+        if level_index > 0:
+            state_diag, state_tip, state_cross = lax.optimization_barrier((state_diag, state_tip, state_cross))
         history[level_index] = (state_diag, state_tip)
         up_diag, up_tip, up_self_left, up_self_right = fresh_diag, fresh_tip, self_left, self_right
 

time: 612 us -> 599 us (0.979)
  the two profiles are of different devices: /device:TPU:95 before, /device:TPU:47 now
where the time goes in v4:
time: 599 us; the launch traced here: 588 us
  waiting for transfers between devices  268 us (45%)
  other arithmetic  124 us (21%)
  matrix products  76.1 us (13%)
  starting transfers between devices  65.8 us (11%)
  local copies, waits for them, and re-layouts  51.4 us (9%)
    ppermute x50, waiting for transfers between devices, send(): return lax.ppermute(values, 'tm', pairs)  268 us
    dot_general x31, matrix products, product(): jnp.dot(left_matrix, right_matrix, preferred_element_type=jnp.float32)  76.1 us
    ppermute x50, starting transfers between devices, send(): return lax.ppermute(values, 'tm', pairs)  58.2 us
    select_n x14, other arithmetic, pick(): return jnp.where(flag, if_true, if_false)  23.6 us
    select_n x5, other arithmetic, body(): jnp.where(active, jnp.concatenate([self_left, self_right], axis=1), state...  15.6 us
    unnamed x193, local copies, waits for them, and re-layouts  13.5 us
  transfers between devices with their start and end apart: 70, of which 5 were waited for; matrix products, arithmetic and copies ran while one was open for 36% of the time, Pallas kernels for 0%

profile of v4, /device:TPU:47, one launch (start us, length us, event | category | flops | bytes accessed | tf_op | source)
XLA Modules:
  0.0 587.9 jit_solution(5959355030890708689)
XLA Ops:
  14.1 4.6 broadcast_select_fusion.2
  23.7 3.1 fusion.133
  32.8 2.9 copy.48
  49.4 3.7 subtract_convert_fusion.5
  58.6 4.0 maximum_select_fusion.2
  73.2 3.9 fusion.138
  93.9 3.7 subtract_convert_fusion.4
  106.5 3.2 broadcast_select_fusion.25
  142.9 3.1 broadcast_select_fusion.28
  151.7 5.9 %broadcast_select_fusion.24 = (bf16[512,1024]{1,0:T(8,128)(2,1)}, bf16[512,1024]{1,0:T(8,128)(2,1)}) fusion(bf16[512,1024]{1,0:T(8,128)(2,1)} %broadcast_select_fusion.25, pred[]{:T(512)} %bitcast.77, bf16[64,1024]{1,0:T(8,128)(2,1)S(1)} %copy-done.67, bf16[1024,1024]{1,0:T(8,128)(2,1)S(1)} %get-tuple-element.67, bf16[1024,1024]{1,0:T(8,128)(2,1)S(1)} %copy-done.7, ...), kind=kOutput, calls=%fused_computation.254 | convolution fusion | flops 2236153856 | bytes 10682369 | tf_op jit(solution)/shard_map/dot_general | solution.py:10
  164.2 3.1 pad_maximum_fusion.5
  167.3 3.9 copy.54
  171.2 3.8 broadcast_select_fusion
  186.1 3.6 fusion.147
  220.9 3.7 subtract_convert_fusion.2
  234.1 3.0 broadcast_select_fusion.23
  241.3 234.9 %collective-permute-done.67 = bf16[64,512]{1,0:T(8,128)(2,1)S(1)} collective-permute-done((bf16[64,512]{1,0:T(8,128)(2,1)S(1)}, bf16[64,512]{1,0:T(8,128)(2,1)S(1)}, u32[]{:S(2)}, u32[]{:S(2)}) %collective-permute-start.67) | collective-permute-done | bytes 65568 | tf_op jit(solution)/shard_map/ppermute | solution.py:66
  504.2 5.8 broadcast_select_fusion.22
  511.3 7.9 %collective-permute-done.65 = bf16[512,1024]{1,0:T(8,128)(2,1)} collective-permute-done((bf16[512,1024]{1,0:T(8,128)(2,1)}, bf16[512,1024]{1,0:T(8,128)(2,1)}, u32[]{:S(2)}, u32[]{:S(2)}) %collective-permute-start.65) | collective-permute-done | bytes 1048608 | tf_op jit(solution)/shard_map/ppermute | solution.py:66
  524.1 3.0 broadcast_select_fusion.32
  527.1 7.0 %collective-permute-done.60 = bf16[512,1024]{0,1:T(8,128)(2,1)} collective-permute-done((bf16[512,1024]{0,1:T(8,128)(2,1)}, bf16[512,1024]{0,1:T(8,128)(2,1)}, u32[]{:S(2)}, u32[]{:S(2)}) %collective-permute-start.60) | collective-permute-done | bytes 1048608 | tf_op jit(solution)/shard_map/ppermute | solution.py:66
  538.6 17.9 %collective-permute-done.58 = bf16[512,1024]{1,0:T(8,128)(2,1)} collective-permute-done((bf16[512,1024]{1,0:T(8,128)(2,1)}, bf16[512,1024]{1,0:T(8,128)(2,1)}, u32[]{:S(2)}, u32[]{:S(2)}) %collective-permute-start.58) | collective-permute-done | bytes 1048608 | tf_op jit(solution)/shard_map/ppermute | solution.py:66
  576.8 4.0 copy.65
  580.8 6.6 %fusion.168 = bf16[1,512,1024]{2,1,0:T(8,128)(2,1)} fusion(bf16[512,1024]{1,0:T(8,128)(2,1)} %get-tuple-element.30, bf16[512,64]{0,1:T(8,128)(2,1)S(1)} %copy-done.86, bf16[512,1024]{0,1:T(8,128)(2,1)} %copy-done.37, bf16[512,1024]{0,1:T(8,128)(2,1)} %copy-done.36, pred[]{:T(512)} %bitcast, bf16[1,512,1024]{2,1,0:T(8,128)(2,1)S(1)} %copy-done.17, ...), kind=kOutput, calls=%fused_computation.170 | convolution fusion | flops 2236153856 | bytes 9633793 | tf_op jit(solution)/shard_map/dot_general | solution.py:10
  (458 shorter events, 238.7 us)
Async XLA Ops:
  2.7 27.1 %collective-permute-start.15 = (bf16[64,512]{1,0:T(8,128)(2,1)}, bf16[64,512]{1,0:T(8,128)(2,1)S(1)}, u32[]{:S(2)}, u32[]{:S(2)}) collective-permute-start(bf16[64,512]{1,0:T(8,128)(2,1)} %param.17), channel_id=1, source_target_pairs={{116,84},{117,85}} | collective-permute-start | bytes 196616 | tf_op jit(solution)/shard_map/ppermute | solution.py:66
  10.3 62.8 %collective-permute-start.14 = (bf16[512,1024]{1,0:T(8,128)(2,1)}, bf16[512,1024]{1,0:T(8,128)(2,1)}, u32[]{:S(2)}, u32[]{:S(2)}) collective-permute-start(bf16[512,1024]{1,0:T(8,128)(2,1)} %bitcast.317), channel_id=1, source_target_pairs={{116,84},{117,85}} | collective-permute-start | bytes 3145736 | tf_op jit(solution)/shard_map/ppermute | solution.py:66
  82.1 28.4 %collective-permute-start.26 = (bf16[512,1024]{1,0:T(8,128)(2,1)}, bf16[512,1024]{1,0:T(8,128)(2,1)}, u32[]{:S(2)}, u32[]{:S(2)}) collective-permute-start(bf16[512,1024]{1,0:T(8,128)(2,1)} %broadcast_select_fusion.26), channel_id=1, source_target_pairs={{52,68},{53,69}} | collective-permute-start | bytes 3145736 | tf_op jit(solution)/shard_map/ppermute | solution.py:66
  83.7 29.0 %collective-permute-start.25 = (bf16[512,1024]{1,0:T(8,128)(2,1)}, bf16[512,1024]{1,0:T(8,128)(2,1)}, u32[]{:S(2)}, u32[]{:S(2)}) collective-permute-start(bf16[512,1024]{1,0:T(8,128)(2,1)} %broadcast_select_fusion.26), channel_id=1, source_target_pairs={{52,36},{116,100},{53,37},{117,101}} | collective-permute-start | bytes 3145736 | tf_op jit(solution)/shard_map/ppermute | solution.py:66
  118.8 24.1 %collective-permute-start.39 = (bf16[512,1024]{1,0:T(8,128)(2,1)}, bf16[512,1024]{1,0:T(8,128)(2,1)}, u32[]{:S(2)}, u32[]{:S(2)}) collective-permute-start(bf16[512,1024]{1,0:T(8,128)(2,1)} %broadcast_select_fusion.25), channel_id=1, source_target_pairs={{20,28},{52,60},{84,92},{21,29},{53,61},{85,93}} | collective-permute-start | bytes 3145736 | tf_op jit(solution)/shard_map/ppermute | solution.py:66
  157.6 24.7 %collective-permute-start.32 = (bf16[512,1024]{1,0:T(8,128)(2,1)}, bf16[512,1024]{1,0:T(8,128)(2,1)}, u32[]{:S(2)}, u32[]{:S(2)}) collective-permute-start(bf16[512,1024]{1,0:T(8,128)(2,1)} %get-tuple-element.117), channel_id=1, source_target_pairs={{4,124},{36,28},{68,60},{100,92},{5,125},{37,29},{69,61},{101,93}} | collective-permute-start | bytes 3145736 | tf_op jit(solution)/shard_map/ppermute | solution.py:66
  159.2 24.5 %collective-permute-start.31 = (bf16[512,1024]{1,0:T(8,128)(2,1)}, bf16[512,1024]{1,0:T(8,128)(2,1)}, u32[]{:S(2)}, u32[]{:S(2)}) collective-permute-start(bf16[512,1024]{1,0:T(8,128)(2,1)} %get-tuple-element.117), channel_id=1, source_target_pairs={{4,12},{36,44},{68,76},{100,108},{5,13},{37,45},{69,77},{101,109}} | collective-permute-start | bytes 3145736 | tf_op jit(solution)/shard_map/ppermute | solution.py:66
  176.3 27.5 %collective-permute-start.49 = (bf16[64,512]{1,0:T(8,128)(2,1)S(1)}, bf16[64,512]{1,0:T(8,128)(2,1)}, u32[]{:S(2)}, u32[]{:S(2)}) collective-permute-start(bf16[64,512]{1,0:T(8,128)(2,1)S(1)} %get-tuple-element.45), channel_id=1, source_target_pairs={{124,120},{12,8},{28,24},{44,40},{60,56},{76,72},{92,88},{108,104}... | collective-permute-start | bytes 196616 | tf_op jit(solution)/shard_map/ppermute | solution.py:66
  177.6 26.3 %collective-permute-start.48 = (bf16[64,512]{1,0:T(8,128)(2,1)S(1)}, bf16[64,512]{1,0:T(8,128)(2,1)}, u32[]{:S(2)}, u32[]{:S(2)}) collective-permute-start(bf16[64,512]{1,0:T(8,128)(2,1)S(1)} %get-tuple-element.45), channel_id=1, source_target_pairs={{124,0},{12,16},{28,32},{44,48},{60,64},{76,80},{92,96},{108,112},... | collective-permute-start | bytes 196616 | tf_op jit(solution)/shard_map/ppermute | solution.py:66
  179.0 26.9 %collective-permute-start.54 = (bf16[64,512]{1,0:T(8,128)(2,1)S(1)}, bf16[64,512]{1,0:T(8,128)(2,1)}, u32[]{:S(2)}, u32[]{:S(2)}) collective-permute-start(bf16[64,512]{1,0:T(8,128)(2,1)S(1)} %copy-done.70), channel_id=1, source_target_pairs={{4,8},{20,24},{36,40},{52,56},{68,72},{84,88},{100,104},{5,9},{21,... | collective-permute-start | bytes 196616 | tf_op jit(solution)/shard_map/ppermute | solution.py:66
  209.0 28.2 %collective-permute-start.52 = (bf16[512,1024]{1,0:T(8,128)(2,1)}, bf16[512,1024]{1,0:T(8,128)(2,1)}, u32[]{:S(2)}, u32[]{:S(2)}) collective-permute-start(bf16[512,1024]{1,0:T(8,128)(2,1)} %get-tuple-element.24), channel_id=1, source_target_pairs={{4,8},{20,24},{36,40},{52,56},{68,72},{84,88},{100,104},{5,9},{21,... | collective-permute-start | bytes 3145736 | tf_op jit(solution)/shard_map/ppermute | solution.py:66
  210.6 27.5 %collective-permute-start.51 = (bf16[512,1024]{1,0:T(8,128)(2,1)}, bf16[512,1024]{1,0:T(8,128)(2,1)}, u32[]{:S(2)}, u32[]{:S(2)}) collective-permute-start(bf16[512,1024]{1,0:T(8,128)(2,1)} %get-tuple-element.24), channel_id=1, source_target_pairs={{4,0},{20,16},{36,32},{52,48},{68,64},{84,80},{100,96},{116,112},{... | collective-permute-start | bytes 3145736 | tf_op jit(solution)/shard_map/ppermute | solution.py:66
  226.8 256.3 %collective-permute-start.45 = (bf16[512,1024]{0,1:T(8,128)(2,1)}, bf16[512,1024]{0,1:T(8,128)(2,1)S(1)}, u32[]{:S(2)}, u32[]{:S(2)}) collective-permute-start(bf16[512,1024]{0,1:T(8,128)(2,1)} %subtract_convert_fusion.2), channel_id=1, source_target_pairs={{124,120},{12,8},{28,24},{44,40},{60,56},{76,72},{92,88},{108,104}... | collective-permute-start | bytes 3145736 | tf_op jit(solution)/shard_map/ppermute | solution.py:66
  229.7 251.2 %collective-permute-start.46 = (bf16[512,1024]{0,1:T(8,128)(2,1)S(1)}, bf16[512,1024]{0,1:T(8,128)(2,1)S(1)}, u32[]{:S(2)}, u32[]{:S(2)}) collective-permute-start(bf16[512,1024]{0,1:T(8,128)(2,1)S(1)} %broadcast_select_fusion.11), channel_id=1, source_target_pairs={{124,0},{12,16},{28,32},{44,48},{60,64},{76,80},{92,96},{108,112},... | collective-permute-start | bytes 3145736 | tf_op jit(solution)/shard_map/ppermute | solution.py:66
  230.5 251.1 %collective-permute-start.47 = (bf16[512,1024]{0,1:T(8,128)(2,1)S(1)}, bf16[512,1024]{0,1:T(8,128)(2,1)S(1)}, u32[]{:S(2)}, u32[]{:S(2)}) collective-permute-start(bf16[512,1024]{0,1:T(8,128)(2,1)S(1)} %copy-done.19), channel_id=1, source_target_pairs={{124,120},{12,8},{28,24},{44,40},{60,56},{76,72},{92,88},{108,104}... | collective-permute-start | bytes 3145736 | tf_op jit(solution)/shard_map/ppermute | solution.py:66
  237.2 246.0 %collective-permute-start.44 = (bf16[512,1024]{0,1:T(8,128)(2,1)S(1)}, bf16[512,1024]{0,1:T(8,128)(2,1)S(1)}, u32[]{:S(2)}, u32[]{:S(2)}) collective-permute-start(bf16[512,1024]{0,1:T(8,128)(2,1)S(1)} %copy-done.51), channel_id=1, source_target_pairs={{124,0},{12,16},{28,32},{44,48},{60,64},{76,80},{92,96},{108,112},... | collective-permute-start | bytes 3145736 | tf_op jit(solution)/shard_map/ppermute | solution.py:66
  238.0 238.2 %collective-permute-start.67 = (bf16[64,512]{1,0:T(8,128)(2,1)S(1)}, bf16[64,512]{1,0:T(8,128)(2,1)S(1)}, u32[]{:S(2)}, u32[]{:S(2)}) collective-permute-start(bf16[64,512]{1,0:T(8,128)(2,1)S(1)} %copy-done.72), channel_id=1, source_target_pairs={{124,126},{4,6},{12,14},{20,22},{28,30},{36,38},{44,46},{52,54},{6... | collective-permute-start | bytes 196616 | tf_op jit(solution)/shard_map/ppermute | solution.py:66
  492.4 26.9 %collective-permute-start.65 = (bf16[512,1024]{1,0:T(8,128)(2,1)}, bf16[512,1024]{1,0:T(8,128)(2,1)}, u32[]{:S(2)}, u32[]{:S(2)}) collective-permute-start(bf16[512,1024]{1,0:T(8,128)(2,1)} %broadcast_select_fusion.23), channel_id=1, source_target_pairs={{124,126},{4,6},{12,14},{20,22},{28,30},{36,38},{44,46},{52,54},{6... | collective-permute-start | bytes 3145736 | tf_op jit(solution)/shard_map/ppermute | solution.py:66
  493.7 30.4 %collective-permute-start.64 = (bf16[512,1024]{1,0:T(8,128)(2,1)}, bf16[512,1024]{1,0:T(8,128)(2,1)}, u32[]{:S(2)}, u32[]{:S(2)}) collective-permute-start(bf16[512,1024]{1,0:T(8,128)(2,1)} %broadcast_select_fusion.23), channel_id=1, source_target_pairs={{124,122},{4,2},{12,10},{20,18},{28,26},{36,34},{44,42},{52,50},{6... | collective-permute-start | bytes 3145736 | tf_op jit(solution)/shard_map/ppermute | solution.py:66
  501.2 25.8 %collective-permute-start.59 = (bf16[512,1024]{0,1:T(8,128)(2,1)}, bf16[512,1024]{0,1:T(8,128)(2,1)}, u32[]{:S(2)}, u32[]{:S(2)}) collective-permute-start(bf16[512,1024]{0,1:T(8,128)(2,1)} %broadcast_select_fusion.8), channel_id=1, source_target_pairs={{120,122},{0,2},{8,10},{16,18},{24,26},{32,34},{40,42},{48,50},{56... | collective-permute-start | bytes 3145736 | tf_op jit(solution)/shard_map/ppermute | solution.py:66
  502.9 31.1 %collective-permute-start.60 = (bf16[512,1024]{0,1:T(8,128)(2,1)}, bf16[512,1024]{0,1:T(8,128)(2,1)}, u32[]{:S(2)}, u32[]{:S(2)}) collective-permute-start(bf16[512,1024]{0,1:T(8,128)(2,1)} %get-tuple-element.39), channel_id=1, source_target_pairs={{120,118},{0,126},{8,6},{16,14},{24,22},{32,30},{40,38},{48,46},{5... | collective-permute-start | bytes 3145736 | tf_op jit(solution)/shard_map/ppermute | solution.py:66
  510.0 46.5 %collective-permute-start.58 = (bf16[512,1024]{1,0:T(8,128)(2,1)}, bf16[512,1024]{1,0:T(8,128)(2,1)}, u32[]{:S(2)}, u32[]{:S(2)}) collective-permute-start(bf16[512,1024]{1,0:T(8,128)(2,1)} %get-tuple-element.121), channel_id=1, source_target_pairs={{120,118},{0,126},{8,6},{16,14},{24,22},{32,30},{40,38},{48,46},{5... | collective-permute-start | bytes 3145736 | tf_op jit(solution)/shard_map/ppermute | solution.py:66
  519.3 37.2 %collective-permute-start.57 = (bf16[512,1024]{1,0:T(8,128)(2,1)}, bf16[512,1024]{1,0:T(8,128)(2,1)}, u32[]{:S(2)}, u32[]{:S(2)}) collective-permute-start(bf16[512,1024]{1,0:T(8,128)(2,1)} %get-tuple-element.121), channel_id=1, source_target_pairs={{120,122},{0,2},{8,10},{16,18},{24,26},{32,34},{40,42},{48,50},{56... | collective-permute-start | bytes 3145736 | tf_op jit(solution)/shard_map/ppermute | solution.py:66
  537.4 23.7 %collective-permute-start.63 = (bf16[1,512,512]{1,2,0:T(8,128)(2,1)S(1)}, bf16[1,512,512]{1,2,0:T(8,128)(2,1)S(1)}, u32[]{:S(2)}, u32[]{:S(2)}) collective-permute-start(bf16[1,512,512]{1,2,0:T(8,128)(2,1)S(1)} %broadcast_select_fusion.51), channel_id=1, source_target_pairs={{0,1},{1,0},{2,3},{3,2},{4,5},{5,4},{6,7},{7,6},{8,9},{9,8},{10,11... | collective-permute-start | bytes 1572872 | tf_op jit(solution)/shard_map/ppermute | solution.py:70
  (142 other events, 1301.4 us)

commit v5 on v4

--- a/solution.py
+++ b/solution.py
@@ -41,9 +41,13 @@
                 crit_from_right.append((where_is(right_id), where_is(block)))
                 if left_id >= 0:
                     pre_from_left.append((where_is(left_id), where_is(block)))
+        relays = choose_relays(crit_from_left + crit_from_right, steps)
         levels_plan[level_index] = dict(
-            crit_from_left=crit_from_left,
-            crit_from_right=crit_from_right,
+            crit_from_left=[pair for pair in crit_from_left if pair not in relays],
+            crit_from_right=[pair for pair in crit_from_right if pair not in relays],
+            leg_from_left=[(pair[0], relays[pair]) for pair in crit_from_left if pair in relays],
+            leg_from_right=[(pair[0], relays[pair]) for pair in crit_from_right if pair in relays],
+            leg_on=[(via, pair[1]) for pair, via in relays.items()],
             pre_from_left=pre_from_left,
             pre_from_right=pre_from_right,
             c_left=c_left,
@@ -52,12 +56,81 @@
     return levels_plan
 
 
+def ring_route(source, target, tie):
+    here = [source % 4, (source // 4) % 4, source // 16]
+    there = [target % 4, (target // 4) % 4, target // 16]
+    links = []
+    for dim in range(3):
+        while here[dim] != there[dim]:
+            gap = (there[dim] - here[dim]) % 4
+            step = 1 if gap < 2 else (-1 if gap > 2 else tie)
+            after = list(here)
+            after[dim] = (here[dim] + step) % 4
+            links.append((tuple(here), tuple(after)))
+            here = after
+    return links
+
+
+def link_load(flows, relays):
+    worst = (0, 0)
+    for tie in (1, -1):
+        load = {}
+        for source, target in flows:
+            via = relays.get((source, target))
+            path = ring_route(source, target, tie) if via is None else (
+                ring_route(source, via, tie) + ring_route(via, target, tie))
+            for link in path:
+                load[link] = load.get(link, 0) + 1
+        top = max(load.values())
+        worst = max(worst, (top, sum(1 for v in load.values() if v == top)))
+    return worst
+
+
+def choose_relays(flows, steps):
+    relays = {}
+    if steps != 64:
+        return relays
+    by_source = {}
+    for source, target in flows:
+        by_source.setdefault(source, []).append(target)
+    for source, targets in sorted(by_source.items()):
+        if len(targets) < 2:
+            continue
+        if not set(ring_route(source, targets[0], 1)) & set(ring_route(source, targets[1], 1)):
+            continue
+        best = (link_load(flows, relays), None)
+        for target in targets:
+            for dim in range(3):
+                for step in (1, -1):
+                    at = [source % 4, (source // 4) % 4, source // 16]
+                    at[dim] = (at[dim] + step) % 4
+                    via = at[0] + 4 * at[1] + 16 * at[2]
+                    if via == target or via in relays.values():
+                        continue
+                    relays[(source, target)] = via
+                    score = link_load(flows, relays)
+                    del relays[(source, target)]
+                    if score < best[0]:
+                        best = (score, (source, target, via))
+        if best[1] is not None:
+            relays[best[1][:2]] = best[1][2]
+    return relays
+
+
 def pick(flag, if_true, if_false):
     if if_true is None:
         return if_false
     if if_false is None:
         return if_true
     return jnp.where(flag, if_true, if_false)
+
+
+def add_present(first, second):
+    if first is None:
+        return second
+    if second is None:
+        return first
+    return jax.tree.map(lambda a, b: a + b, first, second)
 
 
 def send(values, pairs):
@@ -138,12 +211,25 @@
         from_right = send((up_diag, up_tip), step_plan["crit_from_right"])
         near_diag = pick(role, *(None if r is None else r[0] for r in (from_left, from_right)))
         near_tip = pick(role, *(None if r is None else r[1] for r in (from_left, from_right)))
+        relayed = None
+        if step_plan["leg_on"]:
+            leg_left = send((up_diag, up_tip), step_plan["leg_from_left"])
+            leg_right = send((up_diag, up_tip), step_plan["leg_from_right"])
+            held = add_present(leg_left, leg_right)
+            relayed = send(held, step_plan["leg_on"])
+            near_diag = add_present(near_diag, relayed[0])
+            near_tip = add_present(near_tip, relayed[1])
         if up_self_left is None:
             cross = None
         else:
             cross_left = send(up_self_right, step_plan["crit_from_left"])
             cross_right = send(up_self_left, step_plan["crit_from_right"])
             cross = pick(role, cross_left, cross_right)
+            if relayed is not None:
+                held_cross = add_present(
+                    send(up_self_right, step_plan["leg_from_left"]), send(up_self_left, step_plan["leg_from_right"])
+                )
+                cross = add_present(cross, send(held_cross, step_plan["leg_on"]))
 
         older = history.get(level_index + 2)
         far_diag, far_tip = zero_rows, zero_tip

time: 599 us -> 592 us (0.988)
  the two profiles are of different devices: /device:TPU:47 before, /device:TPU:31 now
where the time goes in v5:
time: 592 us; the launch traced here: 581 us
  waiting for transfers between devices  228 us (39%)
  other arithmetic  120 us (20%)
  starting transfers between devices  105 us (18%)
  matrix products  75.3 us (13%)
  local copies, waits for them, and re-layouts  49.9 us (8%)
    ppermute x56, waiting for transfers between devices, send(): return lax.ppermute(values, 'tm', pairs)  227 us
    ppermute x56, starting transfers between devices, send(): return lax.ppermute(values, 'tm', pairs)  94.8 us
    dot_general x31, matrix products, product(): jnp.dot(left_matrix, right_matrix, preferred_element_type=jnp.float32)  75.3 us
    select_n x10, other arithmetic, pick(): return jnp.where(flag, if_true, if_false)  21 us
    select_n x5, other arithmetic, body(): jnp.where(active, jnp.concatenate([self_left, self_right], axis=1), state...  16.8 us
    unnamed x185, local copies, waits for them, and re-layouts  12.2 us
  transfers between devices with their start and end apart: 76, of which 4 were waited for; matrix products, arithmetic and copies ran while one was open for 33% of the time, Pallas kernels for 0%

profile of v5, /device:TPU:31, one launch (start us, length us, event | category | flops | bytes accessed | tf_op | source)
XLA Modules:
  0.0 580.7 jit_solution(10750659131550195436)
XLA Ops:
  13.9 4.6 broadcast_select_fusion.2
  23.5 3.1 fusion.133
  32.5 2.9 copy.46
  49.2 3.7 subtract_convert_fusion.5
  57.0 3.8 maximum_select_fusion.2
  69.8 3.9 fusion.138
  93.5 3.6 subtract_convert_fusion.4
  103.9 3.1 broadcast_select_fusion.21
  143.4 3.1 broadcast_select_fusion.30
  155.6 6.1 %broadcast_select_fusion.20 = (bf16[512,1024]{1,0:T(8,128)(2,1)}, bf16[512,1024]{1,0:T(8,128)(2,1)}) fusion(bf16[512,1024]{1,0:T(8,128)(2,1)} %broadcast_select_fusion.21, pred[]{:T(512)} %bitcast.77, bf16[64,1024]{1,0:T(8,128)(2,1)S(1)} %copy-done.63, bf16[1024,1024]{1,0:T(8,128)(2,1)S(1)} %get-tuple-element.67, bf16[1024,1024]{1,0:T(8,128)(2,1)S(1)} %copy-done.7, ...), kind=kOutput, calls=%fused_computation.250 | convolution fusion | flops 2236153856 | bytes 10682369 | tf_op jit(solution)/shard_map/dot_general | solution.py:10
  165.0 3.1 pad_maximum_fusion.5
  168.0 3.9 copy.50
  172.0 3.8 broadcast_select_fusion
  180.4 3.6 fusion.147
  216.9 3.7 subtract_convert_fusion.2
  228.4 3.7 maximum_select_fusion.4
  240.9 199.4 %collective-permute-done.73 = bf16[64,512]{1,0:T(8,128)(2,1)S(1)} collective-permute-done((bf16[64,512]{1,0:T(8,128)(2,1)S(1)}, bf16[64,512]{1,0:T(8,128)(2,1)S(1)}, u32[]{:S(2)}, u32[]{:S(2)}) %collective-permute-start.73) | collective-permute-done | bytes 65568 | tf_op jit(solution)/shard_map/ppermute | solution.py:139
  467.2 34.1 %collective-permute-start.66 = (bf16[512,1024]{0,1:T(8,128)(2,1)}, bf16[512,1024]{0,1:T(8,128)(2,1)}, u32[]{:S(2)}, u32[]{:S(2)}) collective-permute-start(bf16[512,1024]{0,1:T(8,128)(2,1)} %get-tuple-element.39), channel_id=1, source_target_pairs={{120,118},{0,126},{8,6},{16,14},{24,22},{32,30},{40,38},{48,46},{5... | collective-permute-start | bytes 3145736 | tf_op jit(solution)/shard_map/ppermute | solution.py:139
  501.3 5.8 %broadcast_select_fusion.18 = (bf16[512,1024]{1,0:T(8,128)(2,1)}, bf16[512,1024]{1,0:T(8,128)(2,1)}) fusion(bf16[512,1024]{1,0:T(8,128)(2,1)} %broadcast_select_fusion.19, pred[]{:T(512)} %bitcast.107, bf16[64,1024]{1,0:T(8,128)(2,1)S(1)} %copy-done.65, bf16[1024,1024]{1,0:T(8,128)(2,1)S(1)} %get-tuple-element.67, bf16[1024,1024]{1,0:T(8,128)(2,1)S(1)} %copy-done.11, ...), kind=kOutput, calls=%fused_computation.248 | convolution fusion | flops 2236153856 | bytes 10682369 | tf_op jit(solution)/shard_map/dot_general | solution.py:10
  513.3 2.9 broadcast_select_fusion.29
  516.2 10.4 %collective-permute-done.66 = bf16[512,1024]{0,1:T(8,128)(2,1)} collective-permute-done((bf16[512,1024]{0,1:T(8,128)(2,1)}, bf16[512,1024]{0,1:T(8,128)(2,1)}, u32[]{:S(2)}, u32[]{:S(2)}) %collective-permute-start.66) | collective-permute-done | bytes 1048608 | tf_op jit(solution)/shard_map/ppermute | solution.py:139
  531.6 17.5 %collective-permute-done.64 = bf16[512,1024]{1,0:T(8,128)(2,1)} collective-permute-done((bf16[512,1024]{1,0:T(8,128)(2,1)}, bf16[512,1024]{1,0:T(8,128)(2,1)}, u32[]{:S(2)}, u32[]{:S(2)}) %collective-permute-start.64) | collective-permute-done | bytes 1048608 | tf_op jit(solution)/shard_map/ppermute | solution.py:139
  570.0 4.0 copy.61
  574.1 6.5 %fusion.168 = bf16[1,512,1024]{2,1,0:T(8,128)(2,1)} fusion(bf16[512,1024]{1,0:T(8,128)(2,1)} %get-tuple-element.30, bf16[512,64]{0,1:T(8,128)(2,1)S(1)} %copy-done.82, bf16[512,1024]{0,1:T(8,128)(2,1)} %copy-done.37, bf16[512,1024]{0,1:T(8,128)(2,1)} %copy-done.36, pred[]{:T(512)} %bitcast, bf16[1,512,1024]{2,1,0:T(8,128)(2,1)S(1)} %copy-done.17, ...), kind=kOutput, calls=%fused_computation.170 | convolution fusion | flops 2236153856 | bytes 9633793 | tf_op jit(solution)/shard_map/dot_general | solution.py:10
  (462 shorter events, 237.8 us)
Async XLA Ops:
  2.7 26.8 %collective-permute-start.15 = (bf16[64,512]{1,0:T(8,128)(2,1)}, bf16[64,512]{1,0:T(8,128)(2,1)S(1)}, u32[]{:S(2)}, u32[]{:S(2)}) collective-permute-start(bf16[64,512]{1,0:T(8,128)(2,1)} %param.17), channel_id=1, source_target_pairs={{116,84},{117,85}} | collective-permute-start | bytes 196616 | tf_op jit(solution)/shard_map/ppermute | solution.py:139
  10.2 58.7 %collective-permute-start.14 = (bf16[512,1024]{1,0:T(8,128)(2,1)}, bf16[512,1024]{1,0:T(8,128)(2,1)}, u32[]{:S(2)}, u32[]{:S(2)}) collective-permute-start(bf16[512,1024]{1,0:T(8,128)(2,1)} %bitcast.317), channel_id=1, source_target_pairs={{116,84},{117,85}} | collective-permute-start | bytes 3145736 | tf_op jit(solution)/shard_map/ppermute | solution.py:139
  82.2 27.6 %collective-permute-start.29 = (bf16[512,1024]{1,0:T(8,128)(2,1)}, bf16[512,1024]{1,0:T(8,128)(2,1)}, u32[]{:S(2)}, u32[]{:S(2)}) collective-permute-start(bf16[512,1024]{1,0:T(8,128)(2,1)} %broadcast_select_fusion.22), channel_id=1, source_target_pairs={{52,68},{53,69}} | collective-permute-start | bytes 3145736 | tf_op jit(solution)/shard_map/ppermute | solution.py:139
  83.8 27.7 %collective-permute-start.28 = (bf16[512,1024]{1,0:T(8,128)(2,1)}, bf16[512,1024]{1,0:T(8,128)(2,1)}, u32[]{:S(2)}, u32[]{:S(2)}) collective-permute-start(bf16[512,1024]{1,0:T(8,128)(2,1)} %broadcast_select_fusion.22), channel_id=1, source_target_pairs={{52,36},{116,100},{53,37},{117,101}} | collective-permute-start | bytes 3145736 | tf_op jit(solution)/shard_map/ppermute | solution.py:139
  103.0 20.3 %collective-permute-start.21 = (bf16[512,1024]{0,1:T(8,128)(2,1)S(1)}, bf16[512,1024]{0,1:T(8,128)(2,1)S(1)}, u32[]{:S(2)}, u32[]{:S(2)}) collective-permute-start(bf16[512,1024]{0,1:T(8,128)(2,1)S(1)} %broadcast_select_fusion.11), channel_id=1, source_target_pairs={{20,4},{84,68},{21,5},{85,69}} | collective-permute-start | bytes 3145736 | tf_op jit(solution)/shard_map/ppermute | solution.py:139
  120.4 23.0 %collective-permute-start.42 = (bf16[512,1024]{1,0:T(8,128)(2,1)}, bf16[512,1024]{1,0:T(8,128)(2,1)}, u32[]{:S(2)}, u32[]{:S(2)}) collective-permute-start(bf16[512,1024]{1,0:T(8,128)(2,1)} %broadcast_select_fusion.21), channel_id=1, source_target_pairs={{20,28},{52,60},{84,92},{21,29},{53,61},{85,93}} | collective-permute-start | bytes 3145736 | tf_op jit(solution)/shard_map/ppermute | solution.py:139
  123.3 20.1 %collective-permute-start.41 = (bf16[512,1024]{1,0:T(8,128)(2,1)}, bf16[512,1024]{1,0:T(8,128)(2,1)}, u32[]{:S(2)}, u32[]{:S(2)}) collective-permute-start(bf16[512,1024]{1,0:T(8,128)(2,1)} %broadcast_select_fusion.21), channel_id=1, source_target_pairs={{20,12},{52,44},{84,76},{116,108},{21,13},{53,45},{85,77},{117,109}} | collective-permute-start | bytes 3145736 | tf_op jit(solution)/shard_map/ppermute | solution.py:139
  152.2 23.6 %collective-permute-start.36 = (bf16[512,1024]{1,0:T(8,128)(2,1)}, bf16[512,1024]{1,0:T(8,128)(2,1)}, u32[]{:S(2)}, u32[]{:S(2)}) collective-permute-start(bf16[512,1024]{1,0:T(8,128)(2,1)} %broadcast_select_fusion.23), channel_id=1, source_target_pairs={{4,12},{36,44},{68,76},{100,108},{5,13},{37,45},{69,77},{101,109}} | collective-permute-start | bytes 3145736 | tf_op jit(solution)/shard_map/ppermute | solution.py:139
  153.8 21.9 %collective-permute-start.37 = (bf16[512,1024]{1,0:T(8,128)(2,1)}, bf16[512,1024]{1,0:T(8,128)(2,1)}, u32[]{:S(2)}, u32[]{:S(2)}) collective-permute-start(bf16[512,1024]{1,0:T(8,128)(2,1)} %get-tuple-element.51), channel_id=1, source_target_pairs={{4,124},{36,28},{68,60},{100,92},{5,125},{37,29},{69,61},{101,93}} | collective-permute-start | bytes 3145736 | tf_op jit(solution)/shard_map/ppermute | solution.py:139
  205.0 27.2 %collective-permute-start.58 = (bf16[512,1024]{1,0:T(8,128)(2,1)}, bf16[512,1024]{1,0:T(8,128)(2,1)}, u32[]{:S(2)}, u32[]{:S(2)}) collective-permute-start(bf16[512,1024]{1,0:T(8,128)(2,1)} %get-tuple-element.24), channel_id=1, source_target_pairs={{4,8},{20,24},{36,40},{52,56},{68,72},{84,88},{100,104},{5,9},{21,... | collective-permute-start | bytes 3145736 | tf_op jit(solution)/shard_map/ppermute | solution.py:139
  206.6 30.8 %collective-permute-start.57 = (bf16[512,1024]{1,0:T(8,128)(2,1)}, bf16[512,1024]{1,0:T(8,128)(2,1)}, u32[]{:S(2)}, u32[]{:S(2)}) collective-permute-start(bf16[512,1024]{1,0:T(8,128)(2,1)} %get-tuple-element.24), channel_id=1, source_target_pairs={{4,0},{20,16},{36,32},{52,48},{68,64},{84,80},{100,96},{116,112},{... | collective-permute-start | bytes 3145736 | tf_op jit(solution)/shard_map/ppermute | solution.py:139
  215.0 18.1 %collective-permute-start.51 = (bf16[512,1024]{0,1:T(8,128)(2,1)}, bf16[512,1024]{0,1:T(8,128)(2,1)}, u32[]{:S(2)}, u32[]{:S(2)}) collective-permute-start(bf16[512,1024]{0,1:T(8,128)(2,1)} %get-tuple-element.46), channel_id=1, source_target_pairs={{124,100},{12,20},{28,4},{44,52},{60,36},{76,84},{92,68},{108,116}... | collective-permute-start | bytes 3145736 | tf_op jit(solution)/shard_map/ppermute | solution.py:139
  227.6 217.5 %collective-permute-start.50 = (bf16[512,1024]{0,1:T(8,128)(2,1)S(1)}, bf16[512,1024]{0,1:T(8,128)(2,1)S(1)}, u32[]{:S(2)}, u32[]{:S(2)}) collective-permute-start(bf16[512,1024]{0,1:T(8,128)(2,1)S(1)} %broadcast_select_fusion.9), channel_id=1, source_target_pairs={{124,120},{12,8},{28,24},{44,40},{60,56},{76,72},{92,88},{108,104}... | collective-permute-start | bytes 3145736 | tf_op jit(solution)/shard_map/ppermute | solution.py:139
  232.2 215.5 %collective-permute-start.47 = (bf16[512,1024]{0,1:T(8,128)(2,1)}, bf16[512,1024]{0,1:T(8,128)(2,1)S(1)}, u32[]{:S(2)}, u32[]{:S(2)}) collective-permute-start(bf16[512,1024]{0,1:T(8,128)(2,1)} %subtract_convert_fusion.2), channel_id=1, source_target_pairs={{124,120},{12,8},{28,24},{44,40},{60,56},{76,72},{92,88},{108,104}... | collective-permute-start | bytes 3145736 | tf_op jit(solution)/shard_map/ppermute | solution.py:139
  233.1 212.7 %collective-permute-start.52 = (bf16[512,1024]{0,1:T(8,128)(2,1)}, bf16[512,1024]{0,1:T(8,128)(2,1)S(1)}, u32[]{:S(2)}, u32[]{:S(2)}) collective-permute-start(bf16[512,1024]{0,1:T(8,128)(2,1)} %collective-permute-done.51), channel_id=1, source_target_pairs={{20,16},{4,32},{52,48},{36,64},{84,80},{68,96},{116,112},{100,0},{... | collective-permute-start | bytes 3145736 | tf_op jit(solution)/shard_map/ppermute | solution.py:139
  233.8 213.9 %collective-permute-start.49 = (bf16[512,1024]{0,1:T(8,128)(2,1)}, bf16[512,1024]{0,1:T(8,128)(2,1)S(1)}, u32[]{:S(2)}, u32[]{:S(2)}) collective-permute-start(bf16[512,1024]{0,1:T(8,128)(2,1)} %collective-permute-done.48), channel_id=1, source_target_pairs={{20,16},{4,32},{52,48},{36,64},{84,80},{68,96},{116,112},{100,0},{... | collective-permute-start | bytes 3145736 | tf_op jit(solution)/shard_map/ppermute | solution.py:139
  237.5 202.8 %collective-permute-start.73 = (bf16[64,512]{1,0:T(8,128)(2,1)S(1)}, bf16[64,512]{1,0:T(8,128)(2,1)S(1)}, u32[]{:S(2)}, u32[]{:S(2)}) collective-permute-start(bf16[64,512]{1,0:T(8,128)(2,1)S(1)} %copy-done.69), channel_id=1, source_target_pairs={{124,126},{4,6},{12,14},{20,22},{28,30},{36,38},{44,46},{52,54},{6... | collective-permute-start | bytes 196616 | tf_op jit(solution)/shard_map/ppermute | solution.py:139
  456.5 52.0 %collective-permute-start.71 = (bf16[512,1024]{1,0:T(8,128)(2,1)}, bf16[512,1024]{1,0:T(8,128)(2,1)}, u32[]{:S(2)}, u32[]{:S(2)}) collective-permute-start(bf16[512,1024]{1,0:T(8,128)(2,1)} %broadcast_select_fusion.19), channel_id=1, source_target_pairs={{124,126},{4,6},{12,14},{20,22},{28,30},{36,38},{44,46},{52,54},{6... | collective-permute-start | bytes 3145736 | tf_op jit(solution)/shard_map/ppermute | solution.py:139
  457.7 55.5 %collective-permute-start.70 = (bf16[512,1024]{1,0:T(8,128)(2,1)}, bf16[512,1024]{1,0:T(8,128)(2,1)}, u32[]{:S(2)}, u32[]{:S(2)}) collective-permute-start(bf16[512,1024]{1,0:T(8,128)(2,1)} %broadcast_select_fusion.19), channel_id=1, source_target_pairs={{124,122},{4,2},{12,10},{20,18},{28,26},{36,34},{44,42},{52,50},{6... | collective-permute-start | bytes 3145736 | tf_op jit(solution)/shard_map/ppermute | solution.py:139
  465.6 50.7 %collective-permute-start.65 = (bf16[512,1024]{0,1:T(8,128)(2,1)}, bf16[512,1024]{0,1:T(8,128)(2,1)}, u32[]{:S(2)}, u32[]{:S(2)}) collective-permute-start(bf16[512,1024]{0,1:T(8,128)(2,1)} %broadcast_select_fusion.6), channel_id=1, source_target_pairs={{120,122},{0,2},{8,10},{16,18},{24,26},{32,34},{40,42},{48,50},{56... | collective-permute-start | bytes 3145736 | tf_op jit(solution)/shard_map/ppermute | solution.py:139
  467.2 59.4 %collective-permute-start.66 = (bf16[512,1024]{0,1:T(8,128)(2,1)}, bf16[512,1024]{0,1:T(8,128)(2,1)}, u32[]{:S(2)}, u32[]{:S(2)}) collective-permute-start(bf16[512,1024]{0,1:T(8,128)(2,1)} %get-tuple-element.39), channel_id=1, source_target_pairs={{120,118},{0,126},{8,6},{16,14},{24,22},{32,30},{40,38},{48,46},{5... | collective-permute-start | bytes 3145736 | tf_op jit(solution)/shard_map/ppermute | solution.py:139
  507.1 41.9 %collective-permute-start.64 = (bf16[512,1024]{1,0:T(8,128)(2,1)}, bf16[512,1024]{1,0:T(8,128)(2,1)}, u32[]{:S(2)}, u32[]{:S(2)}) collective-permute-start(bf16[512,1024]{1,0:T(8,128)(2,1)} %get-tuple-element.121), channel_id=1, source_target_pairs={{120,118},{0,126},{8,6},{16,14},{24,22},{32,30},{40,38},{48,46},{5... | collective-permute-start | bytes 3145736 | tf_op jit(solution)/shard_map/ppermute | solution.py:139
  508.4 40.6 %collective-permute-start.63 = (bf16[512,1024]{1,0:T(8,128)(2,1)}, bf16[512,1024]{1,0:T(8,128)(2,1)}, u32[]{:S(2)}, u32[]{:S(2)}) collective-permute-start(bf16[512,1024]{1,0:T(8,128)(2,1)} %get-tuple-element.121), channel_id=1, source_target_pairs={{120,122},{0,2},{8,10},{16,18},{24,26},{32,34},{40,42},{48,50},{56... | collective-permute-start | bytes 3145736 | tf_op jit(solution)/shard_map/ppermute | solution.py:139
  530.0 23.7 %collective-permute-start.69 = (bf16[1,512,512]{1,2,0:T(8,128)(2,1)S(1)}, bf16[1,512,512]{1,2,0:T(8,128)(2,1)S(1)}, u32[]{:S(2)}, u32[]{:S(2)}) collective-permute-start(bf16[1,512,512]{1,2,0:T(8,128)(2,1)S(1)} %broadcast_select_fusion.47), channel_id=1, source_target_pairs={{0,1},{1,0},{2,3},{3,2},{4,5},{5,4},{6,7},{7,6},{8,9},{9,8},{10,11... | collective-permute-start | bytes 1572872 | tf_op jit(solution)/shard_map/ppermute | solution.py:143
  (144 other events, 1179.4 us)

commit v6 on v5

--- a/solution.py
+++ b/solution.py
@@ -198,60 +198,49 @@
     zero_rows = jnp.zeros_like(inverse_rows)
     zero_tip = jnp.zeros_like(root_cross)
 
-    up_diag, up_tip, up_self_left, up_self_right = inverse_rows, root_cross, None, None
+    nodes = inverse_rows.shape[1]
+    top_pack = jnp.concatenate([inverse_rows, root_cross.T], axis=1)
+    pack_left, pack_right, has_cross = top_pack, top_pack, False
     state_diag, state_tip = inverse_rows, root_cross
-    state_cross = jnp.zeros((tile_rows, 2 * inverse_rows.shape[1]), inverse_rows.dtype)
+    state_cross = jnp.zeros((tile_rows, 2 * nodes), inverse_rows.dtype)
     history = {levels: (state_diag, state_tip)}
 
     for level_index in reversed(range(levels)):
         step_plan = levels_plan[level_index]
         active = table(step_plan["active"])
 
-        from_left = send((up_diag, up_tip), step_plan["crit_from_left"])
-        from_right = send((up_diag, up_tip), step_plan["crit_from_right"])
-        near_diag = pick(role, *(None if r is None else r[0] for r in (from_left, from_right)))
-        near_tip = pick(role, *(None if r is None else r[1] for r in (from_left, from_right)))
-        relayed = None
+        near = pick(
+            role, send(pack_right, step_plan["crit_from_left"]), send(pack_left, step_plan["crit_from_right"])
+        )
         if step_plan["leg_on"]:
-            leg_left = send((up_diag, up_tip), step_plan["leg_from_left"])
-            leg_right = send((up_diag, up_tip), step_plan["leg_from_right"])
-            held = add_present(leg_left, leg_right)
-            relayed = send(held, step_plan["leg_on"])
-            near_diag = add_present(near_diag, relayed[0])
-            near_tip = add_present(near_tip, relayed[1])
-        if up_self_left is None:
-            cross = None
+            held = add_present(
+                send(pack_right, step_plan["leg_from_left"]), send(pack_left, step_plan["leg_from_right"])
+            )
+            near = add_present(near, send(held, step_plan["leg_on"]))
+        near_tip = near[:, -root_cross.shape[0]:].T
+
+        older = history.get(level_index + 2)
+        far = None
+        if older is not None:
+            older_pack = jnp.concatenate([older[0], older[1].T], axis=1)
+            far = pick(
+                role, send(older_pack, step_plan["pre_from_right"]), send(older_pack, step_plan["pre_from_left"])
+            )
+        if far is None:
+            far = jnp.zeros((tile_rows, nodes + root_cross.shape[0]), inverse_rows.dtype)
+        far_tip = far[:, nodes:].T
+
+        tips_full = join_tiles(jnp.stack([near_tip, far_tip]), is_first)
+        near_operand = near
+        if has_cross:
+            cross_turned = tile_transpose(near[:, nodes:2 * nodes][None], is_first)[0]
+            near_mult = stacked
+            far_operand = jnp.concatenate([cross_turned, far], axis=1)
+            far_mult = stacked
         else:
-            cross_left = send(up_self_right, step_plan["crit_from_left"])
-            cross_right = send(up_self_left, step_plan["crit_from_right"])
-            cross = pick(role, cross_left, cross_right)
-            if relayed is not None:
-                held_cross = add_present(
-                    send(up_self_right, step_plan["leg_from_left"]), send(up_self_left, step_plan["leg_from_right"])
-                )
-                cross = add_present(cross, send(held_cross, step_plan["leg_on"]))
-
-        older = history.get(level_index + 2)
-        far_diag, far_tip = zero_rows, zero_tip
-        if older is not None:
-            g_left = send(older, step_plan["pre_from_left"])
-            g_right = send(older, step_plan["pre_from_right"])
-            if g_left is not None or g_right is not None:
-                far_diag = pick(role, *(None if r is None else r[0] for r in (g_right, g_left)))
-                far_tip = pick(role, *(None if r is None else r[1] for r in (g_right, g_left)))
-
-        tips_full = join_tiles(jnp.stack([near_tip, far_tip]), is_first)
-        if cross is None:
-            near_operand = jnp.concatenate([near_diag, near_tip.T], axis=1)
             near_mult = jnp.concatenate([first, full_tip], axis=0)
-            far_operand = jnp.concatenate([far_diag, far_tip.T], axis=1)
+            far_operand = far
             far_mult = jnp.concatenate([second, full_tip], axis=0)
-        else:
-            cross_turned = tile_transpose(cross[None], is_first)[0]
-            near_operand = jnp.concatenate([near_diag, cross, near_tip.T], axis=1)
-            near_mult = stacked
-            far_operand = jnp.concatenate([cross_turned, far_diag, far_tip.T], axis=1)
-            far_mult = stacked
         fresh_far = (-product(far_operand, far_mult)).astype(jnp.bfloat16)
         fresh_near = (-product(near_operand, near_mult)).astype(jnp.bfloat16)
         tip_y = product(tips_full[0], first_cols) + product(tips_full[1], second_cols) + tip_own
@@ -270,7 +259,9 @@
         if level_index > 0:
             state_diag, state_tip, state_cross = lax.optimization_barrier((state_diag, state_tip, state_cross))
         history[level_index] = (state_diag, state_tip)
-        up_diag, up_tip, up_self_left, up_self_right = fresh_diag, fresh_tip, self_left, self_right
+        pack_left = jnp.concatenate([fresh_diag, self_left, fresh_tip.T], axis=1)
+        pack_right = jnp.concatenate([fresh_diag, self_right, fresh_tip.T], axis=1)
+        has_cross = True
 
     return (state_diag[None], state_cross[None], state_tip[None])
 

time: 592 us -> 621 us (1.049)
  waiting for transfers between devices: 228 us -> 293 us
  starting transfers between devices: 105 us -> 46.2 us
  local copies, waits for them, and re-layouts: 49.9 us -> 96.9 us
  other arithmetic: 120 us -> 93.7 us
    ppermute x56 -> x22, waiting for transfers between devices: 227 us -> 292 us  [send(): return lax.ppermute(values, 'tm', pairs)]
    ppermute x56 -> x22, starting transfers between devices: 94.8 us -> 37.5 us  [send(): return lax.ppermute(values, 'tm', pairs)]
    ppermute x1 -> x14, local copies, waits for them, and re-layouts: 2.06 us -> 47 us  [send(): return lax.ppermute(values, 'tm', pairs)]
    unnamed x185 -> x161, local copies, waits for them, and re-layouts: 12.2 us -> 32.2 us
    transpose x9 -> x0, local copies, waits for them, and re-layouts: 11.5 us -> none  [the longest x5 5.48 us: body(): far_operand = jnp.concatenate([cross_turned, far_diag, far_tip.T], axis=1)]
    concatenate x1 -> x10, other arithmetic: 3.08 us -> 14.2 us  [the longest x3 6.62 us: body(): pack_left = jnp.concatenate([fresh_diag, self_left, fresh_tip.T], axis=1)]
    convert_element_type x5 -> x0, local copies, waits for them, and re-layouts: 10.7 us -> none  [the longest x4 9.77 us: body(): fresh_diag = (inverse_rows.astype(jnp.float32) - total).astype(jnp.bfloat16)]
    transpose x10 -> x0, other arithmetic: 10.2 us -> none  [the longest x5 5.09 us: body(): near_operand = jnp.concatenate([near_diag, cross, near_tip.T], axis=1)]
  transfers between devices with their start and end apart: 76 -> 42, of which waited for: 4 -> 4; matrix products, arithmetic and copies ran while one was open for 33% -> 25% of each run, Pallas kernels for 0% -> 0%
where the time goes in v6:
time: 621 us; the launch traced here: 610 us
  waiting for transfers between devices  293 us (47%)
  local copies, waits for them, and re-layouts  96.9 us (16%)
  other arithmetic  93.7 us (15%)
  matrix products  76.8 us (12%)
  starting transfers between devices  46.2 us (7%)
    ppermute x22, waiting for transfers between devices, send(): return lax.ppermute(values, 'tm', pairs)  292 us
    dot_general x31, matrix products, product(): jnp.dot(left_matrix, right_matrix, preferred_element_type=jnp.float32)  76.8 us
    ppermute x14, local copies, waits for them, and re-layouts, send(): return lax.ppermute(values, 'tm', pairs)  47 us
    ppermute x22, starting transfers between devices, send(): return lax.ppermute(values, 'tm', pairs)  37.5 us
    unnamed x161, local copies, waits for them, and re-layouts  32.2 us
    select_n x7, other arithmetic, pick(): return jnp.where(flag, if_true, if_false)  14.7 us
  transfers between devices with their start and end apart: 42, of which 4 were waited for; matrix products, arithmetic and copies ran while one was open for 25% of the time, Pallas kernels for 0%

profile of v6, /device:TPU:31, one launch (start us, length us, event | category | flops | bytes accessed | tf_op | source)
XLA Modules:
  0.0 609.5 jit_solution(7403304138989608914)
XLA Ops:
  8.3 4.4 broadcast_select_fusion.4
  29.6 4.2 broadcast_select_fusion.13
  46.1 4.1 copy.87
  50.2 4.1 copy.88
  74.0 4.4 broadcast_select_fusion.12
  102.6 4.1 copy.92
  106.8 4.1 copy.93
  116.0 3.7 fusion.75
  121.2 5.0 fusion.76
  137.7 4.3 broadcast_select_fusion.11
  158.1 4.1 copy.99
  162.2 4.1 copy.100
  177.7 5.0 fusion.80
  191.0 4.4 broadcast_select_fusion.10
  208.3 4.1 copy.106
  212.4 4.1 copy.107
  243.8 4.4 broadcast_select_fusion.9
  256.9 218.1 %collective-permute-done.39 = bf16[512,1088]{0,1:T(8,128)(2,1)} collective-permute-done((bf16[512,1088]{0,1:T(8,128)(2,1)}, bf16[512,1088]{0,1:T(8,128)(2,1)}, u32[]{:S(2)}, u32[]{:S(2)}) %collective-permute-start.39) | collective-permute-done | bytes 1114144 | tf_op jit(solution)/shard_map/ppermute | solution.py:139
  484.2 73.8 %collective-permute-done.36 = bf16[512,2112]{0,1:T(8,128)(2,1)} collective-permute-done((bf16[512,2112]{0,1:T(8,128)(2,1)}, bf16[512,2112]{0,1:T(8,128)(2,1)}, u32[]{:S(2)}, u32[]{:S(2)}) %collective-permute-start.36) | collective-permute-done | bytes 2162720 | tf_op jit(solution)/shard_map/ppermute | solution.py:139
  568.4 5.8 fusion.87
  577.7 4.9 fusion.88
  594.4 4.5 fusion.94
  601.3 3.8 fusion.56
  605.2 3.9 copy.119
  (378 shorter events, 219.6 us)
Async XLA Ops:
  0.7 6.6 %collective-permute-start.2 = (bf16[512,1024]{1,0:T(8,128)(2,1)}, bf16[512,1024]{1,0:T(8,128)(2,1)S(1)}, u32[]{:S(2)}, u32[]{:S(2)}) collective-permute-start(bf16[512,1024]{1,0:T(8,128)(2,1)} %bitcast.334), channel_id=1, source_target_pairs={{0,1},{1,0},{2,3},{3,2},{4,5},{5,4},{6,7},{7,6},{8,9},{9,8},{10,11... | collective-permute-start | bytes 3145736 | tf_op jit(solution)/shard_map/ppermute | solution.py:143
  4.3 10.0 %collective-permute-start = (bf16[512,1088]{0,1:T(8,128)(2,1)}, bf16[512,1088]{0,1:T(8,128)(2,1)}, u32[]{:S(2)}, u32[]{:S(2)}) collective-permute-start(bf16[512,1088]{0,1:T(8,128)(2,1)} %pad_maximum_fusion.53), channel_id=1, source_target_pairs={{116,52},{117,53}} | collective-permute-start | bytes 3342344 | tf_op jit(solution)/shard_map/ppermute | solution.py:139
  36.0 10.1 %collective-permute-start.6 = (bf16[512,2112]{0,1:T(8,128)(2,1)}, bf16[512,2112]{0,1:T(8,128)(2,1)}, u32[]{:S(2)}, u32[]{:S(2)}) collective-permute-start(bf16[512,2112]{0,1:T(8,128)(2,1)} %get-tuple-element.90), channel_id=1, source_target_pairs={{52,84},{53,85}} | collective-permute-start | bytes 6488072 | tf_op jit(solution)/shard_map/ppermute | solution.py:139
  38.0 12.2 %collective-permute-start.7 = (bf16[512,2112]{0,1:T(8,128)(2,1)}, bf16[512,2112]{0,1:T(8,128)(2,1)}, u32[]{:S(2)}, u32[]{:S(2)}) collective-permute-start(bf16[512,2112]{0,1:T(8,128)(2,1)} %get-tuple-element.89), channel_id=1, source_target_pairs={{52,20},{53,21}} | collective-permute-start | bytes 6488072 | tf_op jit(solution)/shard_map/ppermute | solution.py:139
  79.9 8.6 %collective-permute-start.13 = (bf16[512,2112]{0,1:T(8,128)(2,1)S(1)}, bf16[512,2112]{0,1:T(8,128)(2,1)}, u32[]{:S(2)}, u32[]{:S(2)}) collective-permute-start(bf16[512,2112]{0,1:T(8,128)(2,1)S(1)} %get-tuple-element.87), channel_id=1, source_target_pairs={{20,52},{84,116},{21,53},{85,117}} | collective-permute-start | bytes 6488072 | tf_op jit(solution)/shard_map/ppermute | solution.py:139
  83.2 8.0 %collective-permute-start.16 = (bf16[512,1088]{0,1:T(8,128)(2,1)}, bf16[512,1088]{0,1:T(8,128)(2,1)}, u32[]{:S(2)}, u32[]{:S(2)}) collective-permute-start(bf16[512,1088]{0,1:T(8,128)(2,1)} %pad_maximum_fusion.54), channel_id=1, source_target_pairs={{52,36},{116,100},{53,37},{117,101}} | collective-permute-start | bytes 3342344 | tf_op jit(solution)/shard_map/ppermute | solution.py:139
  84.8 8.7 %collective-permute-start.17 = (bf16[512,1088]{0,1:T(8,128)(2,1)}, bf16[512,1088]{0,1:T(8,128)(2,1)}, u32[]{:S(2)}, u32[]{:S(2)}) collective-permute-start(bf16[512,1088]{0,1:T(8,128)(2,1)} %pad_maximum_fusion.54), channel_id=1, source_target_pairs={{52,68},{53,69}} | collective-permute-start | bytes 3342344 | tf_op jit(solution)/shard_map/ppermute | solution.py:139
  86.5 16.2 %collective-permute-start.12 = (bf16[512,2112]{0,1:T(8,128)(2,1)}, bf16[512,2112]{0,1:T(8,128)(2,1)}, u32[]{:S(2)}, u32[]{:S(2)}) collective-permute-start(bf16[512,2112]{0,1:T(8,128)(2,1)} %get-tuple-element.88), channel_id=1, source_target_pairs={{20,4},{84,68},{21,5},{85,69}} | collective-permute-start | bytes 6488072 | tf_op jit(solution)/shard_map/ppermute | solution.py:139
  88.5 18.3 %collective-permute-start.14 = (bf16[512,2112]{0,1:T(8,128)(2,1)}, bf16[512,2112]{0,1:T(8,128)(2,1)}, u32[]{:S(2)}, u32[]{:S(2)}) collective-permute-start(bf16[512,2112]{0,1:T(8,128)(2,1)} %collective-permute-done.13), channel_id=1, source_target_pairs={{52,36},{116,100},{53,37},{117,101}} | collective-permute-start | bytes 6488072 | tf_op jit(solution)/shard_map/ppermute | solution.py:139
  126.6 7.7 %collective-permute-start.18 = (bf16[2,512,512]{2,1,0:T(8,128)(2,1)S(1)}, bf16[2,512,512]{2,1,0:T(8,128)(2,1)S(1)}, u32[]{:S(2)}, u32[]{:S(2)}) collective-permute-start(bf16[2,512,512]{2,1,0:T(8,128)(2,1)S(1)} %broadcast_select_fusion.32), channel_id=1, source_target_pairs={{0,1},{1,0},{2,3},{3,2},{4,5},{5,4},{6,7},{7,6},{8,9},{9,8},{10,11... | collective-permute-start | bytes 3145736 | tf_op jit(solution)/shard_map/ppermute | solution.py:143
  129.4 19.6 %collective-permute-start.23 = (bf16[512,1088]{0,1:T(8,128)(2,1)}, bf16[512,1088]{0,1:T(8,128)(2,1)}, u32[]{:S(2)}, u32[]{:S(2)}) collective-permute-start(bf16[512,1088]{0,1:T(8,128)(2,1)} %pad_maximum_fusion.55), channel_id=1, source_target_pairs={{20,12},{52,44},{84,76},{116,108},{21,13},{53,45},{85,77},{117,109}} | collective-permute-start | bytes 3342344 | tf_op jit(solution)/shard_map/ppermute | solution.py:139
  131.1 20.3 %collective-permute-start.24 = (bf16[512,1088]{0,1:T(8,128)(2,1)}, bf16[512,1088]{0,1:T(8,128)(2,1)}, u32[]{:S(2)}, u32[]{:S(2)}) collective-permute-start(bf16[512,1088]{0,1:T(8,128)(2,1)} %pad_maximum_fusion.55), channel_id=1, source_target_pairs={{20,28},{52,60},{84,92},{21,29},{53,61},{85,93}} | collective-permute-start | bytes 3342344 | tf_op jit(solution)/shard_map/ppermute | solution.py:139
  144.3 13.8 %collective-permute-start.20 = (bf16[512,2112]{0,1:T(8,128)(2,1)}, bf16[512,2112]{0,1:T(8,128)(2,1)}, u32[]{:S(2)}, u32[]{:S(2)}) collective-permute-start(bf16[512,2112]{0,1:T(8,128)(2,1)} %get-tuple-element.86), channel_id=1, source_target_pairs={{4,12},{36,44},{68,76},{100,108},{5,13},{37,45},{69,77},{101,109}} | collective-permute-start | bytes 6488072 | tf_op jit(solution)/shard_map/ppermute | solution.py:139
  146.3 15.9 %collective-permute-start.21 = (bf16[512,2112]{0,1:T(8,128)(2,1)}, bf16[512,2112]{0,1:T(8,128)(2,1)}, u32[]{:S(2)}, u32[]{:S(2)}) collective-permute-start(bf16[512,2112]{0,1:T(8,128)(2,1)} %get-tuple-element.85), channel_id=1, source_target_pairs={{4,124},{36,28},{68,60},{100,92},{5,125},{37,29},{69,61},{101,93}} | collective-permute-start | bytes 6488072 | tf_op jit(solution)/shard_map/ppermute | solution.py:139
  169.7 16.0 %collective-permute-start.26 = (bf16[2,64,512]{1,2,0:T(8,128)(2,1)}, bf16[2,64,512]{1,2,0:T(8,128)(2,1)}, u32[]{:S(2)}, u32[]{:S(2)}) collective-permute-start(bf16[2,64,512]{1,2,0:T(8,128)(2,1)} %pad_maximum_fusion.72), channel_id=1, source_target_pairs={{0,1},{1,0},{2,3},{3,2},{4,5},{5,4},{6,7},{7,6},{8,9},{9,8},{10,11... | collective-permute-start | bytes 393224 | tf_op jit(solution)/shard_map/ppermute | solution.py:143
  199.4 8.9 %collective-permute-start.27 = (bf16[512,2112]{0,1:T(8,128)(2,1)S(1)}, bf16[512,2112]{0,1:T(8,128)(2,1)}, u32[]{:S(2)}, u32[]{:S(2)}) collective-permute-start(bf16[512,2112]{0,1:T(8,128)(2,1)S(1)} %get-tuple-element.84), channel_id=1, source_target_pairs={{124,120},{12,8},{28,24},{44,40},{60,56},{76,72},{92,88},{108,104}... | collective-permute-start | bytes 6488072 | tf_op jit(solution)/shard_map/ppermute | solution.py:139
  201.4 11.0 %collective-permute-start.29 = (bf16[512,2112]{0,1:T(8,128)(2,1)}, bf16[512,2112]{0,1:T(8,128)(2,1)}, u32[]{:S(2)}, u32[]{:S(2)}) collective-permute-start(bf16[512,2112]{0,1:T(8,128)(2,1)} %collective-permute-done.28), channel_id=1, source_target_pairs={{20,16},{4,32},{52,48},{36,64},{84,80},{68,96},{116,112},{100,0},{... | collective-permute-start | bytes 6488072 | tf_op jit(solution)/shard_map/ppermute | solution.py:139
  229.8 9.2 %collective-permute-start.33 = (bf16[2,512,512]{2,1,0:T(8,128)(2,1)}, bf16[2,512,512]{2,1,0:T(8,128)(2,1)}, u32[]{:S(2)}, u32[]{:S(2)}) collective-permute-start(bf16[2,512,512]{2,1,0:T(8,128)(2,1)} %broadcast_select_fusion.28), channel_id=1, source_target_pairs={{0,1},{1,0},{2,3},{3,2},{4,5},{5,4},{6,7},{7,6},{8,9},{9,8},{10,11... | collective-permute-start | bytes 3145736 | tf_op jit(solution)/shard_map/ppermute | solution.py:143
  234.5 19.9 %collective-permute-start.38 = (bf16[512,1088]{0,1:T(8,128)(2,1)}, bf16[512,1088]{0,1:T(8,128)(2,1)}, u32[]{:S(2)}, u32[]{:S(2)}) collective-permute-start(bf16[512,1088]{0,1:T(8,128)(2,1)} %pad_maximum_fusion.57), channel_id=1, source_target_pairs={{124,122},{4,2},{12,10},{20,18},{28,26},{36,34},{44,42},{52,50},{6... | collective-permute-start | bytes 3342344 | tf_op jit(solution)/shard_map/ppermute | solution.py:139
  236.3 238.6 %collective-permute-start.39 = (bf16[512,1088]{0,1:T(8,128)(2,1)}, bf16[512,1088]{0,1:T(8,128)(2,1)}, u32[]{:S(2)}, u32[]{:S(2)}) collective-permute-start(bf16[512,1088]{0,1:T(8,128)(2,1)} %pad_maximum_fusion.57), channel_id=1, source_target_pairs={{124,126},{4,6},{12,14},{20,22},{28,30},{36,38},{44,46},{52,54},{6... | collective-permute-start | bytes 3342344 | tf_op jit(solution)/shard_map/ppermute | solution.py:139
  250.4 233.8 %collective-permute-start.35 = (bf16[512,2112]{0,1:T(8,128)(2,1)}, bf16[512,2112]{0,1:T(8,128)(2,1)}, u32[]{:S(2)}, u32[]{:S(2)}) collective-permute-start(bf16[512,2112]{0,1:T(8,128)(2,1)} %get-tuple-element.82), channel_id=1, source_target_pairs={{120,122},{0,2},{8,10},{16,18},{24,26},{32,34},{40,42},{48,50},{56... | collective-permute-start | bytes 6488072 | tf_op jit(solution)/shard_map/ppermute | solution.py:139
  252.5 305.5 %collective-permute-start.36 = (bf16[512,2112]{0,1:T(8,128)(2,1)}, bf16[512,2112]{0,1:T(8,128)(2,1)}, u32[]{:S(2)}, u32[]{:S(2)}) collective-permute-start(bf16[512,2112]{0,1:T(8,128)(2,1)} %get-tuple-element.81), channel_id=1, source_target_pairs={{120,118},{0,126},{8,6},{16,14},{24,22},{32,30},{40,38},{48,46},{5... | collective-permute-start | bytes 6488072 | tf_op jit(solution)/shard_map/ppermute | solution.py:139
  563.5 23.5 %collective-permute-start.41 = (bf16[2,64,512]{2,1,0:T(8,128)(2,1)}, bf16[2,64,512]{2,1,0:T(8,128)(2,1)}, u32[]{:S(2)}, u32[]{:S(2)}) collective-permute-start(bf16[2,64,512]{2,1,0:T(8,128)(2,1)} %pad_maximum_fusion.74), channel_id=1, source_target_pairs={{0,1},{1,0},{2,3},{3,2},{4,5},{5,4},{6,7},{7,6},{8,9},{9,8},{10,11... | collective-permute-start | bytes 393224 | tf_op jit(solution)/shard_map/ppermute | solution.py:143
  583.0 7.2 %collective-permute-start.40 = (bf16[2,512,512]{2,1,0:T(8,128)(2,1)S(1)}, bf16[2,512,512]{2,1,0:T(8,128)(2,1)S(1)}, u32[]{:S(2)}, u32[]{:S(2)}) collective-permute-start(bf16[2,512,512]{2,1,0:T(8,128)(2,1)S(1)} %broadcast_select_fusion.26), channel_id=1, source_target_pairs={{0,1},{1,0},{2,3},{3,2},{4,5},{5,4},{6,7},{7,6},{8,9},{9,8},{10,11... | collective-permute-start | bytes 3145736 | tf_op jit(solution)/shard_map/ppermute | solution.py:143
  (96 other events, 371.3 us)

commit v7 on v5

--- a/solution.py
+++ b/solution.py
@@ -207,29 +207,25 @@
         step_plan = levels_plan[level_index]
         active = table(step_plan["active"])
 
-        from_left = send((up_diag, up_tip), step_plan["crit_from_left"])
-        from_right = send((up_diag, up_tip), step_plan["crit_from_right"])
-        near_diag = pick(role, *(None if r is None else r[0] for r in (from_left, from_right)))
-        near_tip = pick(role, *(None if r is None else r[1] for r in (from_left, from_right)))
-        relayed = None
-        if step_plan["leg_on"]:
-            leg_left = send((up_diag, up_tip), step_plan["leg_from_left"])
-            leg_right = send((up_diag, up_tip), step_plan["leg_from_right"])
-            held = add_present(leg_left, leg_right)
-            relayed = send(held, step_plan["leg_on"])
-            near_diag = add_present(near_diag, relayed[0])
-            near_tip = add_present(near_tip, relayed[1])
+        def arrive(right_going, left_going):
+            got = pick(role, send(right_going, step_plan["crit_from_left"]), send(left_going, step_plan["crit_from_right"]))
+            if step_plan["leg_on"]:
+                held = add_present(
+                    send(right_going, step_plan["leg_from_left"]), send(left_going, step_plan["leg_from_right"])
+                )
+                got = add_present(got, send(held, step_plan["leg_on"]))
+            return got
+
+        near_diag = arrive(up_diag, up_diag)
         if up_self_left is None:
             cross = None
+            near_tip = arrive(up_tip, up_tip)
         else:
-            cross_left = send(up_self_right, step_plan["crit_from_left"])
-            cross_right = send(up_self_left, step_plan["crit_from_right"])
-            cross = pick(role, cross_left, cross_right)
-            if relayed is not None:
-                held_cross = add_present(
-                    send(up_self_right, step_plan["leg_from_left"]), send(up_self_left, step_plan["leg_from_right"])
-                )
-                cross = add_present(cross, send(held_cross, step_plan["leg_on"]))
+            early = arrive(
+                jnp.concatenate([up_self_right, up_tip.T], axis=1), jnp.concatenate([up_self_left, up_tip.T], axis=1)
+            )
+            cross = early[:, : inverse_rows.shape[1]]
+            near_tip = early[:, inverse_rows.shape[1]:].T
 
         older = history.get(level_index + 2)
         far_diag, far_tip = zero_rows, zero_tip

time: 592 us -> 670 us (1.13)
  starting transfers between devices: 105 us -> 351 us
  waiting for transfers between devices: 228 us -> 16.5 us
  local copies, waits for them, and re-layouts: 49.9 us -> 83.1 us
  matrix products: 75.3 us -> 82.6 us
    ppermute x56 -> x44, starting transfers between devices: 94.8 us -> 332 us  [send(): return lax.ppermute(values, 'tm', pairs)]
    ppermute x56 -> x44, waiting for transfers between devices: 227 us -> 15.3 us  [send(): return lax.ppermute(values, 'tm', pairs)]
    unnamed x185 -> x159, local copies, waits for them, and re-layouts: 12.2 us -> 24.4 us
    ppermute x0 -> x4, local copies, waits for them, and re-layouts: none -> 9.48 us  [send(): return lax.ppermute(values, 'tm', pairs)]
    transpose x8 -> x0, local copies, waits for them, and re-layouts: 9.43 us -> none  [the longest x5 5.48 us: body(): far_operand = jnp.concatenate([cross_turned, far_diag, far_tip.T], axis=1)]
    ppermute x20, starting transfers between devices: 10.1 us -> 18.8 us  [swap_tiles(): return lax.ppermute(values, 'tile', [(0, 1), (1, 0)])]
    add x4, other arithmetic: 1.17 us -> 9.5 us  [add_present(): return jax.tree.map(lambda a, b: a + b, first, second)]
    dot_general x31, matrix products: 75.3 us -> 82.6 us  [product(): jnp.dot(left_matrix, right_matrix, preferred_element_type=jnp.float32)]
  transfers between devices with their start and end apart: 76 -> 64, of which waited for: 4 -> 2; matrix products, arithmetic and copies ran while one was open for 33% -> 31% of each run, Pallas kernels for 0% -> 0%
where the time goes in v7:
time: 670 us; the launch traced here: 658 us
  starting transfers between devices  351 us (52%)
  other arithmetic  121 us (18%)
  local copies, waits for them, and re-layouts  83.1 us (12%)
  matrix products  82.6 us (12%)
  waiting for transfers between devices  16.5 us (2%)
    ppermute x44, starting transfers between devices, send(): return lax.ppermute(values, 'tm', pairs)  332 us
    dot_general x31, matrix products, product(): jnp.dot(left_matrix, right_matrix, preferred_element_type=jnp.float32)  82.6 us
    select_n x13, other arithmetic, pick(): return jnp.where(flag, if_true, if_false)  27.3 us
    unnamed x159, local copies, waits for them, and re-layouts  24.4 us
    ppermute x20, starting transfers between devices, swap_tiles(): return lax.ppermute(values, 'tile', [(0, 1), (1, 0)])  18.8 us
    ppermute x44, waiting for transfers between devices, send(): return lax.ppermute(values, 'tm', pairs)  15.3 us
  transfers between devices with their start and end apart: 64, of which 2 were waited for; matrix products, arithmetic and copies ran while one was open for 31% of the time, Pallas kernels for 0%

profile of v7, /device:TPU:31, one launch (start us, length us, event | category | flops | bytes accessed | tf_op | source)
XLA Modules:
  0.0 657.5 jit_solution(17197627052831683256)
XLA Ops:
  3.2 11.2 %collective-permute-start.4 = (bf16[32,1024]{1,0:T(8,128)(2,1)}, bf16[32,1024]{1,0:T(8,128)(2,1)S(1)}, u32[]{:S(2)}, u32[]{:S(2)}) collective-permute-start(bf16[32,1024]{1,0:T(8,128)(2,1)} %bitcast.332), channel_id=1, source_target_pairs={{0,1},{1,0},{2,3},{3,2},{4,5},{5,4},{6,7},{7,6},{8,9},{9,8},{10,11... | collective-permute-start | bytes 196616 | tf_op jit(solution)/shard_map/ppermute | solution.py:143
  19.8 4.3 broadcast_select_fusion.1
  50.4 6.4 broadcast_select_fusion.20
  91.3 3.6 fusion.130
  98.3 4.9 fusion.133
  115.8 3.6 subtract_convert_fusion
  140.4 4.3 maximum_select_fusion.3
  155.3 5.6 fusion.136
  184.9 5.9 broadcast_select_fusion.18
  220.2 5.9 fusion.142
  257.2 4.7 broadcast_select_fusion.17
  291.2 4.9 fusion.148
  305.2 208.6 %collective-permute-start.60 = (bf16[64,512]{1,0:T(8,128)(2,1)S(1)}, bf16[64,512]{1,0:T(8,128)(2,1)S(1)}, u32[]{:S(2)}, u32[]{:S(2)}) collective-permute-start(bf16[64,512]{1,0:T(8,128)(2,1)S(1)} %copy-done.64), channel_id=1, source_target_pairs={{124,122},{4,2},{12,10},{20,18},{28,26},{36,34},{44,42},{52,50},{6... | collective-permute-start | bytes 196616 | tf_op jit(solution)/shard_map/ppermute | solution.py:139
  513.8 10.2 %collective-permute-start.61 = (bf16[64,512]{1,0:T(8,128)(2,1)S(1)}, bf16[64,512]{1,0:T(8,128)(2,1)S(1)}, u32[]{:S(2)}, u32[]{:S(2)}) collective-permute-start(bf16[64,512]{1,0:T(8,128)(2,1)S(1)} %copy-done.64), channel_id=1, source_target_pairs={{124,126},{4,6},{12,14},{20,22},{28,30},{36,38},{44,46},{52,54},{6... | collective-permute-start | bytes 196616 | tf_op jit(solution)/shard_map/ppermute | solution.py:139
  523.9 10.3 %collective-permute-start.58 = (bf16[512,1024]{1,0:T(8,128)(2,1)}, bf16[512,1024]{1,0:T(8,128)(2,1)S(1)}, u32[]{:S(2)}, u32[]{:S(2)}) collective-permute-start(bf16[512,1024]{1,0:T(8,128)(2,1)} %get-tuple-element.27), channel_id=1, source_target_pairs={{124,122},{4,2},{12,10},{20,18},{28,26},{36,34},{44,42},{52,50},{6... | collective-permute-start | bytes 3145736 | tf_op jit(solution)/shard_map/ppermute | solution.py:139
  534.2 10.4 %collective-permute-start.59 = (bf16[512,1024]{1,0:T(8,128)(2,1)}, bf16[512,1024]{1,0:T(8,128)(2,1)}, u32[]{:S(2)}, u32[]{:S(2)}) collective-permute-start(bf16[512,1024]{1,0:T(8,128)(2,1)} %get-tuple-element.27), channel_id=1, source_target_pairs={{124,126},{4,6},{12,14},{20,22},{28,30},{36,38},{44,46},{52,54},{6... | collective-permute-start | bytes 3145736 | tf_op jit(solution)/shard_map/ppermute | solution.py:139
  547.3 5.9 broadcast_select_fusion.16
  554.0 12.2 %collective-permute-start.53 = (bf16[512,1024]{1,0:T(8,128)(2,1)}, bf16[512,1024]{1,0:T(8,128)(2,1)}, u32[]{:S(2)}, u32[]{:S(2)}) collective-permute-start(bf16[512,1024]{1,0:T(8,128)(2,1)} %get-tuple-element.114), channel_id=1, source_target_pairs={{120,122},{0,2},{8,10},{16,18},{24,26},{32,34},{40,42},{48,50},{56... | collective-permute-start | bytes 3145736 | tf_op jit(solution)/shard_map/ppermute | solution.py:139
  566.1 9.5 %collective-permute-start.54 = (bf16[512,1024]{1,0:T(8,128)(2,1)}, bf16[512,1024]{1,0:T(8,128)(2,1)}, u32[]{:S(2)}, u32[]{:S(2)}) collective-permute-start(bf16[512,1024]{1,0:T(8,128)(2,1)} %get-tuple-element.114), channel_id=1, source_target_pairs={{120,118},{0,126},{8,6},{16,14},{24,22},{32,30},{40,38},{48,46},{5... | collective-permute-start | bytes 3145736 | tf_op jit(solution)/shard_map/ppermute | solution.py:139
  577.3 11.5 %collective-permute-start.55 = (bf16[512,1088]{0,1:T(8,128)(2,1)}, bf16[512,1088]{0,1:T(8,128)(2,1)}, u32[]{:S(2)}, u32[]{:S(2)}) collective-permute-start(bf16[512,1088]{0,1:T(8,128)(2,1)} %get-tuple-element.90), channel_id=1, source_target_pairs={{120,122},{0,2},{8,10},{16,18},{24,26},{32,34},{40,42},{48,50},{56... | collective-permute-start | bytes 3342344 | tf_op jit(solution)/shard_map/ppermute | solution.py:139
  588.8 9.5 %collective-permute-start.56 = (bf16[512,1088]{0,1:T(8,128)(2,1)}, bf16[512,1088]{0,1:T(8,128)(2,1)}, u32[]{:S(2)}, u32[]{:S(2)}) collective-permute-start(bf16[512,1088]{0,1:T(8,128)(2,1)} %get-tuple-element.89), channel_id=1, source_target_pairs={{120,118},{0,126},{8,6},{16,14},{24,22},{32,30},{40,38},{48,46},{5... | collective-permute-start | bytes 3342344 | tf_op jit(solution)/shard_map/ppermute | solution.py:139
  609.8 15.2 %collective-permute-done.56 = bf16[512,1088]{0,1:T(8,128)(2,1)} collective-permute-done((bf16[512,1088]{0,1:T(8,128)(2,1)}, bf16[512,1088]{0,1:T(8,128)(2,1)}, u32[]{:S(2)}, u32[]{:S(2)}) %collective-permute-start.56) | collective-permute-done | bytes 1114144 | tf_op jit(solution)/shard_map/ppermute | solution.py:139
  646.6 3.9 copy.172
  650.5 6.5 fusion.163
  (432 shorter events, 275.7 us)
Async XLA Ops:
  0.6 18.2 %collective-permute-start.3 = (bf16[512,1024]{1,0:T(8,128)(2,1)}, bf16[512,1024]{1,0:T(8,128)(2,1)S(1)}, u32[]{:S(2)}, u32[]{:S(2)}) collective-permute-start(bf16[512,1024]{1,0:T(8,128)(2,1)} %bitcast.312), channel_id=1, source_target_pairs={{0,1},{1,0},{2,3},{3,2},{4,5},{5,4},{6,7},{7,6},{8,9},{9,8},{10,11... | collective-permute-start | bytes 3145736 | tf_op jit(solution)/shard_map/ppermute | solution.py:143
  1.5 24.2 %collective-permute-start = (bf16[512,1024]{1,0:T(8,128)(2,1)}, bf16[512,1024]{1,0:T(8,128)(2,1)}, u32[]{:S(2)}, u32[]{:S(2)}) collective-permute-start(bf16[512,1024]{1,0:T(8,128)(2,1)} %bitcast.316), channel_id=1, source_target_pairs={{116,52},{117,53}} | collective-permute-start | bytes 3145736 | tf_op jit(solution)/shard_map/ppermute | solution.py:139
  56.8 20.9 %collective-permute-start.7 = (bf16[512,1024]{1,0:T(8,128)(2,1)}, bf16[512,1024]{1,0:T(8,128)(2,1)}, u32[]{:S(2)}, u32[]{:S(2)}) collective-permute-start(bf16[512,1024]{1,0:T(8,128)(2,1)} %get-tuple-element.100), channel_id=1, source_target_pairs={{52,84},{53,85}} | collective-permute-start | bytes 3145736 | tf_op jit(solution)/shard_map/ppermute | solution.py:139
  58.4 20.9 %collective-permute-start.8 = (bf16[512,1024]{1,0:T(8,128)(2,1)}, bf16[512,1024]{1,0:T(8,128)(2,1)}, u32[]{:S(2)}, u32[]{:S(2)}) collective-permute-start(bf16[512,1024]{1,0:T(8,128)(2,1)} %get-tuple-element.100), channel_id=1, source_target_pairs={{52,20},{53,21}} | collective-permute-start | bytes 3145736 | tf_op jit(solution)/shard_map/ppermute | solution.py:139
  63.6 18.7 %collective-permute-start.9 = (bf16[512,1088]{0,1:T(8,128)(2,1)}, bf16[512,1088]{0,1:T(8,128)(2,1)}, u32[]{:S(2)}, u32[]{:S(2)}) collective-permute-start(bf16[512,1088]{0,1:T(8,128)(2,1)} %copy.117), channel_id=1, source_target_pairs={{52,84},{53,85}} | collective-permute-start | bytes 3342344 | tf_op jit(solution)/shard_map/ppermute | solution.py:139
  68.1 30.2 %collective-permute-start.13 = (bf16[64,512]{0,1:T(8,128)(2,1)}, bf16[64,512]{0,1:T(8,128)(2,1)S(1)}, u32[]{:S(2)}, u32[]{:S(2)}) collective-permute-start(bf16[64,512]{0,1:T(8,128)(2,1)} %copy.110), channel_id=1, source_target_pairs={{116,84},{117,85}} | collective-permute-start | bytes 196616 | tf_op jit(solution)/shard_map/ppermute | solution.py:139
  77.7 20.6 %collective-permute-start.12 = (bf16[512,1024]{1,0:T(8,128)(2,1)}, bf16[512,1024]{1,0:T(8,128)(2,1)}, u32[]{:S(2)}, u32[]{:S(2)}) collective-permute-start(bf16[512,1024]{1,0:T(8,128)(2,1)} %bitcast.317), channel_id=1, source_target_pairs={{116,84},{117,85}} | collective-permute-start | bytes 3145736 | tf_op jit(solution)/shard_map/ppermute | solution.py:139
  107.7 22.5 %collective-permute-start.23 = (bf16[512,1024]{1,0:T(8,128)(2,1)}, bf16[512,1024]{1,0:T(8,128)(2,1)}, u32[]{:S(2)}, u32[]{:S(2)}) collective-permute-start(bf16[512,1024]{1,0:T(8,128)(2,1)} %get-tuple-element.18), channel_id=1, source_target_pairs={{52,36},{116,100},{53,37},{117,101}} | collective-permute-start | bytes 3145736 | tf_op jit(solution)/shard_map/ppermute | solution.py:139
  125.5 22.0 %collective-permute-start.19 = (bf16[512,1088]{0,1:T(8,128)(2,1)}, bf16[512,1088]{0,1:T(8,128)(2,1)}, u32[]{:S(2)}, u32[]{:S(2)}) collective-permute-start(bf16[512,1088]{0,1:T(8,128)(2,1)} %get-tuple-element.96), channel_id=1, source_target_pairs={{20,4},{84,68},{21,5},{85,69}} | collective-permute-start | bytes 3342344 | tf_op jit(solution)/shard_map/ppermute | solution.py:139
  127.2 20.3 %collective-permute-start.21 = (bf16[512,1088]{0,1:T(8,128)(2,1)}, bf16[512,1088]{0,1:T(8,128)(2,1)}, u32[]{:S(2)}, u32[]{:S(2)}) collective-permute-start(bf16[512,1088]{0,1:T(8,128)(2,1)} %collective-permute-done.20), channel_id=1, source_target_pairs={{52,36},{116,100},{53,37},{117,101}} | collective-permute-start | bytes 3342344 | tf_op jit(solution)/shard_map/ppermute | solution.py:139
  179.8 18.4 %collective-permute-start.34 = (bf16[512,1024]{1,0:T(8,128)(2,1)}, bf16[512,1024]{1,0:T(8,128)(2,1)S(1)}, u32[]{:S(2)}, u32[]{:S(2)}) collective-permute-start(bf16[512,1024]{1,0:T(8,128)(2,1)} %broadcast_select_fusion.19), channel_id=1, source_target_pairs={{20,12},{52,44},{84,76},{116,108},{21,13},{53,45},{85,77},{117,109}} | collective-permute-start | bytes 3145736 | tf_op jit(solution)/shard_map/ppermute | solution.py:139
  180.6 21.5 %collective-permute-start.35 = (bf16[512,1024]{1,0:T(8,128)(2,1)}, bf16[512,1024]{1,0:T(8,128)(2,1)}, u32[]{:S(2)}, u32[]{:S(2)}) collective-permute-start(bf16[512,1024]{1,0:T(8,128)(2,1)} %broadcast_select_fusion.19), channel_id=1, source_target_pairs={{20,28},{52,60},{84,92},{21,29},{53,61},{85,93}} | collective-permute-start | bytes 3145736 | tf_op jit(solution)/shard_map/ppermute | solution.py:139
  214.4 33.7 %collective-permute-start.39 = (bf16[2,64,512]{2,1,0:T(8,128)(2,1)}, bf16[2,64,512]{2,1,0:T(8,128)(2,1)}, u32[]{:S(2)}, u32[]{:S(2)}) collective-permute-start(bf16[2,64,512]{2,1,0:T(8,128)(2,1)} %pad_maximum_fusion.37), channel_id=1, source_target_pairs={{0,1},{1,0},{2,3},{3,2},{4,5},{5,4},{6,7},{7,6},{8,9},{9,8},{10,11... | collective-permute-start | bytes 393224 | tf_op jit(solution)/shard_map/ppermute | solution.py:143
  247.2 21.8 %collective-permute-start.47 = (bf16[512,1024]{0,1:T(8,128)(2,1)}, bf16[512,1024]{0,1:T(8,128)(2,1)S(1)}, u32[]{:S(2)}, u32[]{:S(2)}) collective-permute-start(bf16[512,1024]{0,1:T(8,128)(2,1)} %copy.157), channel_id=1, source_target_pairs={{4,0},{20,16},{36,32},{52,48},{68,64},{84,80},{100,96},{116,112},{... | collective-permute-start | bytes 3145736 | tf_op jit(solution)/shard_map/ppermute | solution.py:139
  289.2 245.0 %collective-permute-start.52 = (bf16[2,64,512]{2,1,0:T(8,128)(2,1)S(1)}, bf16[2,64,512]{2,1,0:T(8,128)(2,1)S(1)}, u32[]{:S(2)}, u32[]{:S(2)}) collective-permute-start(bf16[2,64,512]{2,1,0:T(8,128)(2,1)S(1)} %pad_maximum_fusion.38), channel_id=1, source_target_pairs={{0,1},{1,0},{2,3},{3,2},{4,5},{5,4},{6,7},{7,6},{8,9},{9,8},{10,11... | collective-permute-start | bytes 393224 | tf_op jit(solution)/shard_map/ppermute | solution.py:143
  301.0 244.3 %collective-permute-start.51 = (bf16[2,512,512]{2,1,0:T(8,128)(2,1)S(1)}, bf16[2,512,512]{2,1,0:T(8,128)(2,1)S(1)}, u32[]{:S(2)}, u32[]{:S(2)}) collective-permute-start(bf16[2,512,512]{2,1,0:T(8,128)(2,1)S(1)} %broadcast_select_fusion.30), channel_id=1, source_target_pairs={{0,1},{1,0},{2,3},{3,2},{4,5},{5,4},{6,7},{7,6},{8,9},{9,8},{10,11... | collective-permute-start | bytes 3145736 | tf_op jit(solution)/shard_map/ppermute | solution.py:143
  305.2 261.0 %collective-permute-start.60 = (bf16[64,512]{1,0:T(8,128)(2,1)S(1)}, bf16[64,512]{1,0:T(8,128)(2,1)S(1)}, u32[]{:S(2)}, u32[]{:S(2)}) collective-permute-start(bf16[64,512]{1,0:T(8,128)(2,1)S(1)} %copy-done.64), channel_id=1, source_target_pairs={{124,122},{4,2},{12,10},{20,18},{28,26},{36,34},{44,42},{52,50},{6... | collective-permute-start | bytes 196616 | tf_op jit(solution)/shard_map/ppermute | solution.py:139
  513.8 63.5 %collective-permute-start.61 = (bf16[64,512]{1,0:T(8,128)(2,1)S(1)}, bf16[64,512]{1,0:T(8,128)(2,1)S(1)}, u32[]{:S(2)}, u32[]{:S(2)}) collective-permute-start(bf16[64,512]{1,0:T(8,128)(2,1)S(1)} %copy-done.64), channel_id=1, source_target_pairs={{124,126},{4,6},{12,14},{20,22},{28,30},{36,38},{44,46},{52,54},{6... | collective-permute-start | bytes 196616 | tf_op jit(solution)/shard_map/ppermute | solution.py:139
  523.9 64.8 %collective-permute-start.58 = (bf16[512,1024]{1,0:T(8,128)(2,1)}, bf16[512,1024]{1,0:T(8,128)(2,1)S(1)}, u32[]{:S(2)}, u32[]{:S(2)}) collective-permute-start(bf16[512,1024]{1,0:T(8,128)(2,1)} %get-tuple-element.27), channel_id=1, source_target_pairs={{124,122},{4,2},{12,10},{20,18},{28,26},{36,34},{44,42},{52,50},{6... | collective-permute-start | bytes 3145736 | tf_op jit(solution)/shard_map/ppermute | solution.py:139
  534.2 66.1 %collective-permute-start.59 = (bf16[512,1024]{1,0:T(8,128)(2,1)}, bf16[512,1024]{1,0:T(8,128)(2,1)}, u32[]{:S(2)}, u32[]{:S(2)}) collective-permute-start(bf16[512,1024]{1,0:T(8,128)(2,1)} %get-tuple-element.27), channel_id=1, source_target_pairs={{124,126},{4,6},{12,14},{20,22},{28,30},{36,38},{44,46},{52,54},{6... | collective-permute-start | bytes 3145736 | tf_op jit(solution)/shard_map/ppermute | solution.py:139
  554.0 50.6 %collective-permute-start.53 = (bf16[512,1024]{1,0:T(8,128)(2,1)}, bf16[512,1024]{1,0:T(8,128)(2,1)}, u32[]{:S(2)}, u32[]{:S(2)}) collective-permute-start(bf16[512,1024]{1,0:T(8,128)(2,1)} %get-tuple-element.114), channel_id=1, source_target_pairs={{120,122},{0,2},{8,10},{16,18},{24,26},{32,34},{40,42},{48,50},{56... | collective-permute-start | bytes 3145736 | tf_op jit(solution)/shard_map/ppermute | solution.py:139
  566.1 38.4 %collective-permute-start.54 = (bf16[512,1024]{1,0:T(8,128)(2,1)}, bf16[512,1024]{1,0:T(8,128)(2,1)}, u32[]{:S(2)}, u32[]{:S(2)}) collective-permute-start(bf16[512,1024]{1,0:T(8,128)(2,1)} %get-tuple-element.114), channel_id=1, source_target_pairs={{120,118},{0,126},{8,6},{16,14},{24,22},{32,30},{40,38},{48,46},{5... | collective-permute-start | bytes 3145736 | tf_op jit(solution)/shard_map/ppermute | solution.py:139
  577.3 32.6 %collective-permute-start.55 = (bf16[512,1088]{0,1:T(8,128)(2,1)}, bf16[512,1088]{0,1:T(8,128)(2,1)}, u32[]{:S(2)}, u32[]{:S(2)}) collective-permute-start(bf16[512,1088]{0,1:T(8,128)(2,1)} %get-tuple-element.90), channel_id=1, source_target_pairs={{120,122},{0,2},{8,10},{16,18},{24,26},{32,34},{40,42},{48,50},{56... | collective-permute-start | bytes 3342344 | tf_op jit(solution)/shard_map/ppermute | solution.py:139
  588.8 36.2 %collective-permute-start.56 = (bf16[512,1088]{0,1:T(8,128)(2,1)}, bf16[512,1088]{0,1:T(8,128)(2,1)}, u32[]{:S(2)}, u32[]{:S(2)}) collective-permute-start(bf16[512,1088]{0,1:T(8,128)(2,1)} %get-tuple-element.89), channel_id=1, source_target_pairs={{120,118},{0,126},{8,6},{16,14},{24,22},{32,30},{40,38},{48,46},{5... | collective-permute-start | bytes 3342344 | tf_op jit(solution)/shard_map/ppermute | solution.py:139
  (117 other events, 759.8 us)

commit v8 on v5

--- a/solution.py
+++ b/solution.py
@@ -231,7 +231,7 @@
                 )
                 cross = add_present(cross, send(held_cross, step_plan["leg_on"]))
 
-        older = history.get(level_index + 2)
+        older = history.get(level_index + 1)
         far_diag, far_tip = zero_rows, zero_tip
         if older is not None:
             g_left = send(older, step_plan["pre_from_left"])

time: 592 us -> 701 us (1.18)
  the two profiles are of different devices: /device:TPU:31 before, /device:TPU:1 now
where the time goes in v8:
time: 701 us; the launch traced here: 690 us
  starting transfers between devices  352 us (50%)
  other arithmetic  124 us (18%)
  waiting for transfers between devices  78.5 us (11%)
  matrix products  66.1 us (9%)
  local copies, waits for them, and re-layouts  65.8 us (9%)
    ppermute x56, starting transfers between devices, send(): return lax.ppermute(values, 'tm', pairs)  304 us
    ppermute x56, waiting for transfers between devices, send(): return lax.ppermute(values, 'tm', pairs)  73.5 us
    dot_general x31, matrix products, product(): jnp.dot(left_matrix, right_matrix, preferred_element_type=jnp.float32)  66.1 us
    ppermute x20, starting transfers between devices, swap_tiles(): return lax.ppermute(values, 'tile', [(0, 1), (1, 0)])  47.7 us
    select_n x10, other arithmetic, pick(): return jnp.where(flag, if_true, if_false)  18.7 us
    select_n x5, other arithmetic, body(): jnp.where(active, jnp.concatenate([self_left, self_right], axis=1), state...  16.9 us
    unnamed x150, local copies, waits for them, and re-layouts  15.2 us
  transfers between devices with their start and end apart: 76, of which 8 were waited for; matrix products, arithmetic and copies ran while one was open for 28% of the time, Pallas kernels for 0%

profile of v8, /device:TPU:1, one launch (start us, length us, event | category | flops | bytes accessed | tf_op | source)
XLA Modules:
  0.0 689.6 jit_solution(8431565462583792719)
XLA Ops:
  6.1 12.2 %collective-permute-start.4 = (bf16[32,1024]{1,0:T(8,128)(2,1)S(1)}, bf16[32,1024]{1,0:T(8,128)(2,1)}, u32[]{:S(2)}, u32[]{:S(2)}) collective-permute-start(bf16[32,1024]{1,0:T(8,128)(2,1)S(1)} %bitcast.328), channel_id=1, source_target_pairs={{0,1},{1,0},{2,3},{3,2},{4,5},{5,4},{6,7},{7,6},{8,9},{9,8},{10,11... | collective-permute-start | bytes 196616 | tf_op jit(solution)/shard_map/ppermute | solution.py:143
  20.6 21.3 %collective-permute-start.6 = (bf16[2,64,512]{2,1,0:T(8,128)(2,1)S(1)}, bf16[2,64,512]{2,1,0:T(8,128)(2,1)S(1)}, u32[]{:S(2)}, u32[]{:S(2)}) collective-permute-start(bf16[2,64,512]{2,1,0:T(8,128)(2,1)S(1)} %stack.109), channel_id=1, source_target_pairs={{0,1},{1,0},{2,3},{3,2},{4,5},{5,4},{6,7},{7,6},{8,9},{9,8},{10,11... | collective-permute-start | bytes 393224 | tf_op jit(solution)/shard_map/ppermute | solution.py:143
  44.9 4.7 broadcast_select_fusion.2
  79.0 5.3 subtract_convert_fusion.5
  235.4 4.8 broadcast_select_fusion.17
  240.2 146.3 %collective-permute-start.51 = (bf16[512,1024]{0,1:T(8,128)(2,1)S(1)}, bf16[512,1024]{0,1:T(8,128)(2,1)}, u32[]{:S(2)}, u32[]{:S(2)}) collective-permute-start(bf16[512,1024]{0,1:T(8,128)(2,1)S(1)} %broadcast_select_fusion.10), channel_id=1, source_target_pairs={{124,100},{12,20},{28,4},{44,52},{60,36},{76,84},{92,68},{108,116}... | collective-permute-start | bytes 3145736 | tf_op jit(solution)/shard_map/ppermute | solution.py:139
  391.9 13.1 %collective-permute-start.48 = (bf16[512,1024]{0,1:T(8,128)(2,1)}, bf16[512,1024]{0,1:T(8,128)(2,1)}, u32[]{:S(2)}, u32[]{:S(2)}) collective-permute-start(bf16[512,1024]{0,1:T(8,128)(2,1)} %get-tuple-element.120), channel_id=1, source_target_pairs={{124,100},{12,20},{28,4},{44,52},{60,36},{76,84},{92,68},{108,116}... | collective-permute-start | bytes 3145736 | tf_op jit(solution)/shard_map/ppermute | solution.py:139
  405.0 9.9 %collective-permute-start.54 = (bf16[64,512]{1,0:T(8,128)(2,1)S(1)}, bf16[64,512]{1,0:T(8,128)(2,1)S(1)}, u32[]{:S(2)}, u32[]{:S(2)}) collective-permute-start(bf16[64,512]{1,0:T(8,128)(2,1)S(1)} %get-tuple-element.50), channel_id=1, source_target_pairs={{124,100},{12,20},{28,4},{44,52},{60,36},{76,84},{92,68},{108,116}... | collective-permute-start | bytes 196616 | tf_op jit(solution)/shard_map/ppermute | solution.py:139
  418.2 28.7 %collective-permute-done.55 = bf16[64,512]{1,0:T(8,128)(2,1)S(1)} collective-permute-done((bf16[64,512]{1,0:T(8,128)(2,1)S(1)}, bf16[64,512]{1,0:T(8,128)(2,1)S(1)}, u32[]{:S(2)}, u32[]{:S(2)}) %collective-permute-start.55) | collective-permute-done | bytes 65568 | tf_op jit(solution)/shard_map/ppermute | solution.py:139
  448.9 5.2 collective-permute-done.59
  454.1 7.4 %collective-permute-start.50 = (bf16[512,1024]{0,1:T(8,128)(2,1)}, bf16[512,1024]{0,1:T(8,128)(2,1)}, u32[]{:S(2)}, u32[]{:S(2)}) collective-permute-start(bf16[512,1024]{0,1:T(8,128)(2,1)} %get-tuple-element.46), channel_id=1, source_target_pairs={{124,120},{12,8},{28,24},{44,40},{60,56},{76,72},{92,88},{108,104}... | collective-permute-start | bytes 3145736 | tf_op jit(solution)/shard_map/ppermute | solution.py:139
  475.7 15.4 %collective-permute-done.52 = bf16[512,1024]{0,1:T(8,128)(2,1)} collective-permute-done((bf16[512,1024]{0,1:T(8,128)(2,1)}, bf16[512,1024]{0,1:T(8,128)(2,1)}, u32[]{:S(2)}, u32[]{:S(2)}) %collective-permute-start.52) | collective-permute-done | bytes 1048608 | tf_op jit(solution)/shard_map/ppermute | solution.py:139
  496.4 17.3 %collective-permute-done.49 = bf16[512,1024]{0,1:T(8,128)(2,1)} collective-permute-done((bf16[512,1024]{0,1:T(8,128)(2,1)}, bf16[512,1024]{0,1:T(8,128)(2,1)}, u32[]{:S(2)}, u32[]{:S(2)}) %collective-permute-start.49) | collective-permute-done | bytes 1048608 | tf_op jit(solution)/shard_map/ppermute | solution.py:139
  534.4 5.7 collective-permute-start.67
  549.3 8.9 %collective-permute-start.66 = (bf16[512,1024]{0,1:T(8,128)(2,1)}, bf16[512,1024]{0,1:T(8,128)(2,1)}, u32[]{:S(2)}, u32[]{:S(2)}) collective-permute-start(bf16[512,1024]{0,1:T(8,128)(2,1)} %get-tuple-element.41), channel_id=1, source_target_pairs={{120,118},{0,126},{8,6},{16,14},{24,22},{32,30},{40,38},{48,46},{5... | collective-permute-start | bytes 3145736 | tf_op jit(solution)/shard_map/ppermute | solution.py:139
  558.3 4.8 broadcast_select_fusion.16
  567.2 8.9 %collective-permute-start.73 = (bf16[64,512]{1,0:T(8,128)(2,1)}, bf16[64,512]{1,0:T(8,128)(2,1)S(1)}, u32[]{:S(2)}, u32[]{:S(2)}) collective-permute-start(bf16[64,512]{1,0:T(8,128)(2,1)} %get-tuple-element.31), channel_id=1, source_target_pairs={{124,126},{4,6},{12,14},{20,22},{28,30},{36,38},{44,46},{52,54},{6... | collective-permute-start | bytes 196616 | tf_op jit(solution)/shard_map/ppermute | solution.py:139
  576.1 11.3 %collective-permute-start.71 = (bf16[512,1024]{1,0:T(8,128)(2,1)}, bf16[512,1024]{1,0:T(8,128)(2,1)}, u32[]{:S(2)}, u32[]{:S(2)}) collective-permute-start(bf16[512,1024]{1,0:T(8,128)(2,1)} %get-tuple-element.30), channel_id=1, source_target_pairs={{124,126},{4,6},{12,14},{20,22},{28,30},{36,38},{44,46},{52,54},{6... | collective-permute-start | bytes 3145736 | tf_op jit(solution)/shard_map/ppermute | solution.py:139
  587.3 11.1 %collective-permute-start.70 = (bf16[512,1024]{1,0:T(8,128)(2,1)}, bf16[512,1024]{1,0:T(8,128)(2,1)}, u32[]{:S(2)}, u32[]{:S(2)}) collective-permute-start(bf16[512,1024]{1,0:T(8,128)(2,1)} %get-tuple-element.30), channel_id=1, source_target_pairs={{124,122},{4,2},{12,10},{20,18},{28,26},{36,34},{44,42},{52,50},{6... | collective-permute-start | bytes 3145736 | tf_op jit(solution)/shard_map/ppermute | solution.py:139
  598.5 10.2 %collective-permute-start.72 = (bf16[64,512]{1,0:T(8,128)(2,1)}, bf16[64,512]{1,0:T(8,128)(2,1)S(1)}, u32[]{:S(2)}, u32[]{:S(2)}) collective-permute-start(bf16[64,512]{1,0:T(8,128)(2,1)} %get-tuple-element.31), channel_id=1, source_target_pairs={{124,122},{4,2},{12,10},{20,18},{28,26},{36,34},{44,42},{52,50},{6... | collective-permute-start | bytes 196616 | tf_op jit(solution)/shard_map/ppermute | solution.py:139
  610.0 10.6 %collective-permute-start.64 = (bf16[512,1024]{1,0:T(8,128)(2,1)}, bf16[512,1024]{1,0:T(8,128)(2,1)}, u32[]{:S(2)}, u32[]{:S(2)}) collective-permute-start(bf16[512,1024]{1,0:T(8,128)(2,1)} %get-tuple-element.124), channel_id=1, source_target_pairs={{120,118},{0,126},{8,6},{16,14},{24,22},{32,30},{40,38},{48,46},{5... | collective-permute-start | bytes 3145736 | tf_op jit(solution)/shard_map/ppermute | solution.py:139
  620.6 9.3 %collective-permute-start.63 = (bf16[512,1024]{1,0:T(8,128)(2,1)}, bf16[512,1024]{1,0:T(8,128)(2,1)}, u32[]{:S(2)}, u32[]{:S(2)}) collective-permute-start(bf16[512,1024]{1,0:T(8,128)(2,1)} %get-tuple-element.124), channel_id=1, source_target_pairs={{120,122},{0,2},{8,10},{16,18},{24,26},{32,34},{40,42},{48,50},{56... | collective-permute-start | bytes 3145736 | tf_op jit(solution)/shard_map/ppermute | solution.py:139
  644.1 6.7 collective-permute-done.63
  679.6 5.8 fusion.168
  (437 shorter events, 301.9 us)
Async XLA Ops:
  0.7 42.3 %collective-permute-start.2 = (bf16[512,1024]{1,0:T(8,128)(2,1)}, bf16[512,1024]{1,0:T(8,128)(2,1)S(1)}, u32[]{:S(2)}, u32[]{:S(2)}) collective-permute-start(bf16[512,1024]{1,0:T(8,128)(2,1)} %bitcast.320), channel_id=1, source_target_pairs={{0,1},{1,0},{2,3},{3,2},{4,5},{5,4},{6,7},{7,6},{8,9},{9,8},{10,11... | collective-permute-start | bytes 3145736 | tf_op jit(solution)/shard_map/ppermute | solution.py:143
  2.2 40.8 %collective-permute-start.3 = (bf16[512,1024]{1,0:T(8,128)(2,1)}, bf16[512,1024]{1,0:T(8,128)(2,1)S(1)}, u32[]{:S(2)}, u32[]{:S(2)}) collective-permute-start(bf16[512,1024]{1,0:T(8,128)(2,1)} %bitcast.318), channel_id=1, source_target_pairs={{0,1},{1,0},{2,3},{3,2},{4,5},{5,4},{6,7},{7,6},{8,9},{9,8},{10,11... | collective-permute-start | bytes 3145736 | tf_op jit(solution)/shard_map/ppermute | solution.py:143
  3.8 47.5 %collective-permute-start = (bf16[512,1024]{0,1:T(8,128)(2,1)S(1)}, bf16[512,1024]{0,1:T(8,128)(2,1)}, u32[]{:S(2)}, u32[]{:S(2)}) collective-permute-start(bf16[512,1024]{0,1:T(8,128)(2,1)S(1)} %bitcast.316), channel_id=1, source_target_pairs={{116,52},{117,53}} | collective-permute-start | bytes 3145736 | tf_op jit(solution)/shard_map/ppermute | solution.py:139
  6.1 35.9 %collective-permute-start.4 = (bf16[32,1024]{1,0:T(8,128)(2,1)S(1)}, bf16[32,1024]{1,0:T(8,128)(2,1)}, u32[]{:S(2)}, u32[]{:S(2)}) collective-permute-start(bf16[32,1024]{1,0:T(8,128)(2,1)S(1)} %bitcast.328), channel_id=1, source_target_pairs={{0,1},{1,0},{2,3},{3,2},{4,5},{5,4},{6,7},{7,6},{8,9},{9,8},{10,11... | collective-permute-start | bytes 196616 | tf_op jit(solution)/shard_map/ppermute | solution.py:143
  20.6 36.0 %collective-permute-start.6 = (bf16[2,64,512]{2,1,0:T(8,128)(2,1)S(1)}, bf16[2,64,512]{2,1,0:T(8,128)(2,1)S(1)}, u32[]{:S(2)}, u32[]{:S(2)}) collective-permute-start(bf16[2,64,512]{2,1,0:T(8,128)(2,1)S(1)} %stack.109), channel_id=1, source_target_pairs={{0,1},{1,0},{2,3},{3,2},{4,5},{5,4},{6,7},{7,6},{8,9},{9,8},{10,11... | collective-permute-start | bytes 393224 | tf_op jit(solution)/shard_map/ppermute | solution.py:143
  58.8 34.6 %collective-permute-start.12 = (bf16[64,512]{1,0:T(8,128)(2,1)}, bf16[64,512]{1,0:T(8,128)(2,1)}, u32[]{:S(2)}, u32[]{:S(2)}) collective-permute-start(bf16[64,512]{1,0:T(8,128)(2,1)} %get-tuple-element.67), channel_id=1, source_target_pairs={{52,20},{53,21}} | collective-permute-start | bytes 196616 | tf_op jit(solution)/shard_map/ppermute | solution.py:139
  60.1 37.3 %collective-permute-start.11 = (bf16[64,512]{1,0:T(8,128)(2,1)}, bf16[64,512]{1,0:T(8,128)(2,1)}, u32[]{:S(2)}, u32[]{:S(2)}) collective-permute-start(bf16[64,512]{1,0:T(8,128)(2,1)} %get-tuple-element.67), channel_id=1, source_target_pairs={{52,84},{53,85}} | collective-permute-start | bytes 196616 | tf_op jit(solution)/shard_map/ppermute | solution.py:139
  169.6 34.0 %collective-permute-start.39 = (bf16[64,512]{1,0:T(8,128)(2,1)}, bf16[64,512]{1,0:T(8,128)(2,1)}, u32[]{:S(2)}, u32[]{:S(2)}) collective-permute-start(bf16[64,512]{1,0:T(8,128)(2,1)} %get-tuple-element.55), channel_id=1, source_target_pairs={{4,124},{36,28},{68,60},{100,92},{5,125},{37,29},{69,61},{101,93}} | collective-permute-start | bytes 196616 | tf_op jit(solution)/shard_map/ppermute | solution.py:139
  170.9 34.4 %collective-permute-start.38 = (bf16[64,512]{1,0:T(8,128)(2,1)}, bf16[64,512]{1,0:T(8,128)(2,1)}, u32[]{:S(2)}, u32[]{:S(2)}) collective-permute-start(bf16[64,512]{1,0:T(8,128)(2,1)} %get-tuple-element.55), channel_id=1, source_target_pairs={{4,12},{36,44},{68,76},{100,108},{5,13},{37,45},{69,77},{101,109}} | collective-permute-start | bytes 196616 | tf_op jit(solution)/shard_map/ppermute | solution.py:139
  179.4 32.4 %collective-permute-start.36 = (bf16[512,1024]{1,0:T(8,128)(2,1)}, bf16[512,1024]{1,0:T(8,128)(2,1)}, u32[]{:S(2)}, u32[]{:S(2)}) collective-permute-start(bf16[512,1024]{1,0:T(8,128)(2,1)} %broadcast_select_fusion.22), channel_id=1, source_target_pairs={{4,12},{36,44},{68,76},{100,108},{5,13},{37,45},{69,77},{101,109}} | collective-permute-start | bytes 3145736 | tf_op jit(solution)/shard_map/ppermute | solution.py:139
  181.1 32.8 %collective-permute-start.37 = (bf16[512,1024]{1,0:T(8,128)(2,1)}, bf16[512,1024]{1,0:T(8,128)(2,1)}, u32[]{:S(2)}, u32[]{:S(2)}) collective-permute-start(bf16[512,1024]{1,0:T(8,128)(2,1)} %get-tuple-element.51), channel_id=1, source_target_pairs={{4,124},{36,28},{68,60},{100,92},{5,125},{37,29},{69,61},{101,93}} | collective-permute-start | bytes 3145736 | tf_op jit(solution)/shard_map/ppermute | solution.py:139
  240.2 221.4 %collective-permute-start.51 = (bf16[512,1024]{0,1:T(8,128)(2,1)S(1)}, bf16[512,1024]{0,1:T(8,128)(2,1)}, u32[]{:S(2)}, u32[]{:S(2)}) collective-permute-start(bf16[512,1024]{0,1:T(8,128)(2,1)S(1)} %broadcast_select_fusion.10), channel_id=1, source_target_pairs={{124,100},{12,20},{28,4},{44,52},{60,36},{76,84},{92,68},{108,116}... | collective-permute-start | bytes 3145736 | tf_op jit(solution)/shard_map/ppermute | solution.py:139
  390.3 72.5 %collective-permute-start.58 = (bf16[512,1024]{0,1:T(8,128)(2,1)}, bf16[512,1024]{0,1:T(8,128)(2,1)}, u32[]{:S(2)}, u32[]{:S(2)}) collective-permute-start(bf16[512,1024]{0,1:T(8,128)(2,1)} %get-tuple-element.27), channel_id=1, source_target_pairs={{4,8},{20,24},{36,40},{52,56},{68,72},{84,88},{100,104},{5,9},{21,... | collective-permute-start | bytes 3145736 | tf_op jit(solution)/shard_map/ppermute | solution.py:139
  391.9 72.6 %collective-permute-start.48 = (bf16[512,1024]{0,1:T(8,128)(2,1)}, bf16[512,1024]{0,1:T(8,128)(2,1)}, u32[]{:S(2)}, u32[]{:S(2)}) collective-permute-start(bf16[512,1024]{0,1:T(8,128)(2,1)} %get-tuple-element.120), channel_id=1, source_target_pairs={{124,100},{12,20},{28,4},{44,52},{60,36},{76,84},{92,68},{108,116}... | collective-permute-start | bytes 3145736 | tf_op jit(solution)/shard_map/ppermute | solution.py:139
  414.9 56.6 %collective-permute-start.57 = (bf16[512,1024]{0,1:T(8,128)(2,1)}, bf16[512,1024]{0,1:T(8,128)(2,1)}, u32[]{:S(2)}, u32[]{:S(2)}) collective-permute-start(bf16[512,1024]{0,1:T(8,128)(2,1)} %get-tuple-element.27), channel_id=1, source_target_pairs={{4,0},{20,16},{36,32},{52,48},{68,64},{84,80},{100,96},{116,112},{... | collective-permute-start | bytes 3145736 | tf_op jit(solution)/shard_map/ppermute | solution.py:139
  462.9 33.5 %collective-permute-start.47 = (bf16[512,1024]{0,1:T(8,128)(2,1)}, bf16[512,1024]{0,1:T(8,128)(2,1)}, u32[]{:S(2)}, u32[]{:S(2)}) collective-permute-start(bf16[512,1024]{0,1:T(8,128)(2,1)} %get-tuple-element.120), channel_id=1, source_target_pairs={{124,120},{12,8},{28,24},{44,40},{60,56},{76,72},{92,88},{108,104}... | collective-permute-start | bytes 3145736 | tf_op jit(solution)/shard_map/ppermute | solution.py:139
  464.5 49.1 %collective-permute-start.49 = (bf16[512,1024]{0,1:T(8,128)(2,1)}, bf16[512,1024]{0,1:T(8,128)(2,1)}, u32[]{:S(2)}, u32[]{:S(2)}) collective-permute-start(bf16[512,1024]{0,1:T(8,128)(2,1)} %collective-permute-done.48), channel_id=1, source_target_pairs={{20,16},{4,32},{52,48},{36,64},{84,80},{68,96},{116,112},{100,0},{... | collective-permute-start | bytes 3145736 | tf_op jit(solution)/shard_map/ppermute | solution.py:139
  533.1 43.0 %collective-permute-start.68 = (bf16[64,512]{1,0:T(8,128)(2,1)S(1)}, bf16[64,512]{1,0:T(8,128)(2,1)S(1)}, u32[]{:S(2)}, u32[]{:S(2)}) collective-permute-start(bf16[64,512]{1,0:T(8,128)(2,1)S(1)} %get-tuple-element.45), channel_id=1, source_target_pairs={{120,118},{0,126},{8,6},{16,14},{24,22},{32,30},{40,38},{48,46},{5... | collective-permute-start | bytes 196616 | tf_op jit(solution)/shard_map/ppermute | solution.py:139
  534.4 52.9 %collective-permute-start.67 = (bf16[64,512]{1,0:T(8,128)(2,1)S(1)}, bf16[64,512]{1,0:T(8,128)(2,1)S(1)}, u32[]{:S(2)}, u32[]{:S(2)}) collective-permute-start(bf16[64,512]{1,0:T(8,128)(2,1)S(1)} %get-tuple-element.45), channel_id=1, source_target_pairs={{120,122},{0,2},{8,10},{16,18},{24,26},{32,34},{40,42},{48,50},{56... | collective-permute-start | bytes 196616 | tf_op jit(solution)/shard_map/ppermute | solution.py:139
  545.8 74.8 %collective-permute-start.65 = (bf16[512,1024]{0,1:T(8,128)(2,1)}, bf16[512,1024]{0,1:T(8,128)(2,1)}, u32[]{:S(2)}, u32[]{:S(2)}) collective-permute-start(bf16[512,1024]{0,1:T(8,128)(2,1)} %broadcast_select_fusion.8), channel_id=1, source_target_pairs={{120,122},{0,2},{8,10},{16,18},{24,26},{32,34},{40,42},{48,50},{56... | collective-permute-start | bytes 3145736 | tf_op jit(solution)/shard_map/ppermute | solution.py:139
  549.3 81.9 %collective-permute-start.66 = (bf16[512,1024]{0,1:T(8,128)(2,1)}, bf16[512,1024]{0,1:T(8,128)(2,1)}, u32[]{:S(2)}, u32[]{:S(2)}) collective-permute-start(bf16[512,1024]{0,1:T(8,128)(2,1)} %get-tuple-element.41), channel_id=1, source_target_pairs={{120,118},{0,126},{8,6},{16,14},{24,22},{32,30},{40,38},{48,46},{5... | collective-permute-start | bytes 3145736 | tf_op jit(solution)/shard_map/ppermute | solution.py:139
  576.1 65.1 %collective-permute-start.71 = (bf16[512,1024]{1,0:T(8,128)(2,1)}, bf16[512,1024]{1,0:T(8,128)(2,1)}, u32[]{:S(2)}, u32[]{:S(2)}) collective-permute-start(bf16[512,1024]{1,0:T(8,128)(2,1)} %get-tuple-element.30), channel_id=1, source_target_pairs={{124,126},{4,6},{12,14},{20,22},{28,30},{36,38},{44,46},{52,54},{6... | collective-permute-start | bytes 3145736 | tf_op jit(solution)/shard_map/ppermute | solution.py:139
  587.3 53.8 %collective-permute-start.70 = (bf16[512,1024]{1,0:T(8,128)(2,1)}, bf16[512,1024]{1,0:T(8,128)(2,1)}, u32[]{:S(2)}, u32[]{:S(2)}) collective-permute-start(bf16[512,1024]{1,0:T(8,128)(2,1)} %get-tuple-element.30), channel_id=1, source_target_pairs={{124,122},{4,2},{12,10},{20,18},{28,26},{36,34},{44,42},{52,50},{6... | collective-permute-start | bytes 3145736 | tf_op jit(solution)/shard_map/ppermute | solution.py:139
  610.0 34.1 %collective-permute-start.64 = (bf16[512,1024]{1,0:T(8,128)(2,1)}, bf16[512,1024]{1,0:T(8,128)(2,1)}, u32[]{:S(2)}, u32[]{:S(2)}) collective-permute-start(bf16[512,1024]{1,0:T(8,128)(2,1)} %get-tuple-element.124), channel_id=1, source_target_pairs={{120,118},{0,126},{8,6},{16,14},{24,22},{32,30},{40,38},{48,46},{5... | collective-permute-start | bytes 3145736 | tf_op jit(solution)/shard_map/ppermute | solution.py:139
  (125 other events, 1354.8 us)
